TPU v7x, 128 devices: a whole 4x4x4 slice. The times are simulated.
128 devices in a mesh: row: 16 (over z, x), col: 8 (over y, core).
Axes of the slice: x: 4, y: 4, z: 4, core: 2. Of those that a mesh axis runs over, the one named last changes fastest.
Arguments:
- inputs: bfloat16 [2048, 6144], P('col', 'row'), may hold values from -6 to 6
- out_grad: bfloat16 [2048, 6144], P('col', 'row'), may hold values from -6 to 6
- pre_act: bfloat16 [2048, 24576], P('row', 'col'), may hold values from -8 to 8
- w_in: bfloat16 [6144, 24576], P('row', 'col'), may hold values from -0.078125 to 0.078125
- w_out: bfloat16 [24576, 6144], P('col', 'row'), may hold values from -0.0390625 to 0.0390625
Outputs:
- in_grad: bfloat16 [2048, 6144], P('col', 'row')
- w_in_grad: bfloat16 [6144, 24576], P('row', 'col')
- w_out_grad: bfloat16 [24576, 6144], P('col', 'row')
All inputs are finite; a program needn't handle non-finite values.
Results may differ from a plain program's by a relative error of at most 0.03.
Values may be sent and summed in bfloat16 or wider, within the bound.
No kernel may reach another device: no remote copies, remote signals or barrier semaphores. Data moves between devices by JAX's collectives and lax.ppermute only.
A program may use at most 128 MiB of HBM per device.

v0:
```python
import jax
import jax.numpy as jnp
from jax import lax
from jax.sharding import PartitionSpec as P


def gelu_parts(pre_act):
    value = pre_act.astype(jnp.float32)
    cumul = 0.5 * (1.0 + jax.scipy.special.erf(value * 0.7071067811865476))
    density = jnp.exp(-0.5 * value * value) * 0.3989422804014327
    return (value * cumul, cumul + value * density)


def on_device(inputs, out_grad, pre_act, w_in, w_out):
    inputs_all, grad_all = (
        lax.all_gather(inputs, "col", axis=0, tiled=True),
        lax.all_gather(out_grad, "col", axis=0, tiled=True),
    )
    block = grad_all
    total = lax.psum(
        lax.dot_general(
            block, w_out, (((1,), (1,)), ((), ())), preferred_element_type=jnp.float32
        ).astype(jnp.bfloat16),
        "row",
    ).astype(jnp.float32)
    pre_all = lax.all_gather(pre_act, "row", axis=0, tiled=True)
    value, slope = gelu_parts(pre_all)
    hidden = value.astype(jnp.bfloat16)
    pre_grad = (total * slope).astype(jnp.bfloat16)
    w_out_grad = lax.dot_general(
        hidden, grad_all, (((0,), (0,)), ((), ())), preferred_element_type=jnp.float32
    ).astype(jnp.bfloat16)
    w_in_grad = lax.dot_general(
        inputs_all, pre_grad, (((0,), (0,)), ((), ())), preferred_element_type=jnp.float32
    ).astype(jnp.bfloat16)
    block = pre_grad
    in_grad = lax.psum_scatter(
        lax.dot_general(
            block, w_in, (((1,), (1,)), ((), ())), preferred_element_type=jnp.float32
        ).astype(jnp.bfloat16),
        "col",
        scatter_dimension=0,
        tiled=True,
    )
    return (in_grad, w_in_grad, w_out_grad)


def solution(mesh):
    in_specs = (P("col", "row"), P("col", "row"), P("row", "col"), P("row", "col"), P("col", "row"))
    out_specs = (P("col", "row"), P("row", "col"), P("col", "row"))
    return jax.shard_map(
        on_device, mesh=mesh, in_specs=in_specs, out_specs=out_specs, check_vma=False
    )
```

profile of v0, /device:TPU:1, one launch (start us, length us, event | category | flops | bytes accessed | tf_op | source)
XLA Modules:
  0.0 384.2 jit_solution(935208402461848215)
XLA Ops:
  7.2 0.0 copy-start
  7.2 0.0 all-gather.4.cloned.1.call-start
  7.2 0.7 all-gather.4.cloned.1.call-update
  7.9 0.0 all-reduce.2.cloned.1.call-start
  8.0 29.6 %all-gather.4.cloned.1.call-done = bf16[2048,384]{1,0:T(8,128)(2,1)} async-done(((bf16[256,384]{1,0:T(8,128)(2,1)}), bf16[2048,384]{1,0:T(8,128)(2,1)}) %all-gather.4.cloned.1.call-update) | async-done | bytes 1572880 | tf_op jit(solution)/shard_map/all_gather | solution.py:17
  37.6 0.0 copy-done
  37.6 11.1 %convolution_convert_fusion = bf16[2048,3072]{1,0:T(8,128)(2,1)} fusion(bf16[2048,384]{1,0:T(8,128)(2,1)} %all-gather.4.cloned.1.call-done, bf16[3072,384]{1,0:T(8,128)(2,1)S(1)} %copy-done), kind=kOutput, calls=%fused_computation.15 | convolution fusion | flops 4838129664 | bytes 16515072 | tf_op jit(solution)/shard_map/dot_general | solution.py:21
  48.7 0.0 all-reduce.2.cloned.1.call-update
  48.8 0.0 all-gather.6.cloned.1.call-start
  48.8 0.7 all-gather.6.cloned.1.call-update
  49.5 0.0 all-gather.8.cloned.1.call-start
  49.5 0.5 all-gather.8.cloned.1.call-update
  50.1 0.0 copy-start.3
  50.1 0.0 reduce-scatter.2.cloned.1.call-start
  50.1 176.8 %all-reduce.2.cloned.1.call-done = bf16[2048,3072]{1,0:T(8,128)(2,1)} async-done(((bf16[2048,3072]{1,0:T(8,128)(2,1)}), bf16[2048,3072]{1,0:T(8,128)(2,1)}) %all-reduce.2.cloned.1.call-update) | async-done | bytes 12582928 | tf_op jit(solution)/shard_map/psum | solution.py:20
  227.0 91.8 %all-gather.6.cloned.1.call-done = bf16[2048,3072]{1,0:T(8,128)(2,1)} async-done(((bf16[128,3072]{1,0:T(8,128)(2,1)}), bf16[2048,3072]{1,0:T(8,128)(2,1)}) %all-gather.6.cloned.1.call-update) | async-done | bytes 12582928 | tf_op jit(solution)/shard_map/all_gather | solution.py:26
  318.8 13.7 %fusion.7 = bf16[2048,3072]{1,0:T(8,128)(2,1)S(1)} fusion(bf16[2048,3072]{1,0:T(8,128)(2,1)} %all-gather.6.cloned.1.call-done, bf16[2048,3072]{1,0:T(8,128)(2,1)} %all-reduce.2.cloned.1.call-done), kind=kLoop, calls=%fused_computation.12 | loop fusion | flops 75497472 | bytes 37748736 | tf_op jit(solution)/shard_map/convert_element_type | solution.py:29
  332.5 0.0 copy-start.2
  332.5 4.5 %copy-done.2 = bf16[2048,3072]{1,0:T(8,128)(2,1)} copy-done((bf16[2048,3072]{1,0:T(8,128)(2,1)}, bf16[2048,3072]{1,0:T(8,128)(2,1)S(1)}, u32[]{:S(2)}) %copy-start.2) | copy-done | bytes 12582936
  336.9 0.0 copy-done.3
  336.9 7.8 %convolution_convert_fusion.2 = bf16[2048,384]{1,0:T(8,128)(2,1)} fusion(bf16[2048,3072]{1,0:T(8,128)(2,1)S(1)} %fusion.7, bf16[384,3072]{1,0:T(8,128)(2,1)S(1)} %copy-done.3), kind=kOutput, calls=%fused_computation.19 | convolution fusion | flops 4832624640 | bytes 16515072 | tf_op jit(solution)/shard_map/dot_general | solution.py:38
  344.7 0.0 reduce-scatter.2.cloned.1.call-update
  344.7 0.0 all-gather.8.cloned.1.call-done
  344.8 10.2 %fusion.14 = bf16[384,3072]{0,1:T(8,128)(2,1)S(1)} fusion(bf16[2048,3072]{1,0:T(8,128)(2,1)} %copy-done.2, bf16[2048,384]{1,0:T(8,128)(2,1)} %all-gather.8.cloned.1.call-done), kind=kOutput, calls=%fused_computation.18 | convolution fusion | flops 4833017856 | bytes 16515072 | tf_op jit(solution)/shard_map/dot_general | solution.py:33
  355.0 2.6 copy.8
  357.6 0.0 copy-start.1
  357.6 11.9 %fusion.11 = bf16[3072,384]{1,0:T(8,128)(2,1)} fusion(bf16[2048,384]{1,0:T(8,128)(2,1)} %all-gather.4.cloned.1.call-done, bf16[2048,3072]{1,0:T(8,128)(2,1)} %all-gather.6.cloned.1.call-done), kind=kOutput, calls=%fused_computation.16 | convolution fusion | flops 4870766592 | bytes 16515072 | tf_op jit(solution)/shard_map/dot_general | solution.py:30
  369.5 8.2 %reduce-scatter.2.cloned.1.call-done = bf16[256,384]{1,0:T(8,128)(2,1)} async-done(((bf16[2048,384]{1,0:T(8,128)(2,1)}), bf16[256,384]{1,0:T(8,128)(2,1)}) %reduce-scatter.2.cloned.1.call-update) | async-done | bytes 196624 | tf_op jit(solution)/shard_map/reduce_scatter | solution.py:37
  377.7 0.0 copy-done.1
Async XLA Ops:
  7.2 30.4 %copy-start = (bf16[3072,384]{1,0:T(8,128)(2,1)S(1)}, bf16[3072,384]{1,0:T(8,128)(2,1)}, u32[]{:S(2)}) copy-start(bf16[3072,384]{1,0:T(8,128)(2,1)} %param.9) | copy-start | bytes 7077892
  7.2 30.4 %all-gather.4.cloned.1.call-start = ((), (), s32[]{:S(2)}) async-start(), calls=%async_computation.1 | async-start | bytes 1769472 | tf_op jit(solution)/shard_map/all_gather | solution.py:17
  7.9 219.1 %all-reduce.2.cloned.1.call-start = ((), (), s32[]{:S(2)}) async-start(), calls=%async_computation.2 | async-start | bytes 25165824 | tf_op jit(solution)/shard_map/psum | solution.py:20
  48.8 270.0 %all-gather.6.cloned.1.call-start = ((), (), s32[]{:S(2)}) async-start(), calls=%async_computation.3 | async-start | bytes 13369344 | tf_op jit(solution)/shard_map/all_gather | solution.py:26
  49.5 295.3 %all-gather.8.cloned.1.call-start = ((), (), s32[]{:S(2)}) async-start(), calls=%async_computation.5 | async-start | bytes 1769472 | tf_op jit(solution)/shard_map/all_gather | solution.py:16
  50.1 286.9 %copy-start.3 = (bf16[384,3072]{1,0:T(8,128)(2,1)S(1)}, bf16[384,3072]{1,0:T(8,128)(2,1)}, u32[]{:S(2)}) copy-start(bf16[384,3072]{1,0:T(8,128)(2,1)} %param.8) | copy-start | bytes 7077892
  50.1 327.6 %reduce-scatter.2.cloned.1.call-start = ((), (), s32[]{:S(2)}) async-start(), calls=%async_computation.4 | async-start | bytes 1769472 | tf_op jit(solution)/shard_map/reduce_scatter | solution.py:37
  332.5 4.5 %copy-start.2 = (bf16[2048,3072]{1,0:T(8,128)(2,1)}, bf16[2048,3072]{1,0:T(8,128)(2,1)S(1)}, u32[]{:S(2)}) copy-start(bf16[2048,3072]{1,0:T(8,128)(2,1)S(1)} %fusion.7) | copy-start | bytes 37748740
  357.6 20.1 %copy-start.1 = (bf16[3072,384]{1,0:T(8,128)(2,1)S(1)}, bf16[3072,384]{1,0:T(8,128)(2,1)}, u32[]{:S(2)}) copy-start(bf16[3072,384]{1,0:T(8,128)(2,1)} %param.9) | copy-start | bytes 7077892
Sparse Core Ops, SparseCore 0:
  9.7 27.8 all-gather.3
  48.9 178.0 all-reduce.1
  229.1 89.5 all-gather.5
  320.3 24.4 all-gather.7
  347.6 30.0 reduce-scatter.1
where the time goes:
time: 387 us; the launch traced here: 384 us
  waiting for transfers between devices  308 us (80%)
  matrix products  41 us (11%)
  between operations  13.8 us (4%)
  other arithmetic  13.7 us (4%)
  local copies, waits for them, and re-layouts  7.09 us (2%)
    psum x1, waiting for transfers between devices, on_device(): lax.psum(lax.dot_general(block, w_out, (((1,), (1,)), ((), ())), preferre...  177 us
    all_gather x1, waiting for transfers between devices, on_device(): pre_all = lax.all_gather(pre_act, 'row', axis=0, tiled=True)  91.8 us
    all_gather x1, waiting for transfers between devices, on_device(): lax.all_gather(out_grad, 'col', axis=0, tiled=True)  29.6 us
    convert_element_type x1, other arithmetic, on_device(): pre_grad = (total * slope).astype(jnp.bfloat16)  13.7 us
    dot_general x1, matrix products, on_device(): lax.dot_general(hidden, grad_all, (((0,), (0,)), ((), ())), preferred_ele...  11.9 us
    dot_general x1, matrix products, on_device(): lax.dot_general(block, w_out, (((1,), (1,)), ((), ())), preferred_element...  11.1 us
    dot_general x1, matrix products, on_device(): lax.dot_general(inputs_all, pre_grad, (((0,), (0,)), ((), ())), preferred...  10.2 us
    reduce_scatter x1, waiting for transfers between devices, on_device(): lax.psum_scatter(lax.dot_general(block, w_in, (((1,), (1,)), ((), ())), p...  8.22 us
  transfers between devices with their start and end apart: 5, of which 4 were waited for; matrix products, arithmetic and copies ran while one was open for 12% of the time, Pallas kernels for 0%

commit v1 on v0

v1 whole, which is shorter than its diff:
```python
import jax
import jax.numpy as jnp
from jax import lax
from jax.sharding import PartitionSpec as P


def gelu_parts(pre_act):
    value = pre_act.astype(jnp.float32)
    cumul = 0.5 * (1.0 + jax.scipy.special.erf(value * 0.7071067811865476))
    density = jnp.exp(-0.5 * value * value) * 0.3989422804014327
    return (value * cumul, cumul + value * density)


def gather_by_all_to_all(x, axis, n):
    rep = jnp.concatenate([x] * n, axis=0)
    return lax.all_to_all(rep, axis, 0, 0, tiled=True)


def scatter_sum_by_all_to_all(x, axis, n):
    got = lax.all_to_all(x, axis, 0, 0, tiled=True)
    got = got.reshape((n, x.shape[0] // n) + x.shape[1:])
    acc = got[0].astype(jnp.float32)
    for j in range(1, n):
        acc = acc + got[j].astype(jnp.float32)
    return acc


def on_device(inputs, out_grad, pre_act, w_in, w_out):
    n_col = lax.psum(1, "col")
    value, _ = gelu_parts(pre_act)
    hidden_loc, pre_act = lax.optimization_barrier((value.astype(jnp.bfloat16), pre_act))
    hidden_all = lax.all_gather(hidden_loc, "row", axis=0, tiled=True)
    _, slope = gelu_parts(pre_act)
    grad_all = gather_by_all_to_all(out_grad, "col", n_col)
    inputs_all = gather_by_all_to_all(inputs, "col", n_col)
    partial = lax.dot_general(
        grad_all, w_out, (((1,), (1,)), ((), ())), preferred_element_type=jnp.float32
    ).astype(jnp.bfloat16)
    total = lax.psum_scatter(partial, "row", scatter_dimension=0, tiled=True)
    pre_grad_loc = (total.astype(jnp.float32) * slope).astype(jnp.bfloat16)
    pre_grad = lax.all_gather(pre_grad_loc, "row", axis=0, tiled=True)
    w_out_grad = lax.dot_general(
        hidden_all, grad_all, (((0,), (0,)), ((), ())), preferred_element_type=jnp.float32
    ).astype(jnp.bfloat16)
    w_in_grad = lax.dot_general(
        inputs_all, pre_grad, (((0,), (0,)), ((), ())), preferred_element_type=jnp.float32
    ).astype(jnp.bfloat16)
    in_part = lax.dot_general(
        pre_grad, w_in, (((1,), (1,)), ((), ())), preferred_element_type=jnp.float32
    ).astype(jnp.bfloat16)
    in_grad = scatter_sum_by_all_to_all(in_part, "col", n_col).astype(jnp.bfloat16)
    return (in_grad, w_in_grad, w_out_grad)


def solution(mesh):
    in_specs = (P("col", "row"), P("col", "row"), P("row", "col"), P("row", "col"), P("col", "row"))
    out_specs = (P("col", "row"), P("row", "col"), P("col", "row"))
    return jax.shard_map(
        on_device, mesh=mesh, in_specs=in_specs, out_specs=out_specs, check_vma=False
    )
```

time: 387 us -> 358 us (0.925)
  waiting for transfers between devices: 308 us -> 251 us
  blocking collectives: 0 us -> 26.3 us
  starting transfers between devices: 0.19 us -> 10.7 us
  other arithmetic: 13.7 us -> 6.33 us
    psum x1 -> x0, waiting for transfers between devices: 177 us -> none  [on_device(): lax.psum(lax.dot_general(block, w_out, (((1,), (1,)), ((), ())), preferre...]
    reduce_scatter x1, waiting for transfers between devices: 8.22 us -> 93.4 us  [on_device(): total = lax.psum_scatter(partial, 'row', scatter_dimension=0, tiled=True)]
    all_gather x3 -> x2, waiting for transfers between devices: 121 us -> 157 us  [the longest x1 81.6 us: on_device(): pre_grad = lax.all_gather(pre_grad_loc, 'row', axis=0, tiled=True)]
    all_to_all x0 -> x1, blocking collectives: none -> 26.3 us  [gather_by_all_to_all(): return lax.all_to_all(rep, axis, 0, 0, tiled=True)]
    all_to_all x0 -> x2, starting transfers between devices: none -> 10.6 us  [the longest x1 5.46 us: gather_by_all_to_all(): return lax.all_to_all(rep, axis, 0, 0, tiled=True)]
    convert_element_type x1 -> x3, other arithmetic: 13.7 us -> 6.33 us  [the longest x1 2.79 us: on_device(): pre_grad_loc = (total.astype(jnp.float32) * slope).astype(jnp.bfloat16)]
  transfers between devices with their start and end apart: 5 -> 5, of which waited for: 4 -> 3; matrix products, arithmetic and copies ran while one was open for 12% -> 9% of each run, Pallas kernels for 0% -> 0%
where the time goes in v1:
time: 358 us
  waiting for transfers between devices  251 us (70%)
  matrix products  41.9 us (12%)
  blocking collectives  26.3 us (7%)
  between operations  13.9 us (4%)
  starting transfers between devices  10.7 us (3%)
  local copies, waits for them, and re-layouts  7.76 us (2%)
  other arithmetic  6.33 us (2%)
    reduce_scatter x1, waiting for transfers between devices, on_device(): total = lax.psum_scatter(partial, 'row', scatter_dimension=0, tiled=True)  93.4 us
    all_gather x1, waiting for transfers between devices, on_device(): pre_grad = lax.all_gather(pre_grad_loc, 'row', axis=0, tiled=True)  81.6 us
    all_gather x1, waiting for transfers between devices, on_device(): hidden_all = lax.all_gather(hidden_loc, 'row', axis=0, tiled=True)  75.3 us
    all_to_all x1, blocking collectives, gather_by_all_to_all(): return lax.all_to_all(rep, axis, 0, 0, tiled=True)  26.3 us
    dot_general x1, matrix products, on_device(): lax.dot_general(pre_grad, w_in, (((1,), (1,)), ((), ())), preferred_eleme...  11.3 us
    dot_general x1, matrix products, on_device(): lax.dot_general(hidden_all, grad_all, (((0,), (0,)), ((), ())), preferred...  11.3 us
    dot_general x1, matrix products, on_device(): lax.dot_general(grad_all, w_out, (((1,), (1,)), ((), ())), preferred_elem...  9.84 us
    dot_general x1, matrix products, on_device(): lax.dot_general(inputs_all, pre_grad, (((0,), (0,)), ((), ())), preferred...  9.52 us
  transfers between devices with their start and end apart: 5, of which 3 were waited for; matrix products, arithmetic and copies ran while one was open for 9% of the time, Pallas kernels for 0%

profile of v1, /device:TPU:1, one launch (start us, length us, event | category | flops | bytes accessed | tf_op | source)
XLA Modules:
  0.0 358.0 jit_solution(5899010320322639729)
XLA Ops:
  7.2 0.0 copy-start
  7.2 0.0 copy-start.1
  7.2 0.0 reduce-scatter.2.cloned.1.call-start
  7.2 1.1 constant_dynamic-update-slice_fusion.7
  8.4 1.0 constant_dynamic-update-slice_fusion.6
  9.3 1.0 constant_dynamic-update-slice_fusion.5
  10.3 1.0 constant_dynamic-update-slice_fusion.4
  11.3 0.0 copy-done.1
  11.4 26.3 %all_to_all.33 = bf16[8,256,384]{2,1,0:T(8,128)(2,1)S(1)} all-to-all(bf16[8,256,384]{2,1,0:T(8,128)(2,1)S(1)} %bitcast.15), channel_id=1, replica_groups=mesh['row'=16,'col'=8] {'col'}, dimensions={0} | all-to-all | bytes 3145728 | tf_op jit(solution)/shard_map/all_to_all | solution.py:16
  37.8 0.0 copy-start.5
  37.8 1.1 copy-done.5
  38.9 0.0 copy-done
  38.9 9.8 %convolution_convert_fusion = bf16[2048,3072]{1,0:T(8,128)(2,1)} fusion(bf16[2048,384]{1,0:T(8,128)(2,1)S(1)} %bitcast.17, bf16[3072,384]{1,0:T(8,128)(2,1)S(1)} %copy-done), kind=kOutput, calls=%fused_computation | convolution fusion | flops 4838129664 | bytes 16515072 | tf_op jit(solution)/shard_map/dot_general | solution.py:36
  48.7 0.0 copy-start.3
  48.7 0.0 reduce-scatter.2.cloned.1.call-update
  48.8 0.0 all-gather.3.cloned.1.call-start
  48.8 1.1 copy-done.3
  49.9 1.2 fusion.3
  51.1 0.0 copy-start.2
  51.1 93.4 %reduce-scatter.2.cloned.1.call-done = bf16[128,3072]{1,0:T(8,128)(2,1)} async-done(((bf16[2048,3072]{1,0:T(8,128)(2,1)}), bf16[128,3072]{1,0:T(8,128)(2,1)}) %reduce-scatter.2.cloned.1.call-update) | async-done | bytes 786448 | tf_op jit(solution)/shard_map/reduce_scatter | solution.py:39
  144.5 2.8 fusion.11
  147.3 0.0 all-gather.3.cloned.1.call-update
  147.3 0.0 all-gather.5.cloned.1.call-start
  147.4 0.7 all-gather.5.cloned.1.call-update
  148.1 0.0 copy-done.2
  148.4 0.0 copy-start.4
  148.4 1.1 copy-done.4
  149.5 5.5 %all-to-all-start.2 = ((bf16[8,256,384]{2,1,0:T(8,128)(2,1)}), bf16[8,256,384]{2,1,0:T(8,128)(2,1)}, u32[]{:S(2)}, u32[]{:S(2)}) async-start(bf16[8,256,384]{2,1,0:T(8,128)(2,1)} %bitcast.16), calls=%async_computation.3 | async-start | bytes 3145728 | tf_op jit(solution)/shard_map/all_to_all | solution.py:16
  155.0 81.6 %all-gather.3.cloned.1.call-done = bf16[2048,3072]{1,0:T(8,128)(2,1)} async-done(((bf16[128,3072]{1,0:T(8,128)(2,1)}), bf16[2048,3072]{1,0:T(8,128)(2,1)}) %all-gather.3.cloned.1.call-update) | async-done | bytes 12582928 | tf_op jit(solution)/shard_map/all_gather | solution.py:41
  236.6 11.3 %convolution_convert_fusion.3 = bf16[2048,384]{1,0:T(8,128)(2,1)} fusion(bf16[2048,3072]{1,0:T(8,128)(2,1)} %all-gather.3.cloned.1.call-done, bf16[384,3072]{1,0:T(8,128)(2,1)} %param.8), kind=kOutput, calls=%fused_computation.3 | convolution fusion | flops 4832624640 | bytes 16515072 | tf_op jit(solution)/shard_map/dot_general | solution.py:48
  247.9 0.0 all-to-all-done.2
  247.9 5.1 %all-to-all-start.1 = ((bf16[8,256,384]{2,1,0:T(8,128)(2,1)}), bf16[8,256,384]{2,1,0:T(8,128)(2,1)}, u32[]{:S(2)}, u32[]{:S(2)}) async-start(bf16[8,256,384]{2,1,0:T(8,128)(2,1)} %bitcast.19), calls=%async_computation.2 | async-start | bytes 3145728 | tf_op jit(solution)/shard_map/all_to_all | solution.py:20
  253.0 75.3 %all-gather.5.cloned.1.call-done = bf16[2048,3072]{1,0:T(8,128)(2,1)} async-done(((bf16[128,3072]{1,0:T(8,128)(2,1)}), bf16[2048,3072]{1,0:T(8,128)(2,1)}) %all-gather.5.cloned.1.call-update) | async-done | bytes 12582928 | tf_op jit(solution)/shard_map/all_gather | solution.py:32
  328.3 11.3 %convolution_convert_fusion.2 = bf16[3072,384]{1,0:T(8,128)(2,1)} fusion(bf16[2048,3072]{1,0:T(8,128)(2,1)} %all-gather.5.cloned.1.call-done, bf16[2048,384]{1,0:T(8,128)(2,1)} %bitcast.18), kind=kOutput, calls=%fused_computation.2 | convolution fusion | flops 4833017856 | bytes 16515072 | tf_op jit(solution)/shard_map/dot_general | solution.py:42
  339.6 9.5 %convolution_convert_fusion.1 = bf16[384,3072]{1,0:T(8,128)(2,1)} fusion(bf16[2048,384]{1,0:T(8,128)(2,1)} %bitcast.5, bf16[2048,3072]{1,0:T(8,128)(2,1)} %all-gather.3.cloned.1.call-done), kind=kOutput, calls=%fused_computation.1 | convolution fusion | flops 4833017856 | bytes 16515072 | tf_op jit(solution)/shard_map/dot_general | solution.py:45
  349.1 0.0 all-to-all-done.1
  349.1 2.3 fusion.12
  (12 shorter events, 0.4 us)
Async XLA Ops:
  7.2 31.7 %copy-start = (bf16[3072,384]{1,0:T(8,128)(2,1)S(1)}, bf16[3072,384]{1,0:T(8,128)(2,1)}, u32[]{:S(2)}) copy-start(bf16[3072,384]{1,0:T(8,128)(2,1)} %param.9) | copy-start | bytes 7077892
  7.2 4.1 %copy-start.1 = (bf16[256,384]{1,0:T(8,128)(2,1)S(1)}, bf16[256,384]{1,0:T(8,128)(2,1)}, u32[]{:S(2)}) copy-start(bf16[256,384]{1,0:T(8,128)(2,1)} %param.6) | copy-start | bytes 589828
  7.2 137.3 %reduce-scatter.2.cloned.1.call-start = ((), (), s32[]{:S(2)}) async-start(), calls=%async_computation.4 | async-start | bytes 13369344 | tf_op jit(solution)/shard_map/reduce_scatter | solution.py:39
  37.8 1.1 copy-start.5
  48.7 1.1 copy-start.3
  48.8 187.9 %all-gather.3.cloned.1.call-start = ((), (), s32[]{:S(2)}) async-start(), calls=%async_computation.5 | async-start | bytes 13369344 | tf_op jit(solution)/shard_map/all_gather | solution.py:41
  51.1 97.0 %copy-start.2 = (bf16[256,384]{1,0:T(8,128)(2,1)S(1)}, bf16[256,384]{1,0:T(8,128)(2,1)}, u32[]{:S(2)}) copy-start(bf16[256,384]{1,0:T(8,128)(2,1)} %param.5) | copy-start | bytes 589828
  147.3 181.0 %all-gather.5.cloned.1.call-start = ((), (), s32[]{:S(2)}) async-start(), calls=%async_computation.6 | async-start | bytes 13369344 | tf_op jit(solution)/shard_map/all_gather | solution.py:32
  148.4 1.1 copy-start.4
  149.5 98.4 %all-to-all-start.2 = ((bf16[8,256,384]{2,1,0:T(8,128)(2,1)}), bf16[8,256,384]{2,1,0:T(8,128)(2,1)}, u32[]{:S(2)}, u32[]{:S(2)}) async-start(bf16[8,256,384]{2,1,0:T(8,128)(2,1)} %bitcast.16), calls=%async_computation.3 | async-start | bytes 3145728 | tf_op jit(solution)/shard_map/all_to_all | solution.py:16
  247.9 101.2 %all-to-all-start.1 = ((bf16[8,256,384]{2,1,0:T(8,128)(2,1)}), bf16[8,256,384]{2,1,0:T(8,128)(2,1)}, u32[]{:S(2)}, u32[]{:S(2)}) async-start(bf16[8,256,384]{2,1,0:T(8,128)(2,1)} %bitcast.19), calls=%async_computation.2 | async-start | bytes 3145728 | tf_op jit(solution)/shard_map/all_to_all | solution.py:20
Sparse Core Ops, SparseCore 0:
  48.9 95.5 reduce-scatter.1
  147.4 89.1 all-gather.2
  238.8 89.4 all-gather.4

commit v2 on v1

--- a/solution.py
+++ b/solution.py
@@ -36,19 +36,27 @@
     partial = lax.dot_general(
         grad_all, w_out, (((1,), (1,)), ((), ())), preferred_element_type=jnp.float32
     ).astype(jnp.bfloat16)
+    partial, hidden_all = lax.optimization_barrier((partial, hidden_all))
     total = lax.psum_scatter(partial, "row", scatter_dimension=0, tiled=True)
     pre_grad_loc = (total.astype(jnp.float32) * slope).astype(jnp.bfloat16)
-    pre_grad = lax.all_gather(pre_grad_loc, "row", axis=0, tiled=True)
     w_out_grad = lax.dot_general(
         hidden_all, grad_all, (((0,), (0,)), ((), ())), preferred_element_type=jnp.float32
     ).astype(jnp.bfloat16)
-    w_in_grad = lax.dot_general(
-        inputs_all, pre_grad, (((0,), (0,)), ((), ())), preferred_element_type=jnp.float32
-    ).astype(jnp.bfloat16)
-    in_part = lax.dot_general(
-        pre_grad, w_in, (((1,), (1,)), ((), ())), preferred_element_type=jnp.float32
-    ).astype(jnp.bfloat16)
-    in_grad = scatter_sum_by_all_to_all(in_part, "col", n_col).astype(jnp.bfloat16)
+    n_chunk = 2
+    width = pre_grad_loc.shape[1] // n_chunk
+    w_in_parts, in_part = [], None
+    for k in range(n_chunk):
+        cols = slice(k * width, (k + 1) * width)
+        pre_grad = lax.all_gather(pre_grad_loc[:, cols], "row", axis=0, tiled=True)
+        w_in_parts.append(lax.dot_general(
+            inputs_all, pre_grad, (((0,), (0,)), ((), ())), preferred_element_type=jnp.float32
+        ).astype(jnp.bfloat16))
+        term = lax.dot_general(
+            pre_grad, w_in[:, cols], (((1,), (1,)), ((), ())), preferred_element_type=jnp.float32
+        )
+        in_part = term if in_part is None else in_part + term
+    w_in_grad = jnp.concatenate(w_in_parts, axis=1)
+    in_grad = scatter_sum_by_all_to_all(in_part.astype(jnp.bfloat16), "col", n_col).astype(jnp.bfloat16)
     return (in_grad, w_in_grad, w_out_grad)
 
 

time: 358 us -> 372 us (1.039)
  matrix products: 41.9 us -> 49.9 us
  waiting for transfers between devices: 251 us -> 258 us
  local copies, waits for them, and re-layouts: 7.76 us -> 3.77 us
    all_gather x1, waiting for transfers between devices: 75.3 us -> 56.3 us  [on_device(): hidden_all = lax.all_gather(hidden_loc, 'row', axis=0, tiled=True)]
    all_gather x1 -> x2, waiting for transfers between devices: 81.6 us -> 96.6 us  [on_device(): pre_grad = lax.all_gather(pre_grad_loc[:, cols], 'row', axis=0, tiled=True)]
    all_to_all x1, waiting for transfers between devices: 0.01 us -> 7.13 us  [scatter_sum_by_all_to_all(): got = lax.all_to_all(x, axis, 0, 0, tiled=True)]
    dot_general x1 -> x2, matrix products: 11.3 us -> 16.9 us  [on_device(): lax.dot_general(pre_grad, w_in[:, cols], (((1,), (1,)), ((), ())), prefer...]
    unnamed x26, local copies, waits for them, and re-layouts: 7.7 us -> 2.75 us
    reduce_scatter x1, waiting for transfers between devices: 93.4 us -> 97.5 us  [on_device(): total = lax.psum_scatter(partial, 'row', scatter_dimension=0, tiled=True)]
    dot_general x1 -> x2, matrix products: 9.52 us -> 11.8 us  [on_device(): lax.dot_general(inputs_all, pre_grad, (((0,), (0,)), ((), ())), preferred...]
  transfers between devices with their start and end apart: 5 -> 6, of which waited for: 3 -> 5; matrix products, arithmetic and copies ran while one was open for 9% -> 14% of each run, Pallas kernels for 0% -> 0%
where the time goes in v2:
time: 372 us; the launch traced here: 371 us
  waiting for transfers between devices  258 us (69%)
  matrix products  49.9 us (13%)
  blocking collectives  26.4 us (7%)
  between operations  14 us (4%)
  starting transfers between devices  10.7 us (3%)
  other arithmetic  8.48 us (2%)
  local copies, waits for them, and re-layouts  3.77 us (1%)
    reduce_scatter x1, waiting for transfers between devices, on_device(): total = lax.psum_scatter(partial, 'row', scatter_dimension=0, tiled=True)  97.5 us
    all_gather x2, waiting for transfers between devices, on_device(): pre_grad = lax.all_gather(pre_grad_loc[:, cols], 'row', axis=0, tiled=True)  96.6 us
    all_gather x1, waiting for transfers between devices, on_device(): hidden_all = lax.all_gather(hidden_loc, 'row', axis=0, tiled=True)  56.3 us
    all_to_all x1, blocking collectives, gather_by_all_to_all(): return lax.all_to_all(rep, axis, 0, 0, tiled=True)  26.4 us
    dot_general x2, matrix products, on_device(): lax.dot_general(pre_grad, w_in[:, cols], (((1,), (1,)), ((), ())), prefer...  16.9 us
    dot_general x2, matrix products, on_device(): lax.dot_general(inputs_all, pre_grad, (((0,), (0,)), ((), ())), preferred...  11.8 us
    dot_general x1, matrix products, on_device(): lax.dot_general(hidden_all, grad_all, (((0,), (0,)), ((), ())), preferred...  11.5 us
    dot_general x1, matrix products, on_device(): lax.dot_general(grad_all, w_out, (((1,), (1,)), ((), ())), preferred_elem...  9.75 us
  transfers between devices with their start and end apart: 6, of which 5 were waited for; matrix products, arithmetic and copies ran while one was open for 14% of the time, Pallas kernels for 0%

profile of v2, /device:TPU:1, one launch (start us, length us, event | category | flops | bytes accessed | tf_op | source)
XLA Modules:
  0.0 371.4 jit_solution(3315169167909771370)
XLA Ops:
  7.2 0.0 copy-start
  7.2 0.0 copy-start.1
  7.2 0.0 all-gather.4.cloned.1.call-start
  7.2 2.5 fusion.3
  9.8 0.0 all-gather.4.cloned.1.call-update
  9.8 0.0 reduce-scatter.2.cloned.1.call-start
  9.8 0.0 copy-done.1
  10.2 26.4 %all_to_all.33 = bf16[8,256,384]{2,1,0:T(8,128)(2,1)S(1)} all-to-all(bf16[8,256,384]{2,1,0:T(8,128)(2,1)S(1)} %bitcast.17), channel_id=1, replica_groups=mesh['row'=16,'col'=8] {'col'}, dimensions={0} | all-to-all | bytes 3145728 | tf_op jit(solution)/shard_map/all_to_all | solution.py:16
  36.5 0.0 copy-start.5
  36.5 1.1 copy-done.5
  37.7 0.0 copy-done
  37.7 9.7 %convolution_convert_fusion = bf16[2048,3072]{1,0:T(8,128)(2,1)} fusion(bf16[2048,384]{1,0:T(8,128)(2,1)S(1)} %bitcast.19, bf16[3072,384]{1,0:T(8,128)(2,1)S(1)} %copy-done), kind=kOutput, calls=%fused_computation | convolution fusion | flops 4838129664 | bytes 16515072 | tf_op jit(solution)/shard_map/dot_general | solution.py:36
  47.4 0.0 copy-start.3
  47.4 56.3 %all-gather.4.cloned.1.call-done = bf16[2048,3072]{1,0:T(8,128)(2,1)} async-done(((bf16[128,3072]{1,0:T(8,128)(2,1)}), bf16[2048,3072]{1,0:T(8,128)(2,1)}) %all-gather.4.cloned.1.call-update) | async-done | bytes 12582928 | tf_op jit(solution)/shard_map/all_gather | solution.py:32
  103.7 0.0 reduce-scatter.2.cloned.1.call-update
  103.7 0.0 all-gather.6.cloned.1.call-start
  103.8 97.5 %reduce-scatter.2.cloned.1.call-done = bf16[128,3072]{1,0:T(8,128)(2,1)} async-done(((bf16[2048,3072]{1,0:T(8,128)(2,1)}), bf16[128,3072]{1,0:T(8,128)(2,1)}) %reduce-scatter.2.cloned.1.call-update) | async-done | bytes 786448 | tf_op jit(solution)/shard_map/reduce_scatter | solution.py:40
  201.3 0.0 copy-done.3
  201.3 1.9 fusion.11
  203.2 0.0 copy-start.2
  203.2 1.0 fusion.16
  204.1 0.0 all-gather.6.cloned.1.call-update
  204.2 0.0 all-gather.8.cloned.1.call-start
  204.2 0.5 all-gather.8.cloned.1.call-update
  204.7 0.0 copy-done.2
  205.1 0.0 copy-start.4
  205.1 1.1 copy-done.4
  206.2 5.5 %all-to-all-start.2 = ((bf16[8,256,384]{2,1,0:T(8,128)(2,1)}), bf16[8,256,384]{2,1,0:T(8,128)(2,1)}, u32[]{:S(2)}, u32[]{:S(2)}) async-start(bf16[8,256,384]{2,1,0:T(8,128)(2,1)} %bitcast.18), calls=%async_computation.3 | async-start | bytes 3145728 | tf_op jit(solution)/shard_map/all_to_all | solution.py:16
  211.7 11.5 %convolution_convert_fusion.1 = bf16[3072,384]{1,0:T(8,128)(2,1)} fusion(bf16[2048,3072]{1,0:T(8,128)(2,1)} %all-gather.4.cloned.1.call-done, bf16[2048,384]{1,0:T(8,128)(2,1)} %bitcast.20), kind=kOutput, calls=%fused_computation.1 | convolution fusion | flops 4833017856 | bytes 16515072 | tf_op jit(solution)/shard_map/dot_general | solution.py:42
  223.2 41.8 %all-gather.6.cloned.1.call-done = bf16[2048,1536]{1,0:T(8,128)(2,1)} async-done(((bf16[128,1536]{1,0:T(8,128)(2,1)}), bf16[2048,1536]{1,0:T(8,128)(2,1)}) %all-gather.6.cloned.1.call-update) | async-done | bytes 6291472 | tf_op jit(solution)/shard_map/all_gather | solution.py:50
  265.0 8.2 %fusion.13 = f32[2048,384]{1,0:T(8,128)} fusion(bf16[2048,1536]{1,0:T(8,128)(2,1)} %all-gather.6.cloned.1.call-done, bf16[384,3072]{1,0:T(8,128)(2,1)} %param.8), kind=kOutput, calls=%fused_computation.25 | convolution fusion | flops 2415919104 | bytes 10616832 | tf_op jit(solution)/shard_map/dot_general | solution.py:54
  273.2 54.8 %all-gather.8.cloned.1.call-done = bf16[2048,1536]{1,0:T(8,128)(2,1)} async-done(((bf16[128,1536]{1,0:T(8,128)(2,1)}), bf16[2048,1536]{1,0:T(8,128)(2,1)}) %all-gather.8.cloned.1.call-update) | async-done | bytes 6291472 | tf_op jit(solution)/shard_map/all_gather | solution.py:50
  328.0 8.7 %add_convert_fusion = bf16[2048,384]{1,0:T(8,128)(2,1)} fusion(f32[2048,384]{1,0:T(8,128)} %fusion.13, bf16[2048,1536]{1,0:T(8,128)(2,1)} %all-gather.8.cloned.1.call-done, bf16[384,3072]{1,0:T(8,128)(2,1)} %param.8), kind=kOutput, calls=%fused_computation.2 | convolution fusion | flops 2417491968 | bytes 12189696 | tf_op jit(solution)/shard_map/dot_general | solution.py:54
  336.7 0.0 all-to-all-done.2
  336.7 5.1 %all-to-all-start.1 = ((bf16[8,256,384]{2,1,0:T(8,128)(2,1)}), bf16[8,256,384]{2,1,0:T(8,128)(2,1)}, u32[]{:S(2)}, u32[]{:S(2)}) async-start(bf16[8,256,384]{2,1,0:T(8,128)(2,1)} %bitcast.21), calls=%async_computation.2 | async-start | bytes 3145728 | tf_op jit(solution)/shard_map/all_to_all | solution.py:20
  341.8 5.9 %convolution_convert_fusion.3 = bf16[384,1536]{1,0:T(8,128)(2,1)S(1)} fusion(bf16[2048,384]{1,0:T(8,128)(2,1)} %bitcast.5, bf16[2048,1536]{1,0:T(8,128)(2,1)} %all-gather.6.cloned.1.call-done), kind=kOutput, calls=%fused_computation.4 | convolution fusion | flops 2416508928 | bytes 9043968 | tf_op jit(solution)/shard_map/dot_general | solution.py:51
  347.7 5.9 %convolution_convert_fusion.2 = bf16[384,1536]{1,0:T(8,128)(2,1)S(1)} fusion(bf16[2048,384]{1,0:T(8,128)(2,1)} %bitcast.5, bf16[2048,1536]{1,0:T(8,128)(2,1)} %all-gather.8.cloned.1.call-done), kind=kOutput, calls=%fused_computation.3 | convolution fusion | flops 2416508928 | bytes 9043968 | tf_op jit(solution)/shard_map/dot_general | solution.py:51
  353.6 1.7 pad_maximum_fusion
  355.4 7.1 %all-to-all-done.1 = bf16[8,256,384]{2,1,0:T(8,128)(2,1)} async-done(((bf16[8,256,384]{2,1,0:T(8,128)(2,1)}), bf16[8,256,384]{2,1,0:T(8,128)(2,1)}, u32[]{:S(2)}, u32[]{:S(2)}) %all-to-all-start.1) | async-done | bytes 1572896 | tf_op jit(solution)/shard_map/all_to_all | solution.py:20
  362.5 2.3 fusion.15
  (16 shorter events, 0.5 us)
Async XLA Ops:
  7.2 30.5 %copy-start = (bf16[3072,384]{1,0:T(8,128)(2,1)S(1)}, bf16[3072,384]{1,0:T(8,128)(2,1)}, u32[]{:S(2)}) copy-start(bf16[3072,384]{1,0:T(8,128)(2,1)} %param.9) | copy-start | bytes 7077892
  7.2 2.7 copy-start.1
  7.2 96.5 %all-gather.4.cloned.1.call-start = ((), (), s32[]{:S(2)}) async-start(), calls=%async_computation.4 | async-start | bytes 13369344 | tf_op jit(solution)/shard_map/all_gather | solution.py:32
  9.8 191.5 %reduce-scatter.2.cloned.1.call-start = ((), (), s32[]{:S(2)}) async-start(), calls=%async_computation.5 | async-start | bytes 13369344 | tf_op jit(solution)/shard_map/reduce_scatter | solution.py:40
  36.5 1.1 copy-start.5
  47.4 153.9 %copy-start.3 = (bf16[128,3072]{1,0:T(8,128)(2,1)S(1)}, bf16[128,3072]{1,0:T(8,128)(2,1)}, u32[]{:S(2)}) copy-start(bf16[128,3072]{1,0:T(8,128)(2,1)} %param.7) | copy-start | bytes 2359300
  103.7 161.3 %all-gather.6.cloned.1.call-start = ((), (), s32[]{:S(2)}) async-start(), calls=%async_computation.6 | async-start | bytes 6684672 | tf_op jit(solution)/shard_map/all_gather | solution.py:50
  203.2 1.6 copy-start.2
  204.2 123.8 %all-gather.8.cloned.1.call-start = ((), (), s32[]{:S(2)}) async-start(), calls=%async_computation.7 | async-start | bytes 6684672 | tf_op jit(solution)/shard_map/all_gather | solution.py:50
  205.1 1.1 copy-start.4
  206.2 130.5 %all-to-all-start.2 = ((bf16[8,256,384]{2,1,0:T(8,128)(2,1)}), bf16[8,256,384]{2,1,0:T(8,128)(2,1)}, u32[]{:S(2)}, u32[]{:S(2)}) async-start(bf16[8,256,384]{2,1,0:T(8,128)(2,1)} %bitcast.18), calls=%async_computation.3 | async-start | bytes 3145728 | tf_op jit(solution)/shard_map/all_to_all | solution.py:16
  336.7 25.8 %all-to-all-start.1 = ((bf16[8,256,384]{2,1,0:T(8,128)(2,1)}), bf16[8,256,384]{2,1,0:T(8,128)(2,1)}, u32[]{:S(2)}, u32[]{:S(2)}) async-start(bf16[8,256,384]{2,1,0:T(8,128)(2,1)} %bitcast.21), calls=%async_computation.2 | async-start | bytes 3145728 | tf_op jit(solution)/shard_map/all_to_all | solution.py:20
Sparse Core Ops, SparseCore 0:
  10.7 92.9 all-gather.3
  107.1 94.1 reduce-scatter.1
  204.3 60.6 all-gather.5
  267.0 60.9 all-gather.7

commit v3 on v1

--- a/solution.py
+++ b/solution.py
@@ -25,30 +25,51 @@
     return acc
 
 
+def gather_col_by_permutes(x, n_y):
+    n_col = 2 * n_y
+    me = lax.axis_index("col")
+    pair = [(c, c ^ 1) for c in range(n_col)]
+    other = lax.ppermute(x, "col", pair)
+    core = me % 2
+    both = jnp.where(core == 0, jnp.concatenate([x, other], 0), jnp.concatenate([other, x], 0))
+    fwd = [(c, (c + 2) % n_col) for c in range(n_col)]
+    bwd = [(c, (c - 2) % n_col) for c in range(n_col)]
+    from_prev = lax.ppermute(both, "col", fwd)
+    from_next = lax.ppermute(both, "col", bwd)
+    blocks = [both, from_next]
+    if n_y == 4:
+        blocks.append(lax.ppermute(from_prev, "col", fwd))
+    blocks.append(from_prev)
+    rel = jnp.concatenate(blocks + blocks, axis=0)
+    y = me // 2
+    rows = both.shape[0] * n_y
+    start = (n_y - y) % n_y * both.shape[0]
+    return lax.dynamic_slice_in_dim(rel, start, rows, axis=0)
+
+
 def on_device(inputs, out_grad, pre_act, w_in, w_out):
     n_col = lax.psum(1, "col")
-    value, _ = gelu_parts(pre_act)
-    hidden_loc, pre_act = lax.optimization_barrier((value.astype(jnp.bfloat16), pre_act))
-    hidden_all = lax.all_gather(hidden_loc, "row", axis=0, tiled=True)
-    _, slope = gelu_parts(pre_act)
-    grad_all = gather_by_all_to_all(out_grad, "col", n_col)
+    value, slope = gelu_parts(pre_act)
+    hidden_loc = value.astype(jnp.bfloat16)
+    grad_all = gather_col_by_permutes(out_grad, n_col // 2)
     inputs_all = gather_by_all_to_all(inputs, "col", n_col)
     partial = lax.dot_general(
         grad_all, w_out, (((1,), (1,)), ((), ())), preferred_element_type=jnp.float32
     ).astype(jnp.bfloat16)
     total = lax.psum_scatter(partial, "row", scatter_dimension=0, tiled=True)
     pre_grad_loc = (total.astype(jnp.float32) * slope).astype(jnp.bfloat16)
-    pre_grad = lax.all_gather(pre_grad_loc, "row", axis=0, tiled=True)
+    both = lax.all_gather(jnp.stack([pre_grad_loc, hidden_loc]), "row", axis=1, tiled=True)
+    pre_grad, hidden_all = both[0], both[1]
+    in_part = lax.dot_general(
+        pre_grad, w_in, (((1,), (1,)), ((), ())), preferred_element_type=jnp.float32
+    ).astype(jnp.bfloat16)
+    in_grad = scatter_sum_by_all_to_all(in_part, "col", n_col).astype(jnp.bfloat16)
     w_out_grad = lax.dot_general(
         hidden_all, grad_all, (((0,), (0,)), ((), ())), preferred_element_type=jnp.float32
     ).astype(jnp.bfloat16)
     w_in_grad = lax.dot_general(
         inputs_all, pre_grad, (((0,), (0,)), ((), ())), preferred_element_type=jnp.float32
     ).astype(jnp.bfloat16)
-    in_part = lax.dot_general(
-        pre_grad, w_in, (((1,), (1,)), ((), ())), preferred_element_type=jnp.float32
-    ).astype(jnp.bfloat16)
-    in_grad = scatter_sum_by_all_to_all(in_part, "col", n_col).astype(jnp.bfloat16)
     return (in_grad, w_in_grad, w_out_grad)
 
 

time: 358 us -> 351 us (0.980)
  blocking collectives: 26.3 us -> 0 us
  waiting for transfers between devices: 251 us -> 263 us
  starting transfers between devices: 10.7 us -> 15 us
    all_to_all x1 -> x0, blocking collectives: 26.3 us -> none  [gather_by_all_to_all(): return lax.all_to_all(rep, axis, 0, 0, tiled=True)]
    ppermute x0 -> x4, waiting for transfers between devices: none -> 20.5 us  [the longest x1 9.99 us: gather_col_by_permutes(): blocks.append(lax.ppermute(from_prev, 'col', fwd))]
    all_gather x2 -> x1, waiting for transfers between devices: 157 us -> 147 us  [on_device(): lax.all_gather(jnp.stack([pre_grad_loc, hidden_loc]), 'row', axis=1, tile...]
    ppermute x0 -> x4, starting transfers between devices: none -> 4.31 us  [the longest x1 1.46 us: gather_col_by_permutes(): other = lax.ppermute(x, 'col', pair)]
    convert_element_type x2 -> x0, other arithmetic: 3.99 us -> none  [the longest x1 2.79 us: on_device(): pre_grad_loc = (total.astype(jnp.float32) * slope).astype(jnp.bfloat16)]
    unnamed x26 -> x23, local copies, waits for them, and re-layouts: 7.7 us -> 8.92 us
  transfers between devices with their start and end apart: 5 -> 8, of which waited for: 3 -> 5; matrix products, arithmetic and copies ran while one was open for 9% -> 9% of each run, Pallas kernels for 0% -> 0%
where the time goes in v3:
time: 351 us
  waiting for transfers between devices  263 us (75%)
  matrix products  41.5 us (12%)
  starting transfers between devices  15 us (4%)
  between operations  14.2 us (4%)
  local copies, waits for them, and re-layouts  9.74 us (3%)
  other arithmetic  7.58 us (2%)
    all_gather x1, waiting for transfers between devices, on_device(): lax.all_gather(jnp.stack([pre_grad_loc, hidden_loc]), 'row', axis=1, tile...  147 us
    reduce_scatter x1, waiting for transfers between devices, on_device(): total = lax.psum_scatter(partial, 'row', scatter_dimension=0, tiled=True)  95.6 us
    dot_general x1, matrix products, on_device(): lax.dot_general(hidden_all, grad_all, (((0,), (0,)), ((), ())), preferred...  11.3 us
    dot_general x1, matrix products, on_device(): lax.dot_general(pre_grad, w_in, (((1,), (1,)), ((), ())), preferred_eleme...  11.3 us
    dot_general x1, matrix products, on_device(): lax.dot_general(grad_all, w_out, (((1,), (1,)), ((), ())), preferred_elem...  11.1 us
    ppermute x1, waiting for transfers between devices, gather_col_by_permutes(): blocks.append(lax.ppermute(from_prev, 'col', fwd))  9.99 us
    ppermute x1, waiting for transfers between devices, gather_col_by_permutes(): from_prev = lax.ppermute(both, 'col', fwd)  9.22 us
    unnamed x23, local copies, waits for them, and re-layouts  8.92 us
  transfers between devices with their start and end apart: 8, of which 5 were waited for; matrix products, arithmetic and copies ran while one was open for 9% of the time, Pallas kernels for 0%

profile of v3, /device:TPU:1, one launch (start us, length us, event | category | flops | bytes accessed | tf_op | source)
XLA Modules:
  0.0 350.8 jit_solution(14160486208016181343)
XLA Ops:
  7.2 0.0 copy-start
  7.2 0.0 reduce-scatter.2.cloned.1.call-start
  7.2 1.5 collective-permute-start
  8.7 1.3 collective-permute-done
  10.0 2.0 constant_dynamic-update-slice_fusion.7
  12.0 1.4 collective-permute-start.2
  13.4 1.4 collective-permute-start.1
  14.8 9.2 %collective-permute-done.2 = bf16[512,384]{1,0:T(8,128)(2,1)S(1)} collective-permute-done((bf16[512,384]{1,0:T(8,128)(2,1)}, bf16[512,384]{1,0:T(8,128)(2,1)S(1)}, u32[]{:S(2)}, u32[]{:S(2)}) %collective-permute-start.2) | collective-permute-done | bytes 393248 | tf_op jit(solution)/shard_map/ppermute | solution.py:37
  24.1 0.0 collective-permute-start.3
  24.1 0.0 collective-permute-done.1
  24.1 0.8 constant_dynamic-update-slice_fusion.6
  24.9 10.0 %collective-permute-done.3 = bf16[512,384]{1,0:T(8,128)(2,1)S(1)} collective-permute-done((bf16[512,384]{1,0:T(8,128)(2,1)S(1)}, bf16[512,384]{1,0:T(8,128)(2,1)S(1)}, u32[]{:S(2)}, u32[]{:S(2)}) %collective-permute-start.3) | collective-permute-done | bytes 393248 | tf_op jit(solution)/shard_map/ppermute | solution.py:41
  34.9 0.8 constant_dynamic-update-slice_fusion.5
  35.7 0.8 constant_dynamic-update-slice_fusion.4
  36.5 1.8 constant_dynamic-update-slice_fusion.3
  38.3 0.8 constant_dynamic-update-slice_fusion.2
  39.1 0.8 constant_dynamic-update-slice_fusion.1
  39.9 0.8 constant_dynamic-update-slice_fusion
  40.7 0.0 copy-done
  40.7 11.1 %convolution_convert_fusion = bf16[2048,3072]{1,0:T(8,128)(2,1)} fusion(bf16[3072,384]{1,0:T(8,128)(2,1)S(1)} %copy-done, bf16[4096,384]{1,0:T(8,128)(2,1)} %constant_dynamic-update-slice_fusion, s32[]{:T(128)S(6)} %select_n.31), kind=kOutput, calls=%fused_computation.3 | convolution fusion | flops 4838129664 | bytes 16515076 | tf_op jit(solution)/shard_map/dot_general | solution.py:56
  51.8 0.0 copy-start.3
  51.8 0.0 reduce-scatter.2.cloned.1.call-update
  51.8 0.0 all-gather.2.cloned.1.call-start
  51.8 95.6 %reduce-scatter.2.cloned.1.call-done = bf16[128,3072]{1,0:T(8,128)(2,1)} async-done(((bf16[2048,3072]{1,0:T(8,128)(2,1)}), bf16[128,3072]{1,0:T(8,128)(2,1)}) %reduce-scatter.2.cloned.1.call-update) | async-done | bytes 786448 | tf_op jit(solution)/shard_map/reduce_scatter | solution.py:59
  147.5 0.0 copy-done.3
  147.5 1.9 fusion.18
  149.4 0.0 copy-start.1
  149.5 1.3 pad_maximum_fusion
  150.7 0.0 all-gather.2.cloned.1.call-update
  150.8 0.0 copy-done.1
  151.1 0.0 copy-start.2
  151.1 1.1 copy-done.2
  152.2 5.5 %all-to-all-start.1 = ((bf16[8,256,384]{2,1,0:T(8,128)(2,1)}), bf16[8,256,384]{2,1,0:T(8,128)(2,1)}, u32[]{:S(2)}, u32[]{:S(2)}) async-start(bf16[8,256,384]{2,1,0:T(8,128)(2,1)} %bitcast.25), calls=%async_computation.2 | async-start | bytes 3145728 | tf_op jit(solution)/shard_map/all_to_all | solution.py:16
  157.7 146.7 %all-gather.2.cloned.1.call-done = bf16[2,2048,3072]{2,1,0:T(8,128)(2,1)} async-done(((bf16[2,128,3072]{2,1,0:T(8,128)(2,1)}), bf16[2,2048,3072]{2,1,0:T(8,128)(2,1)}) %all-gather.2.cloned.1.call-update) | async-done | bytes 25165840 | tf_op jit(solution)/shard_map/all_gather | solution.py:61
  304.4 11.3 %fusion.5 = bf16[2048,384]{1,0:T(8,128)(2,1)} fusion(bf16[384,3072]{1,0:T(8,128)(2,1)} %param.8, bf16[2,2048,3072]{2,1,0:T(8,128)(2,1)} %all-gather.2.cloned.1.call-done), kind=kOutput, calls=%fused_computation.13 | convolution fusion | flops 4832624640 | bytes 16515072 | tf_op jit(solution)/shard_map/dot_general | solution.py:63
  315.6 0.0 all-to-all-done.1
  315.7 5.1 %all-to-all-start = ((bf16[8,256,384]{2,1,0:T(8,128)(2,1)}), bf16[8,256,384]{2,1,0:T(8,128)(2,1)}, u32[]{:S(2)}, u32[]{:S(2)}) async-start(bf16[8,256,384]{2,1,0:T(8,128)(2,1)} %bitcast.26), calls=%async_computation.1 | async-start | bytes 3145728 | tf_op jit(solution)/shard_map/all_to_all | solution.py:20
  320.8 0.0 copy-start.4
  320.8 11.3 %fusion.4 = bf16[3072,384]{1,0:T(8,128)(2,1)} fusion(bf16[2,2048,3072]{2,1,0:T(8,128)(2,1)} %all-gather.2.cloned.1.call-done, bf16[4096,384]{1,0:T(8,128)(2,1)} %constant_dynamic-update-slice_fusion, s32[]{:T(128)S(6)} %select_n.31), kind=kOutput, calls=%fused_computation.7 | convolution fusion | flops 4833017856 | bytes 16515076 | tf_op jit(solution)/shard_map/dot_general | solution.py:67
  332.1 1.7 copy-done.4
  333.8 7.8 %fusion.3 = bf16[384,3072]{1,0:T(8,128)(2,1)} fusion(bf16[2048,384]{1,0:T(8,128)(2,1)} %bitcast.6, bf16[2,2048,3072]{2,1,0:T(8,128)(2,1)S(1)} %copy-done.4), kind=kOutput, calls=%fused_computation.6 | convolution fusion | flops 4833017856 | bytes 16515072 | tf_op jit(solution)/shard_map/dot_general | solution.py:70
  341.6 0.0 all-to-all-done
  341.6 2.3 fusion.19
  (8 shorter events, 0.3 us)
Async XLA Ops:
  7.2 33.5 %copy-start = (bf16[3072,384]{1,0:T(8,128)(2,1)S(1)}, bf16[3072,384]{1,0:T(8,128)(2,1)}, u32[]{:S(2)}) copy-start(bf16[3072,384]{1,0:T(8,128)(2,1)} %param.9) | copy-start | bytes 7077892
  7.2 140.3 %reduce-scatter.2.cloned.1.call-start = ((), (), s32[]{:S(2)}) async-start(), calls=%async_computation.3 | async-start | bytes 13369344 | tf_op jit(solution)/shard_map/reduce_scatter | solution.py:59
  7.2 2.7 collective-permute-start
  12.0 12.1 %collective-permute-start.2 = (bf16[512,384]{1,0:T(8,128)(2,1)}, bf16[512,384]{1,0:T(8,128)(2,1)S(1)}, u32[]{:S(2)}, u32[]{:S(2)}) collective-permute-start(bf16[512,384]{1,0:T(8,128)(2,1)} %get-tuple-element.4), channel_id=1, source_target_pairs={{0,2},{1,3},{2,4},{3,5},{4,6},{5,7},{6,0},{7,1},{8,10},{9,11},{10,... | collective-permute-start | bytes 1179656 | tf_op jit(solution)/shard_map/ppermute | solution.py:37
  13.4 10.7 %collective-permute-start.1 = (bf16[512,384]{1,0:T(8,128)(2,1)}, bf16[512,384]{1,0:T(8,128)(2,1)S(1)}, u32[]{:S(2)}, u32[]{:S(2)}) collective-permute-start(bf16[512,384]{1,0:T(8,128)(2,1)} %get-tuple-element.4), channel_id=1, source_target_pairs={{0,6},{1,7},{2,0},{3,1},{4,2},{5,3},{6,4},{7,5},{8,14},{9,15},{10,... | collective-permute-start | bytes 1179656 | tf_op jit(solution)/shard_map/ppermute | solution.py:38
  24.1 10.8 %collective-permute-start.3 = (bf16[512,384]{1,0:T(8,128)(2,1)S(1)}, bf16[512,384]{1,0:T(8,128)(2,1)S(1)}, u32[]{:S(2)}, u32[]{:S(2)}) collective-permute-start(bf16[512,384]{1,0:T(8,128)(2,1)S(1)} %collective-permute-done.2), channel_id=1, source_target_pairs={{0,2},{1,3},{2,4},{3,5},{4,6},{5,7},{6,0},{7,1},{8,10},{9,11},{10,... | collective-permute-start | bytes 1179656 | tf_op jit(solution)/shard_map/ppermute | solution.py:41
  51.8 95.7 %copy-start.3 = (bf16[128,3072]{1,0:T(8,128)(2,1)S(1)}, bf16[128,3072]{1,0:T(8,128)(2,1)}, u32[]{:S(2)}) copy-start(bf16[128,3072]{1,0:T(8,128)(2,1)} %param.7) | copy-start | bytes 2359300
  51.8 252.6 %all-gather.2.cloned.1.call-start = ((), (), s32[]{:S(2)}) async-start(), calls=%async_computation.4 | async-start | bytes 26738688 | tf_op jit(solution)/shard_map/all_gather | solution.py:61
  149.4 1.3 copy-start.1
  151.1 1.1 copy-start.2
  152.2 163.4 %all-to-all-start.1 = ((bf16[8,256,384]{2,1,0:T(8,128)(2,1)}), bf16[8,256,384]{2,1,0:T(8,128)(2,1)}, u32[]{:S(2)}, u32[]{:S(2)}) async-start(bf16[8,256,384]{2,1,0:T(8,128)(2,1)} %bitcast.25), calls=%async_computation.2 | async-start | bytes 3145728 | tf_op jit(solution)/shard_map/all_to_all | solution.py:16
  315.7 26.0 %all-to-all-start = ((bf16[8,256,384]{2,1,0:T(8,128)(2,1)}), bf16[8,256,384]{2,1,0:T(8,128)(2,1)}, u32[]{:S(2)}, u32[]{:S(2)}) async-start(bf16[8,256,384]{2,1,0:T(8,128)(2,1)} %bitcast.26), calls=%async_computation.1 | async-start | bytes 3145728 | tf_op jit(solution)/shard_map/all_to_all | solution.py:20
  320.8 13.1 %copy-start.4 = (bf16[2,2048,3072]{2,1,0:T(8,128)(2,1)S(1)}, bf16[2,2048,3072]{2,1,0:T(8,128)(2,1)}, u32[]{:S(2)}) copy-start(bf16[2,2048,3072]{2,1,0:T(8,128)(2,1)} %all-gather.2.cloned.1.call-done) | copy-start | bytes 75497472
Sparse Core Ops, SparseCore 0:
  51.9 95.5 reduce-scatter.1
  150.9 153.4 all-gather.1

commit v4 on v3

--- a/solution.py
+++ b/solution.py
@@ -50,23 +50,24 @@
 def on_device(inputs, out_grad, pre_act, w_in, w_out):
     n_col = lax.psum(1, "col")
     value, slope = gelu_parts(pre_act)
-    hidden_loc = value.astype(jnp.bfloat16)
-    grad_all = gather_col_by_permutes(out_grad, n_col // 2)
+    hidden_all = lax.all_gather(value.astype(jnp.bfloat16), "row", axis=0, tiled=True)
+    grad_all = gather_by_all_to_all(out_grad, "col", n_col)
     inputs_all = gather_by_all_to_all(inputs, "col", n_col)
     partial = lax.dot_general(
         grad_all, w_out, (((1,), (1,)), ((), ())), preferred_element_type=jnp.float32
     ).astype(jnp.bfloat16)
+    partial, hidden_all = lax.optimization_barrier((partial, hidden_all))
     total = lax.psum_scatter(partial, "row", scatter_dimension=0, tiled=True)
+    w_out_grad = lax.dot_general(
+        hidden_all, grad_all, (((0,), (0,)), ((), ())), preferred_element_type=jnp.float32
+    ).astype(jnp.bfloat16)
+    total, w_out_grad = lax.optimization_barrier((total, w_out_grad))
     pre_grad_loc = (total.astype(jnp.float32) * slope).astype(jnp.bfloat16)
-    both = lax.all_gather(jnp.stack([pre_grad_loc, hidden_loc]), "row", axis=1, tiled=True)
-    pre_grad, hidden_all = both[0], both[1]
+    pre_grad = lax.all_gather(pre_grad_loc, "row", axis=0, tiled=True)
     in_part = lax.dot_general(
         pre_grad, w_in, (((1,), (1,)), ((), ())), preferred_element_type=jnp.float32
     ).astype(jnp.bfloat16)
     in_grad = scatter_sum_by_all_to_all(in_part, "col", n_col).astype(jnp.bfloat16)
-    w_out_grad = lax.dot_general(
-        hidden_all, grad_all, (((0,), (0,)), ((), ())), preferred_element_type=jnp.float32
-    ).astype(jnp.bfloat16)
     w_in_grad = lax.dot_general(
         inputs_all, pre_grad, (((0,), (0,)), ((), ())), preferred_element_type=jnp.float32
     ).astype(jnp.bfloat16)

time: 351 us -> 340 us (0.969)
  blocking collectives: 0 us -> 26.4 us
  waiting for transfers between devices: 263 us -> 237 us
  local copies, waits for them, and re-layouts: 9.74 us -> 2.81 us
  starting transfers between devices: 15 us -> 10.7 us
    all_to_all x0 -> x1, blocking collectives: none -> 26.4 us  [gather_by_all_to_all(): return lax.all_to_all(rep, axis, 0, 0, tiled=True)]
    ppermute x4 -> x0, waiting for transfers between devices: 20.5 us -> none  [the longest x1 9.99 us: gather_col_by_permutes(): blocks.append(lax.ppermute(from_prev, 'col', fwd))]
    all_to_all x1, waiting for transfers between devices: 0.01 us -> 11.2 us  [scatter_sum_by_all_to_all(): got = lax.all_to_all(x, axis, 0, 0, tiled=True)]
    reduce_scatter x1, waiting for transfers between devices: 95.6 us -> 86.8 us  [on_device(): total = lax.psum_scatter(partial, 'row', scatter_dimension=0, tiled=True)]
    all_gather x1 -> x2, waiting for transfers between devices: 147 us -> 139 us  [the longest x1 82.4 us: on_device(): pre_grad = lax.all_gather(pre_grad_loc, 'row', axis=0, tiled=True)]
    unnamed x23 -> x26, local copies, waits for them, and re-layouts: 8.92 us -> 2.74 us
    convert_element_type x0 -> x2, other arithmetic: none -> 5.32 us  [the longest x1 2.78 us: on_device(): pre_grad_loc = (total.astype(jnp.float32) * slope).astype(jnp.bfloat16)]
    ppermute x4 -> x0, starting transfers between devices: 4.31 us -> none  [the longest x1 1.46 us: gather_col_by_permutes(): other = lax.ppermute(x, 'col', pair)]
  transfers between devices with their start and end apart: 8 -> 5, of which waited for: 5 -> 4; matrix products, arithmetic and copies ran while one was open for 9% -> 12% of each run, Pallas kernels for 0% -> 0%
where the time goes in v4:
time: 340 us
  waiting for transfers between devices  237 us (70%)
  matrix products  41.7 us (12%)
  blocking collectives  26.4 us (8%)
  between operations  13.9 us (4%)
  starting transfers between devices  10.7 us (3%)
  other arithmetic  7.65 us (2%)
    reduce_scatter x1, waiting for transfers between devices, on_device(): total = lax.psum_scatter(partial, 'row', scatter_dimension=0, tiled=True)  86.8 us
    all_gather x1, waiting for transfers between devices, on_device(): pre_grad = lax.all_gather(pre_grad_loc, 'row', axis=0, tiled=True)  82.4 us
    all_gather x1, waiting for transfers between devices, on_device(): lax.all_gather(value.astype(jnp.bfloat16), 'row', axis=0, tiled=True)  56.3 us
    all_to_all x1, blocking collectives, gather_by_all_to_all(): return lax.all_to_all(rep, axis, 0, 0, tiled=True)  26.4 us
    dot_general x1, matrix products, on_device(): lax.dot_general(hidden_all, grad_all, (((0,), (0,)), ((), ())), preferred...  11.3 us
    dot_general x1, matrix products, on_device(): lax.dot_general(pre_grad, w_in, (((1,), (1,)), ((), ())), preferred_eleme...  11.3 us
    all_to_all x1, waiting for transfers between devices, scatter_sum_by_all_to_all(): got = lax.all_to_all(x, axis, 0, 0, tiled=True)  11.2 us
    dot_general x1, matrix products, on_device(): lax.dot_general(grad_all, w_out, (((1,), (1,)), ((), ())), preferred_elem...  9.68 us
  transfers between devices with their start and end apart: 5, of which 4 were waited for; matrix products, arithmetic and copies ran while one was open for 12% of the time, Pallas kernels for 0%

profile of v4, /device:TPU:1, one launch (start us, length us, event | category | flops | bytes accessed | tf_op | source)
XLA Modules:
  0.0 339.9 jit_solution(11979060108080205369)
XLA Ops:
  7.2 0.0 copy-start
  7.2 0.0 copy-start.1
  7.2 0.0 all-gather.3.cloned.1.call-start
  7.2 2.5 fusion.3
  9.8 0.0 all-gather.3.cloned.1.call-update
  9.8 0.0 reduce-scatter.2.cloned.1.call-start
  9.8 0.0 copy-done.1
  10.2 26.4 %all_to_all.33 = bf16[8,256,384]{2,1,0:T(8,128)(2,1)S(1)} all-to-all(bf16[8,256,384]{2,1,0:T(8,128)(2,1)S(1)} %bitcast.15), channel_id=1, replica_groups=mesh['row'=16,'col'=8] {'col'}, dimensions={0} | all-to-all | bytes 3145728 | tf_op jit(solution)/shard_map/all_to_all | solution.py:16
  36.5 0.0 copy-start.5
  36.5 1.1 copy-done.5
  37.7 0.0 copy-done
  37.7 9.7 %convolution_convert_fusion = bf16[2048,3072]{1,0:T(8,128)(2,1)} fusion(bf16[2048,384]{1,0:T(8,128)(2,1)S(1)} %bitcast.17, bf16[3072,384]{1,0:T(8,128)(2,1)S(1)} %copy-done), kind=kOutput, calls=%fused_computation | convolution fusion | flops 4838129664 | bytes 16515072 | tf_op jit(solution)/shard_map/dot_general | solution.py:56
  47.4 56.3 %all-gather.3.cloned.1.call-done = bf16[2048,3072]{1,0:T(8,128)(2,1)} async-done(((bf16[128,3072]{1,0:T(8,128)(2,1)}), bf16[2048,3072]{1,0:T(8,128)(2,1)}) %all-gather.3.cloned.1.call-update) | async-done | bytes 12582928 | tf_op jit(solution)/shard_map/all_gather | solution.py:53
  103.7 0.0 reduce-scatter.2.cloned.1.call-update
  103.7 0.0 copy-start.3
  103.7 0.0 all-gather.5.cloned.1.call-start
  103.8 11.3 %convolution_convert_fusion.2 = bf16[3072,384]{1,0:T(8,128)(2,1)} fusion(bf16[2048,3072]{1,0:T(8,128)(2,1)} %all-gather.3.cloned.1.call-done, bf16[2048,384]{1,0:T(8,128)(2,1)} %bitcast.18), kind=kOutput, calls=%fused_computation.2 | convolution fusion | flops 4833017856 | bytes 16515072 | tf_op jit(solution)/shard_map/dot_general | solution.py:61
  115.0 0.0 copy-start.2
  115.0 86.8 %reduce-scatter.2.cloned.1.call-done = bf16[128,3072]{1,0:T(8,128)(2,1)} async-done(((bf16[2048,3072]{1,0:T(8,128)(2,1)}), bf16[128,3072]{1,0:T(8,128)(2,1)}) %reduce-scatter.2.cloned.1.call-update) | async-done | bytes 786448 | tf_op jit(solution)/shard_map/reduce_scatter | solution.py:60
  201.9 0.0 copy-done.3
  201.9 2.8 fusion.8
  204.7 0.0 all-gather.5.cloned.1.call-update
  204.7 0.0 copy-done.2
  205.0 0.0 copy-start.4
  205.0 1.1 copy-done.4
  206.2 5.5 %all-to-all-start.2 = ((bf16[8,256,384]{2,1,0:T(8,128)(2,1)}), bf16[8,256,384]{2,1,0:T(8,128)(2,1)}, u32[]{:S(2)}, u32[]{:S(2)}) async-start(bf16[8,256,384]{2,1,0:T(8,128)(2,1)} %bitcast.16), calls=%async_computation.3 | async-start | bytes 3145728 | tf_op jit(solution)/shard_map/all_to_all | solution.py:16
  211.6 82.4 %all-gather.5.cloned.1.call-done = bf16[2048,3072]{1,0:T(8,128)(2,1)} async-done(((bf16[128,3072]{1,0:T(8,128)(2,1)}), bf16[2048,3072]{1,0:T(8,128)(2,1)}) %all-gather.5.cloned.1.call-update) | async-done | bytes 12582928 | tf_op jit(solution)/shard_map/all_gather | solution.py:66
  294.0 11.3 %convolution_convert_fusion.3 = bf16[2048,384]{1,0:T(8,128)(2,1)} fusion(bf16[2048,3072]{1,0:T(8,128)(2,1)} %all-gather.5.cloned.1.call-done, bf16[384,3072]{1,0:T(8,128)(2,1)} %param.8), kind=kOutput, calls=%fused_computation.8 | convolution fusion | flops 4832624640 | bytes 16515072 | tf_op jit(solution)/shard_map/dot_general | solution.py:67
  305.2 0.0 all-to-all-done.2
  305.2 5.1 %all-to-all-start.1 = ((bf16[8,256,384]{2,1,0:T(8,128)(2,1)}), bf16[8,256,384]{2,1,0:T(8,128)(2,1)}, u32[]{:S(2)}, u32[]{:S(2)}) async-start(bf16[8,256,384]{2,1,0:T(8,128)(2,1)} %bitcast.19), calls=%async_computation.2 | async-start | bytes 3145728 | tf_op jit(solution)/shard_map/all_to_all | solution.py:20
  310.4 9.5 %convolution_convert_fusion.1 = bf16[384,3072]{1,0:T(8,128)(2,1)} fusion(bf16[2048,384]{1,0:T(8,128)(2,1)} %bitcast.5, bf16[2048,3072]{1,0:T(8,128)(2,1)} %all-gather.5.cloned.1.call-done), kind=kOutput, calls=%fused_computation.1 | convolution fusion | flops 4833017856 | bytes 16515072 | tf_op jit(solution)/shard_map/dot_general | solution.py:71
  319.9 11.2 %all-to-all-done.1 = bf16[8,256,384]{2,1,0:T(8,128)(2,1)} async-done(((bf16[8,256,384]{2,1,0:T(8,128)(2,1)}), bf16[8,256,384]{2,1,0:T(8,128)(2,1)}, u32[]{:S(2)}, u32[]{:S(2)}) %all-to-all-start.1) | async-done | bytes 1572896 | tf_op jit(solution)/shard_map/all_to_all | solution.py:20
  331.1 2.3 fusion.9
  (16 shorter events, 0.5 us)
Async XLA Ops:
  7.2 30.5 %copy-start = (bf16[3072,384]{1,0:T(8,128)(2,1)S(1)}, bf16[3072,384]{1,0:T(8,128)(2,1)}, u32[]{:S(2)}) copy-start(bf16[3072,384]{1,0:T(8,128)(2,1)} %param.9) | copy-start | bytes 7077892
  7.2 2.7 copy-start.1
  7.2 96.5 %all-gather.3.cloned.1.call-start = ((), (), s32[]{:S(2)}) async-start(), calls=%async_computation.4 | async-start | bytes 13369344 | tf_op jit(solution)/shard_map/all_gather | solution.py:53
  9.8 192.1 %reduce-scatter.2.cloned.1.call-start = ((), (), s32[]{:S(2)}) async-start(), calls=%async_computation.5 | async-start | bytes 13369344 | tf_op jit(solution)/shard_map/reduce_scatter | solution.py:60
  36.5 1.1 copy-start.5
  103.7 98.2 %copy-start.3 = (bf16[128,3072]{1,0:T(8,128)(2,1)S(1)}, bf16[128,3072]{1,0:T(8,128)(2,1)}, u32[]{:S(2)}) copy-start(bf16[128,3072]{1,0:T(8,128)(2,1)} %param.7) | copy-start | bytes 2359300
  103.7 190.3 %all-gather.5.cloned.1.call-start = ((), (), s32[]{:S(2)}) async-start(), calls=%async_computation.6 | async-start | bytes 13369344 | tf_op jit(solution)/shard_map/all_gather | solution.py:66
  115.0 89.7 %copy-start.2 = (bf16[256,384]{1,0:T(8,128)(2,1)S(1)}, bf16[256,384]{1,0:T(8,128)(2,1)}, u32[]{:S(2)}) copy-start(bf16[256,384]{1,0:T(8,128)(2,1)} %param.5) | copy-start | bytes 589828
  205.0 1.1 copy-start.4
  206.2 99.1 %all-to-all-start.2 = ((bf16[8,256,384]{2,1,0:T(8,128)(2,1)}), bf16[8,256,384]{2,1,0:T(8,128)(2,1)}, u32[]{:S(2)}, u32[]{:S(2)}) async-start(bf16[8,256,384]{2,1,0:T(8,128)(2,1)} %bitcast.16), calls=%async_computation.3 | async-start | bytes 3145728 | tf_op jit(solution)/shard_map/all_to_all | solution.py:16
  305.2 25.8 %all-to-all-start.1 = ((bf16[8,256,384]{2,1,0:T(8,128)(2,1)}), bf16[8,256,384]{2,1,0:T(8,128)(2,1)}, u32[]{:S(2)}, u32[]{:S(2)}) async-start(bf16[8,256,384]{2,1,0:T(8,128)(2,1)} %bitcast.19), calls=%async_computation.2 | async-start | bytes 3145728 | tf_op jit(solution)/shard_map/all_to_all | solution.py:20
Sparse Core Ops, SparseCore 0:
  10.7 92.9 all-gather.2
  107.1 94.7 reduce-scatter.1
  204.8 89.1 all-gather.4

commit v5 on v4

--- a/solution.py
+++ b/solution.py
@@ -47,20 +47,52 @@
     return lax.dynamic_slice_in_dim(rel, start, rows, axis=0)
 
 
+def ring_gather(x, fwd, bwd):
+    from_prev = lax.ppermute(x, "row", fwd)
+    from_next = lax.ppermute(x, "row", bwd)
+    h = x.shape[0] // 2
+    far = jnp.concatenate(
+        [lax.ppermute(from_prev[:h], "row", fwd), lax.ppermute(from_next[h:], "row", bwd)], 0
+    )
+    return jnp.stack([x, from_next, far, from_prev])
+
+
+def torus_gather(block, n_z, n_x):
+    def perm(dz, dx):
+        return [(z * n_x + x, ((z + dz) % n_z) * n_x + (x + dx) % n_x)
+                for z in range(n_z) for x in range(n_x)]
+    fx, bx, fz, bz = perm(0, 1), perm(0, -1), perm(1, 0), perm(-1, 0)
+    w = block.shape[1] // 2
+    a = ring_gather(ring_gather(block[:, :w], fx, bx), fz, bz)
+    b = ring_gather(ring_gather(block[:, w:], fz, bz), fx, bx)
+    return a, b
+
+
 def on_device(inputs, out_grad, pre_act, w_in, w_out):
     n_col = lax.psum(1, "col")
     value, slope = gelu_parts(pre_act)
-    hidden_all = lax.all_gather(value.astype(jnp.bfloat16), "row", axis=0, tiled=True)
+    hidden_loc = value.astype(jnp.bfloat16)
+    n_z, n_x = 4, 4
+    hid_a, hid_b = torus_gather(hidden_loc, n_z, n_x)
     grad_all = gather_by_all_to_all(out_grad, "col", n_col)
     inputs_all = gather_by_all_to_all(inputs, "col", n_col)
     partial = lax.dot_general(
         grad_all, w_out, (((1,), (1,)), ((), ())), preferred_element_type=jnp.float32
     ).astype(jnp.bfloat16)
-    partial, hidden_all = lax.optimization_barrier((partial, hidden_all))
     total = lax.psum_scatter(partial, "row", scatter_dimension=0, tiled=True)
-    w_out_grad = lax.dot_general(
-        hidden_all, grad_all, (((0,), (0,)), ((), ())), preferred_element_type=jnp.float32
-    ).astype(jnp.bfloat16)
+    me = lax.axis_index("row")
+    grad4 = grad_all.reshape((n_z, n_x, -1, grad_all.shape[1]))
+    grad_rel = jnp.roll(grad4, (-(me // n_x), -(me % n_x)), axis=(0, 1))
+    width = hid_a.shape[-1]
+    w_out_a = lax.dot_general(
+        hid_a.reshape(-1, width), grad_rel.reshape(-1, grad_all.shape[1]),
+        (((0,), (0,)), ((), ())), preferred_element_type=jnp.float32
+    )
+    w_out_b = lax.dot_general(
+        hid_b.reshape(-1, width), jnp.swapaxes(grad_rel, 0, 1).reshape(-1, grad_all.shape[1]),
+        (((0,), (0,)), ((), ())), preferred_element_type=jnp.float32
+    )
+    w_out_grad = jnp.concatenate([w_out_a, w_out_b], axis=0).astype(jnp.bfloat16)
     total, w_out_grad = lax.optimization_barrier((total, w_out_grad))
     pre_grad_loc = (total.astype(jnp.float32) * slope).astype(jnp.bfloat16)
     pre_grad = lax.all_gather(pre_grad_loc, "row", axis=0, tiled=True)

time: 340 us -> 338 us (level)
  waiting for transfers between devices: 237 us -> 183 us
  starting transfers between devices: 10.7 us -> 45.4 us
  local copies, waits for them, and re-layouts: 2.81 us -> 16.4 us
  other arithmetic: 7.65 us -> 13.8 us
  matrix products: 41.7 us -> 37.7 us
    ppermute x0 -> x16, waiting for transfers between devices: none -> 89.6 us  [the longest x4 70.3 us: ring_gather(): from_next = lax.ppermute(x, 'row', bwd)]
    reduce_scatter x1, waiting for transfers between devices: 86.8 us -> 6.16 us  [on_device(): total = lax.psum_scatter(partial, 'row', scatter_dimension=0, tiled=True)]
    all_gather x1 -> x0, waiting for transfers between devices: 56.3 us -> none  [on_device(): lax.all_gather(value.astype(jnp.bfloat16), 'row', axis=0, tiled=True)]
    ppermute x0 -> x16, starting transfers between devices: none -> 25 us  [the longest x4 12.6 us: ring_gather(): from_next = lax.ppermute(x, 'row', bwd)]
    all_to_all x1, starting transfers between devices: 5.46 us -> 15.2 us  [gather_by_all_to_all(): return lax.all_to_all(rep, axis, 0, 0, tiled=True)]
    unnamed x26 -> x50, local copies, waits for them, and re-layouts: 2.74 us -> 12.4 us
    another operation x0 -> x6, other arithmetic: none -> 6.04 us  [ring_gather(): return jnp.stack([x, from_next, far, from_prev])]
    all_gather x1, waiting for transfers between devices: 82.4 us -> 76.4 us  [on_device(): pre_grad = lax.all_gather(pre_grad_loc, 'row', axis=0, tiled=True)]
  transfers between devices with their start and end apart: 5 -> 20, of which waited for: 4 -> 13; matrix products, arithmetic and copies ran while one was open for 12% -> 13% of each run, Pallas kernels for 0% -> 0%
where the time goes in v5:
time: 338 us; the launch traced here: 337 us
  waiting for transfers between devices  183 us (54%)
  starting transfers between devices  45.4 us (13%)
  matrix products  37.7 us (11%)
  blocking collectives  26.3 us (8%)
  local copies, waits for them, and re-layouts  16.4 us (5%)
  between operations  14.3 us (4%)
  other arithmetic  13.8 us (4%)
    all_gather x1, waiting for transfers between devices, on_device(): pre_grad = lax.all_gather(pre_grad_loc, 'row', axis=0, tiled=True)  76.4 us
    ppermute x4, waiting for transfers between devices, ring_gather(): from_next = lax.ppermute(x, 'row', bwd)  70.3 us
    all_to_all x1, blocking collectives, gather_by_all_to_all(): return lax.all_to_all(rep, axis, 0, 0, tiled=True)  26.3 us
    all_to_all x1, starting transfers between devices, gather_by_all_to_all(): return lax.all_to_all(rep, axis, 0, 0, tiled=True)  15.2 us
    ppermute x4, starting transfers between devices, ring_gather(): from_next = lax.ppermute(x, 'row', bwd)  12.6 us
    unnamed x50, local copies, waits for them, and re-layouts  12.4 us
    ppermute x4, starting transfers between devices, ring_gather(): lax.ppermute(from_next[h:], 'row', bwd)  11.7 us
    dot_general x1, matrix products, on_device(): lax.dot_general(pre_grad, w_in, (((1,), (1,)), ((), ())), preferred_eleme...  11.2 us
  transfers between devices with their start and end apart: 20, of which 13 were waited for; matrix products, arithmetic and copies ran while one was open for 13% of the time, Pallas kernels for 0%

profile of v5, /device:TPU:1, one launch (start us, length us, event | category | flops | bytes accessed | tf_op | source)
XLA Modules:
  0.0 337.1 jit_solution(12819960291080075814)
XLA Ops:
  7.2 1.1 constant_dynamic-update-slice_fusion.7
  8.4 1.0 constant_dynamic-update-slice_fusion.6
  9.3 1.0 constant_dynamic-update-slice_fusion.5
  10.3 1.0 constant_dynamic-update-slice_fusion.4
  11.4 26.3 %all_to_all.33 = bf16[8,256,384]{2,1,0:T(8,128)(2,1)S(1)} all-to-all(bf16[8,256,384]{2,1,0:T(8,128)(2,1)S(1)} %bitcast.56), channel_id=1, replica_groups=mesh['row'=16,'col'=8] {'col'}, dimensions={0} | all-to-all | bytes 3145728 | tf_op jit(solution)/shard_map/all_to_all | solution.py:16
  37.8 1.2 copy-done.4
  38.9 9.7 %convolution_convert_fusion = bf16[2048,3072]{1,0:T(8,128)(2,1)} fusion(bf16[2048,384]{1,0:T(8,128)(2,1)S(1)} %bitcast.54, bf16[3072,384]{1,0:T(8,128)(2,1)S(1)} %copy-done), kind=kOutput, calls=%fused_computation | convolution fusion | flops 4838129664 | bytes 16515072 | tf_op jit(solution)/shard_map/dot_general | solution.py:79
  48.8 1.1 copy-done.6
  50.3 3.8 %collective-permute-start.8 = (bf16[128,1536]{1,0:T(8,128)(2,1)S(1)}, bf16[128,1536]{1,0:T(8,128)(2,1)S(1)}, u32[]{:S(2)}, u32[]{:S(2)}) collective-permute-start(bf16[128,1536]{1,0:T(8,128)(2,1)S(1)} %get-tuple-element.13), channel_id=1, source_target_pairs={{0,96},{8,104},{16,112},{24,120},{32,0},{40,8},{48,16},{56,24},{64... | collective-permute-start | bytes 1179656 | tf_op jit(solution)/shard_map/ppermute | solution.py:52
  54.1 2.5 collective-permute-start
  56.6 7.6 %collective-permute-done.8 = bf16[128,1536]{1,0:T(8,128)(2,1)S(1)} collective-permute-done((bf16[128,1536]{1,0:T(8,128)(2,1)S(1)}, bf16[128,1536]{1,0:T(8,128)(2,1)S(1)}, u32[]{:S(2)}, u32[]{:S(2)}) %collective-permute-start.8) | collective-permute-done | bytes 393248 | tf_op jit(solution)/shard_map/ppermute | solution.py:52
  64.2 3.6 %collective-permute-start.11 = (bf16[64,1536]{1,0:T(8,128)(2,1)S(1)}, bf16[64,1536]{1,0:T(8,128)(2,1)S(1)}, u32[]{:S(2)}, u32[]{:S(2)}) collective-permute-start(bf16[64,1536]{1,0:T(8,128)(2,1)S(1)} %slice.95), channel_id=1, source_target_pairs={{0,96},{8,104},{16,112},{24,120},{32,0},{40,8},{48,16},{56,24},{64... | collective-permute-start | bytes 589832 | tf_op jit(solution)/shard_map/ppermute | solution.py:55
  67.9 0.9 collective-permute-done
  68.8 3.6 %collective-permute-start.3 = (bf16[64,1536]{1,0:T(8,128)(2,1)S(1)}, bf16[64,1536]{1,0:T(8,128)(2,1)S(1)}, u32[]{:S(2)}, u32[]{:S(2)}) collective-permute-start(bf16[64,1536]{1,0:T(8,128)(2,1)S(1)} %slice.90), channel_id=1, source_target_pairs={{0,24},{8,0},{16,8},{24,16},{32,56},{40,32},{48,40},{56,48},{64,88... | collective-permute-start | bytes 589832 | tf_op jit(solution)/shard_map/ppermute | solution.py:55
  72.5 1.3 collective-permute-done.11
  73.8 3.5 %collective-permute-done.10 = bf16[64,1536]{1,0:T(8,128)(2,1)S(1)} collective-permute-done((bf16[64,1536]{1,0:T(8,128)(2,1)S(1)}, bf16[64,1536]{1,0:T(8,128)(2,1)S(1)}, u32[]{:S(2)}, u32[]{:S(2)}) %collective-permute-start.10) | collective-permute-done | bytes 196640 | tf_op jit(solution)/shard_map/ppermute | solution.py:55
  77.3 1.4 fusion.45
  78.8 3.7 %collective-permute-start.12 = (bf16[4,128,1536]{2,1,0:T(8,128)(2,1)S(1)}, bf16[4,128,1536]{2,1,0:T(8,128)(2,1)S(1)}, u32[]{:S(2)}, u32[]{:S(2)}) collective-permute-start(bf16[4,128,1536]{2,1,0:T(8,128)(2,1)S(1)} %get-tuple-element.10), channel_id=1, source_target_pairs={{0,24},{8,0},{16,8},{24,16},{32,56},{40,32},{48,40},{56,48},{64,88... | collective-permute-start | bytes 4718600 | tf_op jit(solution)/shard_map/ppermute | solution.py:52
  82.5 0.7 collective-permute-done.2
  83.3 1.4 fusion.46
  84.7 2.6 collective-permute-start.4
  87.3 61.9 %collective-permute-done.12 = bf16[4,128,1536]{2,1,0:T(8,128)(2,1)S(1)} collective-permute-done((bf16[4,128,1536]{2,1,0:T(8,128)(2,1)S(1)}, bf16[4,128,1536]{2,1,0:T(8,128)(2,1)S(1)}, u32[]{:S(2)}, u32[]{:S(2)}) %collective-permute-start.12) | collective-permute-done | bytes 1572896 | tf_op jit(solution)/shard_map/ppermute | solution.py:52
  149.2 3.6 %collective-permute-start.15 = (bf16[2,128,1536]{2,1,0:T(8,128)(2,1)S(1)}, bf16[2,128,1536]{2,1,0:T(8,128)(2,1)}, u32[]{:S(2)}, u32[]{:S(2)}) collective-permute-start(bf16[2,128,1536]{2,1,0:T(8,128)(2,1)S(1)} %slice.97), channel_id=1, source_target_pairs={{0,24},{8,0},{16,8},{24,16},{32,56},{40,32},{48,40},{56,48},{64,88... | collective-permute-start | bytes 2359304 | tf_op jit(solution)/shard_map/ppermute | solution.py:55
  153.0 1.0 slice.96
  154.0 1.0 slice.92
  155.0 0.9 collective-permute-start.7
  155.9 1.0 slice.91
  158.1 8.1 %collective-permute-done.15 = bf16[2,128,1536]{2,1,0:T(8,128)(2,1)} collective-permute-done((bf16[2,128,1536]{2,1,0:T(8,128)(2,1)S(1)}, bf16[2,128,1536]{2,1,0:T(8,128)(2,1)}, u32[]{:S(2)}, u32[]{:S(2)}) %collective-permute-start.15) | collective-permute-done | bytes 786464 | tf_op jit(solution)/shard_map/ppermute | solution.py:55
  166.2 3.4 %collective-permute-done.14 = bf16[2,128,1536]{2,1,0:T(8,128)(2,1)} collective-permute-done((bf16[2,128,1536]{2,1,0:T(8,128)(2,1)}, bf16[2,128,1536]{2,1,0:T(8,128)(2,1)}, u32[]{:S(2)}, u32[]{:S(2)}) %collective-permute-start.14) | collective-permute-done | bytes 786464 | tf_op jit(solution)/shard_map/ppermute | solution.py:55
  169.6 1.6 maximum_bitcast_fusion.1
  171.3 1.9 collective-permute-done.6
  173.2 1.5 maximum_bitcast_fusion
  174.8 3.5 %fusion.25 = bf16[1536,384]{1,0:T(8,128)(2,1)S(1)} fusion(bf16[1,4,128,1536]{3,2,1,0:T(8,128)(2,1)S(1)} %bitcast.64, bf16[1,4,128,1536]{3,2,1,0:T(8,128)(2,1)S(1)} %maximum_bitcast_fusion.1, bf16[1,4,128,1536]{3,2,1,0:T(8,128)(2,1)S(1)} %bitcast.63, bf16[1,4,128,1536]{3,2,1,0:T(8,128)(2,1)S(1)} %copy-done.8, s32[]{:T(128)S(6)} %select_n.38, ...), kind=kOutput, calls=%fused_computation.30 | convolution fusion | flops 2426732544 | bytes 9043972 | tf_op jit(solution)/shard_map/dot_general | solution.py:91
  178.4 3.5 %fusion.22 = bf16[1536,384]{1,0:T(8,128)(2,1)S(1)} fusion(bf16[1,4,128,1536]{3,2,1,0:T(8,128)(2,1)S(1)} %bitcast.66, bf16[1,4,128,1536]{3,2,1,0:T(8,128)(2,1)S(1)} %maximum_bitcast_fusion, bf16[1,4,128,1536]{3,2,1,0:T(8,128)(2,1)S(1)} %bitcast.65, bf16[1,4,128,1536]{3,2,1,0:T(8,128)(2,1)S(1)} %copy-done.9, s32[]{:T(128)S(6)} %select_n.38, ...), kind=kOutput, calls=%fused_computation.29 | convolution fusion | flops 2426732544 | bytes 9043972 | tf_op jit(solution)/shard_map/dot_general | solution.py:87
  181.9 1.6 pad_maximum_fusion
  183.6 6.2 %reduce-scatter.2.cloned.1.call-done = bf16[128,3072]{1,0:T(8,128)(2,1)} async-done(((bf16[2048,3072]{1,0:T(8,128)(2,1)}), bf16[128,3072]{1,0:T(8,128)(2,1)}) %reduce-scatter.2.cloned.1.call-update) | async-done | bytes 786448 | tf_op jit(solution)/shard_map/reduce_scatter | solution.py:82
  189.7 2.8 fusion.36
  192.5 0.7 constant_dynamic-update-slice_fusion.15
  193.2 0.7 constant_dynamic-update-slice_fusion.14
  193.9 0.7 constant_dynamic-update-slice_fusion.13
  198.1 15.2 %all-to-all-start.2 = ((bf16[8,256,384]{2,1,0:T(8,128)(2,1)}), bf16[8,256,384]{2,1,0:T(8,128)(2,1)S(1)}, u32[]{:S(2)}, u32[]{:S(2)}) async-start(bf16[8,256,384]{2,1,0:T(8,128)(2,1)} %bitcast.26), calls=%async_computation.3 | async-start | bytes 3145728 | tf_op jit(solution)/shard_map/all_to_all | solution.py:16
  213.3 76.4 %all-gather.2.cloned.1.call-done = bf16[2048,3072]{1,0:T(8,128)(2,1)} async-done(((bf16[128,3072]{1,0:T(8,128)(2,1)}), bf16[2048,3072]{1,0:T(8,128)(2,1)}) %all-gather.2.cloned.1.call-update) | async-done | bytes 12582928 | tf_op jit(solution)/shard_map/all_gather | solution.py:98
  289.7 11.2 %convolution_convert_fusion.2 = bf16[2048,384]{1,0:T(8,128)(2,1)} fusion(bf16[2048,3072]{1,0:T(8,128)(2,1)} %all-gather.2.cloned.1.call-done, bf16[384,3072]{1,0:T(8,128)(2,1)} %param.8), kind=kOutput, calls=%fused_computation.31 | convolution fusion | flops 4832624640 | bytes 16515072 | tf_op jit(solution)/shard_map/dot_general | solution.py:99
  300.9 1.1 copy-done.7
  302.1 5.1 %all-to-all-start.1 = ((bf16[8,256,384]{2,1,0:T(8,128)(2,1)}), bf16[8,256,384]{2,1,0:T(8,128)(2,1)}, u32[]{:S(2)}, u32[]{:S(2)}) async-start(bf16[8,256,384]{2,1,0:T(8,128)(2,1)} %bitcast.58), calls=%async_computation.2 | async-start | bytes 3145728 | tf_op jit(solution)/shard_map/all_to_all | solution.py:20
  307.2 9.7 %convolution_convert_fusion.1 = bf16[384,3072]{1,0:T(8,128)(2,1)} fusion(bf16[2048,384]{1,0:T(8,128)(2,1)} %bitcast.57, bf16[2048,3072]{1,0:T(8,128)(2,1)} %all-gather.2.cloned.1.call-done), kind=kOutput, calls=%fused_computation.17 | convolution fusion | flops 4833017856 | bytes 16515072 | tf_op jit(solution)/shard_map/dot_general | solution.py:103
  316.9 11.0 %all-to-all-done.1 = bf16[8,256,384]{2,1,0:T(8,128)(2,1)} async-done(((bf16[8,256,384]{2,1,0:T(8,128)(2,1)}), bf16[8,256,384]{2,1,0:T(8,128)(2,1)}, u32[]{:S(2)}, u32[]{:S(2)}) %all-to-all-start.1) | async-done | bytes 1572896 | tf_op jit(solution)/shard_map/all_to_all | solution.py:20
  327.9 2.3 fusion.40
  (72 shorter events, 6.0 us)
Async XLA Ops:
  7.2 31.8 %copy-start = (bf16[3072,384]{1,0:T(8,128)(2,1)S(1)}, bf16[3072,384]{1,0:T(8,128)(2,1)}, u32[]{:S(2)}) copy-start(bf16[3072,384]{1,0:T(8,128)(2,1)} %param.9) | copy-start | bytes 7077892
  7.2 4.1 %copy-start.2 = (bf16[256,384]{1,0:T(8,128)(2,1)S(1)}, bf16[256,384]{1,0:T(8,128)(2,1)}, u32[]{:S(2)}) copy-start(bf16[256,384]{1,0:T(8,128)(2,1)} %param.6) | copy-start | bytes 589828
  7.2 182.5 %reduce-scatter.2.cloned.1.call-start = ((), (), s32[]{:S(2)}) async-start(), calls=%async_computation.4 | async-start | bytes 13369344 | tf_op jit(solution)/shard_map/reduce_scatter | solution.py:82
  37.8 1.2 copy-start.4
  48.7 1.1 copy-start.6
  48.7 241.0 %all-gather.2.cloned.1.call-start = ((), (), s32[]{:S(2)}) async-start(), calls=%async_computation.5 | async-start | bytes 13369344 | tf_op jit(solution)/shard_map/all_gather | solution.py:98
  50.3 13.9 %collective-permute-start.8 = (bf16[128,1536]{1,0:T(8,128)(2,1)S(1)}, bf16[128,1536]{1,0:T(8,128)(2,1)S(1)}, u32[]{:S(2)}, u32[]{:S(2)}) collective-permute-start(bf16[128,1536]{1,0:T(8,128)(2,1)S(1)} %get-tuple-element.13), channel_id=1, source_target_pairs={{0,96},{8,104},{16,112},{24,120},{32,0},{40,8},{48,16},{56,24},{64... | collective-permute-start | bytes 1179656 | tf_op jit(solution)/shard_map/ppermute | solution.py:52
  54.1 13.7 %collective-permute-start.9 = (bf16[128,1536]{1,0:T(8,128)(2,1)S(1)}, bf16[128,1536]{1,0:T(8,128)(2,1)S(1)}, u32[]{:S(2)}, u32[]{:S(2)}) collective-permute-start(bf16[128,1536]{1,0:T(8,128)(2,1)S(1)} %get-tuple-element.13), channel_id=1, source_target_pairs={{0,32},{8,40},{16,48},{24,56},{32,64},{40,72},{48,80},{56,88},{64,... | collective-permute-start | bytes 1179656 | tf_op jit(solution)/shard_map/ppermute | solution.py:51
  54.1 14.7 %collective-permute-start = (bf16[128,1536]{1,0:T(8,128)(2,1)S(1)}, bf16[128,1536]{1,0:T(8,128)(2,1)S(1)}, u32[]{:S(2)}, u32[]{:S(2)}) collective-permute-start(bf16[128,1536]{1,0:T(8,128)(2,1)S(1)} %get-tuple-element.14), channel_id=1, source_target_pairs={{0,24},{8,0},{16,8},{24,16},{32,56},{40,32},{48,40},{56,48},{64,88... | collective-permute-start | bytes 1179656 | tf_op jit(solution)/shard_map/ppermute | solution.py:52
  56.6 15.8 %collective-permute-start.1 = (bf16[128,1536]{1,0:T(8,128)(2,1)S(1)}, bf16[128,1536]{1,0:T(8,128)(2,1)S(1)}, u32[]{:S(2)}, u32[]{:S(2)}) collective-permute-start(bf16[128,1536]{1,0:T(8,128)(2,1)S(1)} %get-tuple-element.14), channel_id=1, source_target_pairs={{0,8},{8,16},{16,24},{24,0},{32,40},{40,48},{48,56},{56,32},{64,72... | collective-permute-start | bytes 1179656 | tf_op jit(solution)/shard_map/ppermute | solution.py:51
  64.2 9.6 %collective-permute-start.11 = (bf16[64,1536]{1,0:T(8,128)(2,1)S(1)}, bf16[64,1536]{1,0:T(8,128)(2,1)S(1)}, u32[]{:S(2)}, u32[]{:S(2)}) collective-permute-start(bf16[64,1536]{1,0:T(8,128)(2,1)S(1)} %slice.95), channel_id=1, source_target_pairs={{0,96},{8,104},{16,112},{24,120},{32,0},{40,8},{48,16},{56,24},{64... | collective-permute-start | bytes 589832 | tf_op jit(solution)/shard_map/ppermute | solution.py:55
  67.8 9.5 %collective-permute-start.10 = (bf16[64,1536]{1,0:T(8,128)(2,1)S(1)}, bf16[64,1536]{1,0:T(8,128)(2,1)S(1)}, u32[]{:S(2)}, u32[]{:S(2)}) collective-permute-start(bf16[64,1536]{1,0:T(8,128)(2,1)S(1)} %slice.94), channel_id=1, source_target_pairs={{0,32},{8,40},{16,48},{24,56},{32,64},{40,72},{48,80},{56,88},{64,... | collective-permute-start | bytes 589832 | tf_op jit(solution)/shard_map/ppermute | solution.py:55
  68.8 13.7 %collective-permute-start.3 = (bf16[64,1536]{1,0:T(8,128)(2,1)S(1)}, bf16[64,1536]{1,0:T(8,128)(2,1)S(1)}, u32[]{:S(2)}, u32[]{:S(2)}) collective-permute-start(bf16[64,1536]{1,0:T(8,128)(2,1)S(1)} %slice.90), channel_id=1, source_target_pairs={{0,24},{8,0},{16,8},{24,16},{32,56},{40,32},{48,40},{56,48},{64,88... | collective-permute-start | bytes 589832 | tf_op jit(solution)/shard_map/ppermute | solution.py:55
  72.4 10.9 %collective-permute-start.2 = (bf16[64,1536]{1,0:T(8,128)(2,1)S(1)}, bf16[64,1536]{1,0:T(8,128)(2,1)S(1)}, u32[]{:S(2)}, u32[]{:S(2)}) collective-permute-start(bf16[64,1536]{1,0:T(8,128)(2,1)S(1)} %slice.89), channel_id=1, source_target_pairs={{0,8},{8,16},{16,24},{24,0},{32,40},{40,48},{48,56},{56,32},{64,72... | collective-permute-start | bytes 589832 | tf_op jit(solution)/shard_map/ppermute | solution.py:55
  78.8 70.4 %collective-permute-start.12 = (bf16[4,128,1536]{2,1,0:T(8,128)(2,1)S(1)}, bf16[4,128,1536]{2,1,0:T(8,128)(2,1)S(1)}, u32[]{:S(2)}, u32[]{:S(2)}) collective-permute-start(bf16[4,128,1536]{2,1,0:T(8,128)(2,1)S(1)} %get-tuple-element.10), channel_id=1, source_target_pairs={{0,24},{8,0},{16,8},{24,16},{32,56},{40,32},{48,40},{56,48},{64,88... | collective-permute-start | bytes 4718600 | tf_op jit(solution)/shard_map/ppermute | solution.py:52
  82.5 70.5 %collective-permute-start.13 = (bf16[4,128,1536]{2,1,0:T(8,128)(2,1)S(1)}, bf16[4,128,1536]{2,1,0:T(8,128)(2,1)S(1)}, u32[]{:S(2)}, u32[]{:S(2)}) collective-permute-start(bf16[4,128,1536]{2,1,0:T(8,128)(2,1)S(1)} %get-tuple-element.10), channel_id=1, source_target_pairs={{0,8},{8,16},{16,24},{24,0},{32,40},{40,48},{48,56},{56,32},{64,72... | collective-permute-start | bytes 4718600 | tf_op jit(solution)/shard_map/ppermute | solution.py:51
  84.7 69.3 %collective-permute-start.4 = (bf16[4,128,1536]{2,1,0:T(8,128)(2,1)S(1)}, bf16[4,128,1536]{2,1,0:T(8,128)(2,1)S(1)}, u32[]{:S(2)}, u32[]{:S(2)}) collective-permute-start(bf16[4,128,1536]{2,1,0:T(8,128)(2,1)S(1)} %get-tuple-element.8), channel_id=1, source_target_pairs={{0,96},{8,104},{16,112},{24,120},{32,0},{40,8},{48,16},{56,24},{64... | collective-permute-start | bytes 4718600 | tf_op jit(solution)/shard_map/ppermute | solution.py:52
  87.3 68.7 %collective-permute-start.5 = (bf16[4,128,1536]{2,1,0:T(8,128)(2,1)S(1)}, bf16[4,128,1536]{2,1,0:T(8,128)(2,1)S(1)}, u32[]{:S(2)}, u32[]{:S(2)}) collective-permute-start(bf16[4,128,1536]{2,1,0:T(8,128)(2,1)S(1)} %get-tuple-element.8), channel_id=1, source_target_pairs={{0,32},{8,40},{16,48},{24,56},{32,64},{40,72},{48,80},{56,88},{64,... | collective-permute-start | bytes 4718600 | tf_op jit(solution)/shard_map/ppermute | solution.py:51
  149.1 4.9 %copy-start.10 = (bf16[4,128,1536]{2,1,0:T(8,128)(2,1)}, bf16[4,128,1536]{2,1,0:T(8,128)(2,1)S(1)}, u32[]{:S(2)}) copy-start(bf16[4,128,1536]{2,1,0:T(8,128)(2,1)S(1)} %collective-permute-done.12) | copy-start | bytes 4718596
  149.2 17.0 %collective-permute-start.15 = (bf16[2,128,1536]{2,1,0:T(8,128)(2,1)S(1)}, bf16[2,128,1536]{2,1,0:T(8,128)(2,1)}, u32[]{:S(2)}, u32[]{:S(2)}) collective-permute-start(bf16[2,128,1536]{2,1,0:T(8,128)(2,1)S(1)} %slice.97), channel_id=1, source_target_pairs={{0,24},{8,0},{16,8},{24,16},{32,56},{40,32},{48,40},{56,48},{64,88... | collective-permute-start | bytes 2359304 | tf_op jit(solution)/shard_map/ppermute | solution.py:55
  153.0 2.0 copy-start.12
  154.0 3.5 %copy-start.5 = (bf16[8,256,384]{2,1,0:T(8,128)(2,1)S(1)}, bf16[8,256,384]{2,1,0:T(8,128)(2,1)}, u32[]{:S(2)}) copy-start(bf16[8,256,384]{2,1,0:T(8,128)(2,1)} %copy-done.4) | copy-start | bytes 4718596
  154.0 15.6 %collective-permute-start.14 = (bf16[2,128,1536]{2,1,0:T(8,128)(2,1)}, bf16[2,128,1536]{2,1,0:T(8,128)(2,1)}, u32[]{:S(2)}, u32[]{:S(2)}) collective-permute-start(bf16[2,128,1536]{2,1,0:T(8,128)(2,1)} %slice.96), channel_id=1, source_target_pairs={{0,8},{8,16},{16,24},{24,0},{32,40},{40,48},{48,56},{56,32},{64,72... | collective-permute-start | bytes 2359304 | tf_op jit(solution)/shard_map/ppermute | solution.py:55
  154.0 2.9 copy-start.14
  155.0 16.3 %collective-permute-start.7 = (bf16[2,128,1536]{2,1,0:T(8,128)(2,1)}, bf16[2,128,1536]{2,1,0:T(8,128)(2,1)}, u32[]{:S(2)}, u32[]{:S(2)}) collective-permute-start(bf16[2,128,1536]{2,1,0:T(8,128)(2,1)} %slice.92), channel_id=1, source_target_pairs={{0,96},{8,104},{16,112},{24,120},{32,0},{40,8},{48,16},{56,24},{64... | collective-permute-start | bytes 2359304 | tf_op jit(solution)/shard_map/ppermute | solution.py:55
  155.9 1.5 copy-start.16
  157.0 16.3 %collective-permute-start.6 = (bf16[2,128,1536]{2,1,0:T(8,128)(2,1)}, bf16[2,128,1536]{2,1,0:T(8,128)(2,1)}, u32[]{:S(2)}, u32[]{:S(2)}) collective-permute-start(bf16[2,128,1536]{2,1,0:T(8,128)(2,1)} %slice.91), channel_id=1, source_target_pairs={{0,32},{8,40},{16,48},{24,56},{32,64},{40,72},{48,80},{56,88},{64,... | collective-permute-start | bytes 2359304 | tf_op jit(solution)/shard_map/ppermute | solution.py:55
  169.6 5.2 %copy-start.13 = (bf16[4,128,1536]{2,1,0:T(8,128)(2,1)S(1)}, bf16[4,128,1536]{2,1,0:T(8,128)(2,1)}, u32[]{:S(2)}) copy-start(bf16[4,128,1536]{2,1,0:T(8,128)(2,1)} %copy-done.12) | copy-start | bytes 4718596
  171.3 3.5 %copy-start.8 = (bf16[1,4,128,1536]{3,2,1,0:T(8,128)(2,1)S(1)}, bf16[1,4,128,1536]{3,2,1,0:T(8,128)(2,1)}, u32[]{:S(2)}) copy-start(bf16[1,4,128,1536]{3,2,1,0:T(8,128)(2,1)} %get-tuple-element.9) | copy-start | bytes 4718596
  171.3 3.5 %copy-start.11 = (bf16[4,128,1536]{2,1,0:T(8,128)(2,1)S(1)}, bf16[4,128,1536]{2,1,0:T(8,128)(2,1)}, u32[]{:S(2)}) copy-start(bf16[4,128,1536]{2,1,0:T(8,128)(2,1)} %copy-done.10) | copy-start | bytes 4718596
  174.8 3.6 %copy-start.9 = (bf16[1,4,128,1536]{3,2,1,0:T(8,128)(2,1)S(1)}, bf16[1,4,128,1536]{3,2,1,0:T(8,128)(2,1)}, u32[]{:S(2)}) copy-start(bf16[1,4,128,1536]{3,2,1,0:T(8,128)(2,1)} %get-tuple-element.7) | copy-start | bytes 4718596
  174.8 3.6 %copy-start.15 = (bf16[4,128,1536]{2,1,0:T(8,128)(2,1)S(1)}, bf16[4,128,1536]{2,1,0:T(8,128)(2,1)}, u32[]{:S(2)}) copy-start(bf16[4,128,1536]{2,1,0:T(8,128)(2,1)} %copy-done.14) | copy-start | bytes 4718596
  174.8 3.6 %copy-start.17 = (bf16[4,128,1536]{2,1,0:T(8,128)(2,1)S(1)}, bf16[4,128,1536]{2,1,0:T(8,128)(2,1)}, u32[]{:S(2)}) copy-start(bf16[4,128,1536]{2,1,0:T(8,128)(2,1)} %copy-done.16) | copy-start | bytes 4718596
  183.6 9.0 %copy-start.3 = (bf16[256,384]{1,0:T(8,128)(2,1)S(1)}, bf16[256,384]{1,0:T(8,128)(2,1)}, u32[]{:S(2)}) copy-start(bf16[256,384]{1,0:T(8,128)(2,1)} %param.5) | copy-start | bytes 589828
  198.1 102.8 %all-to-all-start.2 = ((bf16[8,256,384]{2,1,0:T(8,128)(2,1)}), bf16[8,256,384]{2,1,0:T(8,128)(2,1)S(1)}, u32[]{:S(2)}, u32[]{:S(2)}) async-start(bf16[8,256,384]{2,1,0:T(8,128)(2,1)} %bitcast.26), calls=%async_computation.3 | async-start | bytes 3145728 | tf_op jit(solution)/shard_map/all_to_all | solution.py:16
  300.9 1.1 copy-start.7
  302.1 25.8 %all-to-all-start.1 = ((bf16[8,256,384]{2,1,0:T(8,128)(2,1)}), bf16[8,256,384]{2,1,0:T(8,128)(2,1)}, u32[]{:S(2)}, u32[]{:S(2)}) async-start(bf16[8,256,384]{2,1,0:T(8,128)(2,1)} %bitcast.58), calls=%async_computation.2 | async-start | bytes 3145728 | tf_op jit(solution)/shard_map/all_to_all | solution.py:20
  307.2 23.0 %copy-start.1 = (bf16[3072,384]{1,0:T(8,128)(2,1)S(1)}, bf16[3072,384]{1,0:T(8,128)(2,1)}, u32[]{:S(2)}) copy-start(bf16[3072,384]{1,0:T(8,128)(2,1)} %param.9) | copy-start | bytes 7077892
Sparse Core Ops, SparseCore 0:
  48.8 140.8 reduce-scatter.1
  192.7 97.0 all-gather.1

commit v6 on v5

--- a/solution.py
+++ b/solution.py
@@ -57,15 +57,18 @@
     return jnp.stack([x, from_next, far, from_prev])
 
 
-def torus_gather(block, n_z, n_x):
+def torus_gather(block, n_z, n_x, after):
     def perm(dz, dx):
         return [(z * n_x + x, ((z + dz) % n_z) * n_x + (x + dx) % n_x)
                 for z in range(n_z) for x in range(n_x)]
     fx, bx, fz, bz = perm(0, 1), perm(0, -1), perm(1, 0), perm(-1, 0)
     w = block.shape[1] // 2
-    a = ring_gather(ring_gather(block[:, :w], fx, bx), fz, bz)
-    b = ring_gather(ring_gather(block[:, w:], fz, bz), fx, bx)
-    return a, b
+    a1 = ring_gather(block[:, :w], fx, bx)
+    b1 = ring_gather(block[:, w:], fz, bz)
+    a1, b1, after = lax.optimization_barrier((a1, b1, after))
+    a = ring_gather(a1, fz, bz)
+    b = ring_gather(b1, fx, bx)
+    return a, b, after
 
 
 def on_device(inputs, out_grad, pre_act, w_in, w_out):
@@ -73,8 +76,8 @@
     value, slope = gelu_parts(pre_act)
     hidden_loc = value.astype(jnp.bfloat16)
     n_z, n_x = 4, 4
-    hid_a, hid_b = torus_gather(hidden_loc, n_z, n_x)
     grad_all = gather_by_all_to_all(out_grad, "col", n_col)
+    hid_a, hid_b, grad_all = torus_gather(hidden_loc, n_z, n_x, grad_all)
     inputs_all = gather_by_all_to_all(inputs, "col", n_col)
     partial = lax.dot_general(
         grad_all, w_out, (((1,), (1,)), ((), ())), preferred_element_type=jnp.float32

time: 338 us -> 330 us (0.976)
  blocking collectives: 26.3 us -> 0 us
  waiting for transfers between devices: 183 us -> 200 us
  other arithmetic: 13.8 us -> 18.3 us
    ppermute x4, waiting for transfers between devices: 70.3 us -> 1.63 us  [ring_gather(): from_next = lax.ppermute(x, 'row', bwd)]
    ppermute x4, waiting for transfers between devices: 0.22 us -> 53.7 us  [ring_gather(): from_prev = lax.ppermute(x, 'row', fwd)]
    all_to_all x1 -> x0, blocking collectives: 26.3 us -> none  [gather_by_all_to_all(): return lax.all_to_all(rep, axis, 0, 0, tiled=True)]
    ppermute x4, waiting for transfers between devices: 9.63 us -> 33.1 us  [ring_gather(): lax.ppermute(from_prev[:h], 'row', fwd)]
    reduce_scatter x1, waiting for transfers between devices: 6.16 us -> 19 us  [on_device(): total = lax.psum_scatter(partial, 'row', scatter_dimension=0, tiled=True)]
    ppermute x4, waiting for transfers between devices: 9.41 us -> 2.77 us  [ring_gather(): lax.ppermute(from_next[h:], 'row', bwd)]
    unnamed x50 -> x48, local copies, waits for them, and re-layouts: 12.4 us -> 7.45 us
    all_to_all x1 -> x2, starting transfers between devices: 15.2 us -> 11.1 us  [gather_by_all_to_all(): return lax.all_to_all(rep, axis, 0, 0, tiled=True)]
  transfers between devices with their start and end apart: 20 -> 21, of which waited for: 13 -> 13; matrix products, arithmetic and copies ran while one was open for 13% -> 15% of each run, Pallas kernels for 0% -> 0%
where the time goes in v6:
time: 330 us; the launch traced here: 329 us
  waiting for transfers between devices  200 us (61%)
  starting transfers between devices  43.5 us (13%)
  matrix products  39.1 us (12%)
  other arithmetic  18.3 us (6%)
  between operations  14.4 us (4%)
  local copies, waits for them, and re-layouts  14.1 us (4%)
    all_gather x1, waiting for transfers between devices, on_device(): pre_grad = lax.all_gather(pre_grad_loc, 'row', axis=0, tiled=True)  78.3 us
    ppermute x4, waiting for transfers between devices, ring_gather(): from_prev = lax.ppermute(x, 'row', fwd)  53.7 us
    ppermute x4, waiting for transfers between devices, ring_gather(): lax.ppermute(from_prev[:h], 'row', fwd)  33.1 us
    reduce_scatter x1, waiting for transfers between devices, on_device(): total = lax.psum_scatter(partial, 'row', scatter_dimension=0, tiled=True)  19 us
    ppermute x4, starting transfers between devices, ring_gather(): lax.ppermute(from_next[h:], 'row', bwd)  13.3 us
    ppermute x4, starting transfers between devices, ring_gather(): from_next = lax.ppermute(x, 'row', bwd)  12.3 us
    dot_general x1, matrix products, on_device(): lax.dot_general(pre_grad, w_in, (((1,), (1,)), ((), ())), preferred_eleme...  11.2 us
    dot_general x1, matrix products, on_device(): lax.dot_general(grad_all, w_out, (((1,), (1,)), ((), ())), preferred_elem...  11.2 us
  transfers between devices with their start and end apart: 21, of which 13 were waited for; matrix products, arithmetic and copies ran while one was open for 15% of the time, Pallas kernels for 0%

profile of v6, /device:TPU:1, one launch (start us, length us, event | category | flops | bytes accessed | tf_op | source)
XLA Modules:
  0.0 328.9 jit_solution(3319773199391890601)
XLA Ops:
  7.2 1.6 fusion.31
  8.8 1.0 slice_bitcast_fusion
  9.8 4.6 %collective-permute-start.4 = (bf16[128,1536]{1,0:T(8,128)(2,1)}, bf16[128,1536]{1,0:T(8,128)(2,1)S(1)}, u32[]{:S(2)}, u32[]{:S(2)}) collective-permute-start(bf16[128,1536]{1,0:T(8,128)(2,1)} %get-tuple-element.15), channel_id=1, source_target_pairs={{0,96},{8,104},{16,112},{24,120},{32,0},{40,8},{48,16},{56,24},{64... | collective-permute-start | bytes 1179656 | tf_op jit(solution)/shard_map/ppermute | solution.py:52
  14.4 2.5 collective-permute-start
  17.2 1.1 copy-done.5
  18.3 5.7 %all-to-all-start = ((bf16[8,256,384]{2,1,0:T(8,128)(2,1)}), bf16[8,256,384]{2,1,0:T(8,128)(2,1)}, u32[]{:S(2)}, u32[]{:S(2)}) async-start(bf16[8,256,384]{2,1,0:T(8,128)(2,1)} %bitcast.52), calls=%async_computation | async-start | bytes 3145728 | tf_op jit(solution)/shard_map/all_to_all | solution.py:16
  24.1 3.0 collective-permute-start.7
  27.1 0.9 slice.92
  28.1 0.9 slice.90
  29.1 3.0 collective-permute-start.3
  32.1 0.9 slice.89
  33.1 2.1 collective-permute-done.6
  35.3 0.7 collective-permute-done.3
  36.0 4.1 %collective-permute-done.2 = bf16[64,1536]{1,0:T(8,128)(2,1)S(1)} collective-permute-done((bf16[64,1536]{1,0:T(8,128)(2,1)S(1)}, bf16[64,1536]{1,0:T(8,128)(2,1)S(1)}, u32[]{:S(2)}, u32[]{:S(2)}) %collective-permute-start.2) | collective-permute-done | bytes 196640 | tf_op jit(solution)/shard_map/ppermute | solution.py:55
  40.2 2.3 pad_maximum_fusion.2
  42.5 2.5 pad_maximum_fusion.1
  45.0 11.2 %convolution_convert_fusion = bf16[2048,3072]{1,0:T(8,128)(2,1)} fusion(bf16[2048,384]{1,0:T(8,128)(2,1)} %bitcast.9, bf16[3072,384]{1,0:T(8,128)(2,1)S(1)} %copy-done), kind=kOutput, calls=%fused_computation | convolution fusion | flops 4838129664 | bytes 16515072 | tf_op jit(solution)/shard_map/dot_general | solution.py:82
  56.3 2.7 collective-permute-start.8
  59.5 2.5 collective-permute-start.12
  62.0 53.6 %collective-permute-done.9 = bf16[4,128,1536]{2,1,0:T(8,128)(2,1)S(1)} collective-permute-done((bf16[4,128,1536]{2,1,0:T(8,128)(2,1)}, bf16[4,128,1536]{2,1,0:T(8,128)(2,1)S(1)}, u32[]{:S(2)}, u32[]{:S(2)}) %collective-permute-start.9) | collective-permute-done | bytes 1572896 | tf_op jit(solution)/shard_map/ppermute | solution.py:51
  115.7 1.6 collective-permute-done.8
  117.4 3.5 %collective-permute-start.11 = (bf16[2,128,1536]{2,1,0:T(8,128)(2,1)S(1)}, bf16[2,128,1536]{2,1,0:T(8,128)(2,1)}, u32[]{:S(2)}, u32[]{:S(2)}) collective-permute-start(bf16[2,128,1536]{2,1,0:T(8,128)(2,1)S(1)} %slice.95), channel_id=1, source_target_pairs={{0,96},{8,104},{16,112},{24,120},{32,0},{40,8},{48,16},{56,24},{64... | collective-permute-start | bytes 2359304 | tf_op jit(solution)/shard_map/ppermute | solution.py:55
  121.0 1.0 slice.96
  122.0 0.9 collective-permute-start.14
  122.9 1.0 slice.97
  123.9 3.7 %collective-permute-start.15 = (bf16[2,128,1536]{2,1,0:T(8,128)(2,1)}, bf16[2,128,1536]{2,1,0:T(8,128)(2,1)}, u32[]{:S(2)}, u32[]{:S(2)}) collective-permute-start(bf16[2,128,1536]{2,1,0:T(8,128)(2,1)} %slice.97), channel_id=1, source_target_pairs={{0,24},{8,0},{16,8},{24,16},{32,56},{40,32},{48,40},{56,48},{64,88... | collective-permute-start | bytes 2359304 | tf_op jit(solution)/shard_map/ppermute | solution.py:55
  127.7 2.1 fusion.38
  129.7 21.9 %collective-permute-done.10 = bf16[2,128,1536]{2,1,0:T(8,128)(2,1)} collective-permute-done((bf16[2,128,1536]{2,1,0:T(8,128)(2,1)S(1)}, bf16[2,128,1536]{2,1,0:T(8,128)(2,1)}, u32[]{:S(2)}, u32[]{:S(2)}) %collective-permute-start.10) | collective-permute-done | bytes 786464 | tf_op jit(solution)/shard_map/ppermute | solution.py:55
  151.6 1.8 collective-permute-done.11
  153.5 1.5 maximum_bitcast_fusion
  155.0 5.0 %collective-permute-done.14 = bf16[2,128,1536]{2,1,0:T(8,128)(2,1)} collective-permute-done((bf16[2,128,1536]{2,1,0:T(8,128)(2,1)}, bf16[2,128,1536]{2,1,0:T(8,128)(2,1)}, u32[]{:S(2)}, u32[]{:S(2)}) %collective-permute-start.14) | collective-permute-done | bytes 786464 | tf_op jit(solution)/shard_map/ppermute | solution.py:55
  160.1 1.5 maximum_bitcast_fusion.1
  161.7 3.5 %fusion.25 = bf16[1536,384]{1,0:T(8,128)(2,1)S(1)} fusion(bf16[1,4,128,1536]{3,2,1,0:T(8,128)(2,1)S(1)} %bitcast.60, bf16[1,4,128,1536]{3,2,1,0:T(8,128)(2,1)S(1)} %maximum_bitcast_fusion.1, bf16[1,4,128,1536]{3,2,1,0:T(8,128)(2,1)S(1)} %bitcast.61, bf16[1,4,128,1536]{3,2,1,0:T(8,128)(2,1)S(1)} %bitcast.53, s32[]{:T(128)S(6)} %select_n.38, ...), kind=kOutput, calls=%fused_computation.30 | convolution fusion | flops 2426732544 | bytes 9043972 | tf_op jit(solution)/shard_map/dot_general | solution.py:94
  165.3 3.5 %fusion.22 = bf16[1536,384]{1,0:T(8,128)(2,1)S(1)} fusion(bf16[1,4,128,1536]{3,2,1,0:T(8,128)(2,1)S(1)} %bitcast.58, bf16[1,4,128,1536]{3,2,1,0:T(8,128)(2,1)S(1)} %maximum_bitcast_fusion, bf16[1,4,128,1536]{3,2,1,0:T(8,128)(2,1)S(1)} %bitcast.59, bf16[1,4,128,1536]{3,2,1,0:T(8,128)(2,1)S(1)} %bitcast.54, s32[]{:T(128)S(6)} %select_n.38, ...), kind=kOutput, calls=%fused_computation.29 | convolution fusion | flops 2426732544 | bytes 9043972 | tf_op jit(solution)/shard_map/dot_general | solution.py:90
  168.8 1.6 pad_maximum_fusion
  170.4 19.0 %reduce-scatter.2.cloned.1.call-done = bf16[128,3072]{1,0:T(8,128)(2,1)} async-done(((bf16[2048,3072]{1,0:T(8,128)(2,1)}), bf16[128,3072]{1,0:T(8,128)(2,1)}) %reduce-scatter.2.cloned.1.call-update) | async-done | bytes 786448 | tf_op jit(solution)/shard_map/reduce_scatter | solution.py:85
  189.4 2.8 fusion.36
  192.2 0.7 constant_dynamic-update-slice_fusion.15
  192.9 0.7 constant_dynamic-update-slice_fusion.14
  195.0 0.7 constant_dynamic-update-slice_fusion.11
  197.8 5.4 %all-to-all-start.2 = ((bf16[8,256,384]{2,1,0:T(8,128)(2,1)}), bf16[8,256,384]{2,1,0:T(8,128)(2,1)S(1)}, u32[]{:S(2)}, u32[]{:S(2)}) async-start(bf16[8,256,384]{2,1,0:T(8,128)(2,1)} %bitcast.26), calls=%async_computation.3 | async-start | bytes 3145728 | tf_op jit(solution)/shard_map/all_to_all | solution.py:16
  203.2 78.3 %all-gather.2.cloned.1.call-done = bf16[2048,3072]{1,0:T(8,128)(2,1)} async-done(((bf16[128,3072]{1,0:T(8,128)(2,1)}), bf16[2048,3072]{1,0:T(8,128)(2,1)}) %all-gather.2.cloned.1.call-update) | async-done | bytes 12582928 | tf_op jit(solution)/shard_map/all_gather | solution.py:101
  281.5 11.2 %convolution_convert_fusion.2 = bf16[2048,384]{1,0:T(8,128)(2,1)} fusion(bf16[2048,3072]{1,0:T(8,128)(2,1)} %all-gather.2.cloned.1.call-done, bf16[384,3072]{1,0:T(8,128)(2,1)} %param.8), kind=kOutput, calls=%fused_computation.31 | convolution fusion | flops 4832624640 | bytes 16515072 | tf_op jit(solution)/shard_map/dot_general | solution.py:102
  292.8 1.1 copy-done.8
  293.9 5.1 %all-to-all-start.1 = ((bf16[8,256,384]{2,1,0:T(8,128)(2,1)}), bf16[8,256,384]{2,1,0:T(8,128)(2,1)}, u32[]{:S(2)}, u32[]{:S(2)}) async-start(bf16[8,256,384]{2,1,0:T(8,128)(2,1)} %bitcast.56), calls=%async_computation.2 | async-start | bytes 3145728 | tf_op jit(solution)/shard_map/all_to_all | solution.py:20
  299.0 9.7 %convolution_convert_fusion.1 = bf16[384,3072]{1,0:T(8,128)(2,1)} fusion(bf16[2048,384]{1,0:T(8,128)(2,1)} %bitcast.55, bf16[2048,3072]{1,0:T(8,128)(2,1)} %all-gather.2.cloned.1.call-done), kind=kOutput, calls=%fused_computation.17 | convolution fusion | flops 4833017856 | bytes 16515072 | tf_op jit(solution)/shard_map/dot_general | solution.py:106
  308.7 11.0 %all-to-all-done.1 = bf16[8,256,384]{2,1,0:T(8,128)(2,1)} async-done(((bf16[8,256,384]{2,1,0:T(8,128)(2,1)}), bf16[8,256,384]{2,1,0:T(8,128)(2,1)}, u32[]{:S(2)}, u32[]{:S(2)}) %all-to-all-start.1) | async-done | bytes 1572896 | tf_op jit(solution)/shard_map/all_to_all | solution.py:20
  319.7 2.3 fusion.40
  (71 shorter events, 5.2 us)
Async XLA Ops:
  7.2 37.8 %copy-start = (bf16[3072,384]{1,0:T(8,128)(2,1)S(1)}, bf16[3072,384]{1,0:T(8,128)(2,1)}, u32[]{:S(2)}) copy-start(bf16[3072,384]{1,0:T(8,128)(2,1)} %param.9) | copy-start | bytes 7077892
  8.8 8.1 %copy-start.2 = (bf16[256,384]{1,0:T(8,128)(2,1)S(1)}, bf16[256,384]{1,0:T(8,128)(2,1)}, u32[]{:S(2)}) copy-start(bf16[256,384]{1,0:T(8,128)(2,1)} %param.6) | copy-start | bytes 589828
  9.8 14.2 %collective-permute-start.4 = (bf16[128,1536]{1,0:T(8,128)(2,1)}, bf16[128,1536]{1,0:T(8,128)(2,1)S(1)}, u32[]{:S(2)}, u32[]{:S(2)}) collective-permute-start(bf16[128,1536]{1,0:T(8,128)(2,1)} %get-tuple-element.15), channel_id=1, source_target_pairs={{0,96},{8,104},{16,112},{24,120},{32,0},{40,8},{48,16},{56,24},{64... | collective-permute-start | bytes 1179656 | tf_op jit(solution)/shard_map/ppermute | solution.py:52
  14.4 12.7 %collective-permute-start.5 = (bf16[128,1536]{1,0:T(8,128)(2,1)}, bf16[128,1536]{1,0:T(8,128)(2,1)}, u32[]{:S(2)}, u32[]{:S(2)}) collective-permute-start(bf16[128,1536]{1,0:T(8,128)(2,1)} %get-tuple-element.15), channel_id=1, source_target_pairs={{0,32},{8,40},{16,48},{24,56},{32,64},{40,72},{48,80},{56,88},{64,... | collective-permute-start | bytes 1179656 | tf_op jit(solution)/shard_map/ppermute | solution.py:51
  14.4 13.7 %collective-permute-start = (bf16[128,1536]{1,0:T(8,128)(2,1)}, bf16[128,1536]{1,0:T(8,128)(2,1)}, u32[]{:S(2)}, u32[]{:S(2)}) collective-permute-start(bf16[128,1536]{1,0:T(8,128)(2,1)} %get-tuple-element.16), channel_id=1, source_target_pairs={{0,24},{8,0},{16,8},{24,16},{32,56},{40,32},{48,40},{56,48},{64,88... | collective-permute-start | bytes 1179656 | tf_op jit(solution)/shard_map/ppermute | solution.py:52
  16.9 15.2 %collective-permute-start.1 = (bf16[128,1536]{1,0:T(8,128)(2,1)}, bf16[128,1536]{1,0:T(8,128)(2,1)}, u32[]{:S(2)}, u32[]{:S(2)}) collective-permute-start(bf16[128,1536]{1,0:T(8,128)(2,1)} %get-tuple-element.16), channel_id=1, source_target_pairs={{0,8},{8,16},{16,24},{24,0},{32,40},{40,48},{48,56},{56,32},{64,72... | collective-permute-start | bytes 1179656 | tf_op jit(solution)/shard_map/ppermute | solution.py:51
  17.2 1.1 copy-start.5
  18.3 26.7 %all-to-all-start = ((bf16[8,256,384]{2,1,0:T(8,128)(2,1)}), bf16[8,256,384]{2,1,0:T(8,128)(2,1)}, u32[]{:S(2)}, u32[]{:S(2)}) async-start(bf16[8,256,384]{2,1,0:T(8,128)(2,1)} %bitcast.52), calls=%async_computation | async-start | bytes 3145728 | tf_op jit(solution)/shard_map/all_to_all | solution.py:16
  24.0 165.4 %reduce-scatter.2.cloned.1.call-start = ((), (), s32[]{:S(2)}) async-start(), calls=%async_computation.4 | async-start | bytes 13369344 | tf_op jit(solution)/shard_map/reduce_scatter | solution.py:85
  24.1 9.1 %collective-permute-start.7 = (bf16[64,1536]{1,0:T(8,128)(2,1)S(1)}, bf16[64,1536]{1,0:T(8,128)(2,1)S(1)}, u32[]{:S(2)}, u32[]{:S(2)}) collective-permute-start(bf16[64,1536]{1,0:T(8,128)(2,1)S(1)} %slice.93), channel_id=1, source_target_pairs={{0,96},{8,104},{16,112},{24,120},{32,0},{40,8},{48,16},{56,24},{64... | collective-permute-start | bytes 589832 | tf_op jit(solution)/shard_map/ppermute | solution.py:55
  28.0 7.2 %collective-permute-start.6 = (bf16[64,1536]{1,0:T(8,128)(2,1)S(1)}, bf16[64,1536]{1,0:T(8,128)(2,1)S(1)}, u32[]{:S(2)}, u32[]{:S(2)}) collective-permute-start(bf16[64,1536]{1,0:T(8,128)(2,1)S(1)} %slice.92), channel_id=1, source_target_pairs={{0,32},{8,40},{16,48},{24,56},{32,64},{40,72},{48,80},{56,88},{64,... | collective-permute-start | bytes 589832 | tf_op jit(solution)/shard_map/ppermute | solution.py:55
  29.1 6.9 %collective-permute-start.3 = (bf16[64,1536]{1,0:T(8,128)(2,1)S(1)}, bf16[64,1536]{1,0:T(8,128)(2,1)S(1)}, u32[]{:S(2)}, u32[]{:S(2)}) collective-permute-start(bf16[64,1536]{1,0:T(8,128)(2,1)S(1)} %slice.90), channel_id=1, source_target_pairs={{0,24},{8,0},{16,8},{24,16},{32,56},{40,32},{48,40},{56,48},{64,88... | collective-permute-start | bytes 589832 | tf_op jit(solution)/shard_map/ppermute | solution.py:55
  33.0 7.1 %collective-permute-start.2 = (bf16[64,1536]{1,0:T(8,128)(2,1)S(1)}, bf16[64,1536]{1,0:T(8,128)(2,1)S(1)}, u32[]{:S(2)}, u32[]{:S(2)}) collective-permute-start(bf16[64,1536]{1,0:T(8,128)(2,1)S(1)} %slice.89), channel_id=1, source_target_pairs={{0,8},{8,16},{16,24},{24,0},{32,40},{40,48},{48,56},{56,32},{64,72... | collective-permute-start | bytes 589832 | tf_op jit(solution)/shard_map/ppermute | solution.py:55
  56.2 2.9 copy-start.6
  56.2 225.3 %all-gather.2.cloned.1.call-start = ((), (), s32[]{:S(2)}) async-start(), calls=%async_computation.5 | async-start | bytes 13369344 | tf_op jit(solution)/shard_map/all_gather | solution.py:101
  56.2 59.3 %collective-permute-start.9 = (bf16[4,128,1536]{2,1,0:T(8,128)(2,1)}, bf16[4,128,1536]{2,1,0:T(8,128)(2,1)S(1)}, u32[]{:S(2)}, u32[]{:S(2)}) collective-permute-start(bf16[4,128,1536]{2,1,0:T(8,128)(2,1)} %pad_maximum_fusion.1), channel_id=1, source_target_pairs={{0,32},{8,40},{16,48},{24,56},{32,64},{40,72},{48,80},{56,88},{64,... | collective-permute-start | bytes 4718600 | tf_op jit(solution)/shard_map/ppermute | solution.py:51
  56.3 61.0 %collective-permute-start.8 = (bf16[4,128,1536]{2,1,0:T(8,128)(2,1)}, bf16[4,128,1536]{2,1,0:T(8,128)(2,1)S(1)}, u32[]{:S(2)}, u32[]{:S(2)}) collective-permute-start(bf16[4,128,1536]{2,1,0:T(8,128)(2,1)} %pad_maximum_fusion.1), channel_id=1, source_target_pairs={{0,96},{8,104},{16,112},{24,120},{32,0},{40,8},{48,16},{56,24},{64... | collective-permute-start | bytes 4718600 | tf_op jit(solution)/shard_map/ppermute | solution.py:52
  59.1 62.0 %collective-permute-start.13 = (bf16[4,128,1536]{2,1,0:T(8,128)(2,1)S(1)}, bf16[4,128,1536]{2,1,0:T(8,128)(2,1)S(1)}, u32[]{:S(2)}, u32[]{:S(2)}) collective-permute-start(bf16[4,128,1536]{2,1,0:T(8,128)(2,1)S(1)} %copy-done.6), channel_id=1, source_target_pairs={{0,8},{8,16},{16,24},{24,0},{32,40},{40,48},{48,56},{56,32},{64,72... | collective-permute-start | bytes 4718600 | tf_op jit(solution)/shard_map/ppermute | solution.py:51
  59.5 63.4 %collective-permute-start.12 = (bf16[4,128,1536]{2,1,0:T(8,128)(2,1)S(1)}, bf16[4,128,1536]{2,1,0:T(8,128)(2,1)S(1)}, u32[]{:S(2)}, u32[]{:S(2)}) collective-permute-start(bf16[4,128,1536]{2,1,0:T(8,128)(2,1)S(1)} %copy-done.6), channel_id=1, source_target_pairs={{0,24},{8,0},{16,8},{24,16},{32,56},{40,32},{48,40},{56,48},{64,88... | collective-permute-start | bytes 4718600 | tf_op jit(solution)/shard_map/ppermute | solution.py:52
  115.6 1.8 copy-start.9
  115.6 36.0 %collective-permute-start.10 = (bf16[2,128,1536]{2,1,0:T(8,128)(2,1)S(1)}, bf16[2,128,1536]{2,1,0:T(8,128)(2,1)}, u32[]{:S(2)}, u32[]{:S(2)}) collective-permute-start(bf16[2,128,1536]{2,1,0:T(8,128)(2,1)S(1)} %slice.94), channel_id=1, source_target_pairs={{0,32},{8,40},{16,48},{24,56},{32,64},{40,72},{48,80},{56,88},{64,... | collective-permute-start | bytes 2359304 | tf_op jit(solution)/shard_map/ppermute | solution.py:55
  117.3 4.7 %copy-start.11 = (bf16[4,128,1536]{2,1,0:T(8,128)(2,1)}, bf16[4,128,1536]{2,1,0:T(8,128)(2,1)S(1)}, u32[]{:S(2)}) copy-start(bf16[4,128,1536]{2,1,0:T(8,128)(2,1)S(1)} %collective-permute-done.8) | copy-start | bytes 4718596
  117.4 36.1 %collective-permute-start.11 = (bf16[2,128,1536]{2,1,0:T(8,128)(2,1)S(1)}, bf16[2,128,1536]{2,1,0:T(8,128)(2,1)}, u32[]{:S(2)}, u32[]{:S(2)}) collective-permute-start(bf16[2,128,1536]{2,1,0:T(8,128)(2,1)S(1)} %slice.95), channel_id=1, source_target_pairs={{0,96},{8,104},{16,112},{24,120},{32,0},{40,8},{48,16},{56,24},{64... | collective-permute-start | bytes 2359304 | tf_op jit(solution)/shard_map/ppermute | solution.py:55
  121.0 2.9 copy-start.13
  122.0 37.9 %collective-permute-start.14 = (bf16[2,128,1536]{2,1,0:T(8,128)(2,1)}, bf16[2,128,1536]{2,1,0:T(8,128)(2,1)}, u32[]{:S(2)}, u32[]{:S(2)}) collective-permute-start(bf16[2,128,1536]{2,1,0:T(8,128)(2,1)} %slice.96), channel_id=1, source_target_pairs={{0,8},{8,16},{16,24},{24,0},{32,40},{40,48},{48,56},{56,32},{64,72... | collective-permute-start | bytes 2359304 | tf_op jit(solution)/shard_map/ppermute | solution.py:55
  122.9 4.7 %copy-start.15 = (bf16[4,128,1536]{2,1,0:T(8,128)(2,1)}, bf16[4,128,1536]{2,1,0:T(8,128)(2,1)S(1)}, u32[]{:S(2)}) copy-start(bf16[4,128,1536]{2,1,0:T(8,128)(2,1)S(1)} %collective-permute-done.12) | copy-start | bytes 4718596
  123.9 36.2 %collective-permute-start.15 = (bf16[2,128,1536]{2,1,0:T(8,128)(2,1)}, bf16[2,128,1536]{2,1,0:T(8,128)(2,1)}, u32[]{:S(2)}, u32[]{:S(2)}) collective-permute-start(bf16[2,128,1536]{2,1,0:T(8,128)(2,1)} %slice.97), channel_id=1, source_target_pairs={{0,24},{8,0},{16,8},{24,16},{32,56},{40,32},{48,40},{56,48},{64,88... | collective-permute-start | bytes 2359304 | tf_op jit(solution)/shard_map/ppermute | solution.py:55
  155.0 6.7 %copy-start.14 = (bf16[4,128,1536]{2,1,0:T(8,128)(2,1)S(1)}, bf16[4,128,1536]{2,1,0:T(8,128)(2,1)}, u32[]{:S(2)}) copy-start(bf16[4,128,1536]{2,1,0:T(8,128)(2,1)} %copy-done.13) | copy-start | bytes 4718596
  155.0 6.7 %copy-start.16 = (bf16[4,128,1536]{2,1,0:T(8,128)(2,1)S(1)}, bf16[4,128,1536]{2,1,0:T(8,128)(2,1)}, u32[]{:S(2)}) copy-start(bf16[4,128,1536]{2,1,0:T(8,128)(2,1)} %copy-done.15) | copy-start | bytes 4718596
  161.7 3.6 %copy-start.7 = (bf16[4,128,1536]{2,1,0:T(8,128)(2,1)S(1)}, bf16[4,128,1536]{2,1,0:T(8,128)(2,1)}, u32[]{:S(2)}) copy-start(bf16[4,128,1536]{2,1,0:T(8,128)(2,1)} %pad_maximum_fusion.1) | copy-start | bytes 4718596
  161.7 3.6 %copy-start.10 = (bf16[4,128,1536]{2,1,0:T(8,128)(2,1)S(1)}, bf16[4,128,1536]{2,1,0:T(8,128)(2,1)}, u32[]{:S(2)}) copy-start(bf16[4,128,1536]{2,1,0:T(8,128)(2,1)} %copy-done.9) | copy-start | bytes 4718596
  161.7 3.6 %copy-start.12 = (bf16[4,128,1536]{2,1,0:T(8,128)(2,1)S(1)}, bf16[4,128,1536]{2,1,0:T(8,128)(2,1)}, u32[]{:S(2)}) copy-start(bf16[4,128,1536]{2,1,0:T(8,128)(2,1)} %copy-done.11) | copy-start | bytes 4718596
  168.8 20.6 %copy-start.4 = (bf16[128,3072]{1,0:T(8,128)(2,1)S(1)}, bf16[128,3072]{1,0:T(8,128)(2,1)}, u32[]{:S(2)}) copy-start(bf16[128,3072]{1,0:T(8,128)(2,1)} %param.7) | copy-start | bytes 2359300
  170.4 21.8 %copy-start.3 = (bf16[256,384]{1,0:T(8,128)(2,1)S(1)}, bf16[256,384]{1,0:T(8,128)(2,1)}, u32[]{:S(2)}) copy-start(bf16[256,384]{1,0:T(8,128)(2,1)} %param.5) | copy-start | bytes 589828
  197.8 95.0 %all-to-all-start.2 = ((bf16[8,256,384]{2,1,0:T(8,128)(2,1)}), bf16[8,256,384]{2,1,0:T(8,128)(2,1)S(1)}, u32[]{:S(2)}, u32[]{:S(2)}) async-start(bf16[8,256,384]{2,1,0:T(8,128)(2,1)} %bitcast.26), calls=%async_computation.3 | async-start | bytes 3145728 | tf_op jit(solution)/shard_map/all_to_all | solution.py:16
  292.8 1.1 copy-start.8
  293.9 25.8 %all-to-all-start.1 = ((bf16[8,256,384]{2,1,0:T(8,128)(2,1)}), bf16[8,256,384]{2,1,0:T(8,128)(2,1)}, u32[]{:S(2)}, u32[]{:S(2)}) async-start(bf16[8,256,384]{2,1,0:T(8,128)(2,1)} %bitcast.56), calls=%async_computation.2 | async-start | bytes 3145728 | tf_op jit(solution)/shard_map/all_to_all | solution.py:20
  299.0 23.0 %copy-start.1 = (bf16[3072,384]{1,0:T(8,128)(2,1)S(1)}, bf16[3072,384]{1,0:T(8,128)(2,1)}, u32[]{:S(2)}) copy-start(bf16[3072,384]{1,0:T(8,128)(2,1)} %param.9) | copy-start | bytes 7077892
Sparse Core Ops, SparseCore 0:
  56.3 133.0 reduce-scatter.1
  192.3 89.1 all-gather.1

commit v7 on v6

--- a/solution.py
+++ b/solution.py
@@ -76,7 +76,7 @@
     value, slope = gelu_parts(pre_act)
     hidden_loc = value.astype(jnp.bfloat16)
     n_z, n_x = 4, 4
-    grad_all = gather_by_all_to_all(out_grad, "col", n_col)
+    grad_all = lax.all_gather(out_grad, "col", axis=0, tiled=True)
     hid_a, hid_b, grad_all = torus_gather(hidden_loc, n_z, n_x, grad_all)
     inputs_all = gather_by_all_to_all(inputs, "col", n_col)
     partial = lax.dot_general(

time: 330 us -> 320 us (0.970)
  starting transfers between devices: 43.5 us -> 38 us
    ppermute x4, starting transfers between devices: 1.14 us -> 7.03 us  [ring_gather(): lax.ppermute(from_prev[:h], 'row', fwd)]
    ppermute x4, starting transfers between devices: 13.3 us -> 7.64 us  [ring_gather(): lax.ppermute(from_next[h:], 'row', bwd)]
    all_to_all x2 -> x1, starting transfers between devices: 11.1 us -> 5.58 us  [gather_by_all_to_all(): return lax.all_to_all(rep, axis, 0, 0, tiled=True)]
    ppermute x4, waiting for transfers between devices: 1.63 us -> 5.32 us  [ring_gather(): from_next = lax.ppermute(x, 'row', bwd)]
    unnamed x48 -> x37, local copies, waits for them, and re-layouts: 7.45 us -> 6.28 us
  transfers between devices with their start and end apart: 21 -> 21, of which waited for: 13 -> 12; matrix products, arithmetic and copies ran while one was open for 15% -> 15% of each run, Pallas kernels for 0% -> 0%
where the time goes in v7:
time: 320 us
  waiting for transfers between devices  202 us (63%)
  matrix products  38.4 us (12%)
  starting transfers between devices  38 us (12%)
  other arithmetic  16.1 us (5%)
  between operations  14 us (4%)
  local copies, waits for them, and re-layouts  11.2 us (4%)
    all_gather x1, waiting for transfers between devices, on_device(): pre_grad = lax.all_gather(pre_grad_loc, 'row', axis=0, tiled=True)  78.1 us
    ppermute x4, waiting for transfers between devices, ring_gather(): from_prev = lax.ppermute(x, 'row', fwd)  54.1 us
    ppermute x4, waiting for transfers between devices, ring_gather(): lax.ppermute(from_prev[:h], 'row', fwd)  32 us
    reduce_scatter x1, waiting for transfers between devices, on_device(): total = lax.psum_scatter(partial, 'row', scatter_dimension=0, tiled=True)  17.5 us
    dot_general x1, matrix products, on_device(): lax.dot_general(grad_all, w_out, (((1,), (1,)), ((), ())), preferred_elem...  11.1 us
    all_to_all x1, waiting for transfers between devices, scatter_sum_by_all_to_all(): got = lax.all_to_all(x, axis, 0, 0, tiled=True)  11 us
    dot_general x1, matrix products, on_device(): lax.dot_general(pre_grad, w_in, (((1,), (1,)), ((), ())), preferred_eleme...  10.5 us
    ppermute x4, starting transfers between devices, ring_gather(): from_next = lax.ppermute(x, 'row', bwd)  10.1 us
  transfers between devices with their start and end apart: 21, of which 12 were waited for; matrix products, arithmetic and copies ran while one was open for 15% of the time, Pallas kernels for 0%

profile of v7, /device:TPU:1, one launch (start us, length us, event | category | flops | bytes accessed | tf_op | source)
XLA Modules:
  0.0 320.0 jit_solution(81943614433539310)
XLA Ops:
  8.0 1.5 fusion.31
  9.6 4.6 %collective-permute-start.4 = (bf16[128,1536]{1,0:T(8,128)(2,1)S(1)}, bf16[128,1536]{1,0:T(8,128)(2,1)S(1)}, u32[]{:S(2)}, u32[]{:S(2)}) collective-permute-start(bf16[128,1536]{1,0:T(8,128)(2,1)S(1)} %get-tuple-element.15), channel_id=1, source_target_pairs={{0,96},{8,104},{16,112},{24,120},{32,0},{40,8},{48,16},{56,24},{64... | collective-permute-start | bytes 1179656 | tf_op jit(solution)/shard_map/ppermute | solution.py:52
  14.2 2.5 collective-permute-start
  16.7 5.3 %collective-permute-done.4 = bf16[128,1536]{1,0:T(8,128)(2,1)S(1)} collective-permute-done((bf16[128,1536]{1,0:T(8,128)(2,1)S(1)}, bf16[128,1536]{1,0:T(8,128)(2,1)S(1)}, u32[]{:S(2)}, u32[]{:S(2)}) %collective-permute-start.4) | collective-permute-done | bytes 393248 | tf_op jit(solution)/shard_map/ppermute | solution.py:52
  22.0 3.5 %collective-permute-start.7 = (bf16[64,1536]{1,0:T(8,128)(2,1)S(1)}, bf16[64,1536]{1,0:T(8,128)(2,1)S(1)}, u32[]{:S(2)}, u32[]{:S(2)}) collective-permute-start(bf16[64,1536]{1,0:T(8,128)(2,1)S(1)} %slice.93), channel_id=1, source_target_pairs={{0,96},{8,104},{16,112},{24,120},{32,0},{40,8},{48,16},{56,24},{64... | collective-permute-start | bytes 589832 | tf_op jit(solution)/shard_map/ppermute | solution.py:55
  25.6 2.5 collective-permute-start.3
  28.3 3.4 %collective-permute-done.6 = bf16[64,1536]{1,0:T(8,128)(2,1)S(1)} collective-permute-done((bf16[64,1536]{1,0:T(8,128)(2,1)S(1)}, bf16[64,1536]{1,0:T(8,128)(2,1)S(1)}, u32[]{:S(2)}, u32[]{:S(2)}) %collective-permute-start.6) | collective-permute-done | bytes 196640 | tf_op jit(solution)/shard_map/ppermute | solution.py:55
  31.8 2.2 collective-permute-done.2
  34.0 1.3 pad_maximum_fusion.2
  35.4 1.3 pad_maximum_fusion.1
  36.7 1.0 all-gather.3.cloned.1.call-done
  37.7 11.1 %convolution_convert_fusion = bf16[2048,3072]{1,0:T(8,128)(2,1)} fusion(bf16[2048,384]{1,0:T(8,128)(2,1)} %all-gather.3.cloned.1.call-done, bf16[3072,384]{1,0:T(8,128)(2,1)S(1)} %copy-done), kind=kOutput, calls=%fused_computation | convolution fusion | flops 4838129664 | bytes 16515072 | tf_op jit(solution)/shard_map/dot_general | solution.py:82
  48.9 1.3 copy-done.5
  50.2 1.2 collective-permute-start.9
  51.4 1.5 collective-permute-start.8
  52.9 1.2 collective-permute-start.13
  54.1 1.5 collective-permute-start.12
  55.6 54.1 %collective-permute-done.9 = bf16[4,128,1536]{2,1,0:T(8,128)(2,1)S(1)} collective-permute-done((bf16[4,128,1536]{2,1,0:T(8,128)(2,1)S(1)}, bf16[4,128,1536]{2,1,0:T(8,128)(2,1)S(1)}, u32[]{:S(2)}, u32[]{:S(2)}) %collective-permute-start.9) | collective-permute-done | bytes 1572896 | tf_op jit(solution)/shard_map/ppermute | solution.py:51
  109.6 1.0 slice.94
  110.6 2.3 collective-permute-start.10
  112.9 1.0 slice.95
  114.3 1.0 slice.96
  115.4 4.6 %collective-permute-start.14 = (bf16[2,128,1536]{2,1,0:T(8,128)(2,1)}, bf16[2,128,1536]{2,1,0:T(8,128)(2,1)}, u32[]{:S(2)}, u32[]{:S(2)}) collective-permute-start(bf16[2,128,1536]{2,1,0:T(8,128)(2,1)} %slice.96), channel_id=1, source_target_pairs={{0,8},{8,16},{16,24},{24,0},{32,40},{40,48},{48,56},{56,32},{64,72... | collective-permute-start | bytes 2359304 | tf_op jit(solution)/shard_map/ppermute | solution.py:55
  119.9 1.0 slice.97
  120.9 1.2 collective-permute-start.15
  122.2 2.1 fusion.38
  124.2 22.2 %collective-permute-done.10 = bf16[2,128,1536]{2,1,0:T(8,128)(2,1)} collective-permute-done((bf16[2,128,1536]{2,1,0:T(8,128)(2,1)}, bf16[2,128,1536]{2,1,0:T(8,128)(2,1)}, u32[]{:S(2)}, u32[]{:S(2)}) %collective-permute-start.10) | collective-permute-done | bytes 786464 | tf_op jit(solution)/shard_map/ppermute | solution.py:55
  146.4 1.5 collective-permute-done.11
  147.9 1.5 maximum_bitcast_fusion
  149.5 4.2 %collective-permute-done.14 = bf16[2,128,1536]{2,1,0:T(8,128)(2,1)} collective-permute-done((bf16[2,128,1536]{2,1,0:T(8,128)(2,1)}, bf16[2,128,1536]{2,1,0:T(8,128)(2,1)}, u32[]{:S(2)}, u32[]{:S(2)}) %collective-permute-start.14) | collective-permute-done | bytes 786464 | tf_op jit(solution)/shard_map/ppermute | solution.py:55
  153.7 1.1 collective-permute-done.15
  154.8 1.6 maximum_bitcast_fusion.1
  156.4 3.5 %fusion.25 = bf16[1536,384]{1,0:T(8,128)(2,1)S(1)} fusion(bf16[1,4,128,1536]{3,2,1,0:T(8,128)(2,1)S(1)} %bitcast.59, bf16[1,4,128,1536]{3,2,1,0:T(8,128)(2,1)S(1)} %maximum_bitcast_fusion.1, bf16[1,4,128,1536]{3,2,1,0:T(8,128)(2,1)S(1)} %bitcast.60, bf16[1,4,128,1536]{3,2,1,0:T(8,128)(2,1)S(1)} %bitcast.50, s32[]{:T(128)S(6)} %select_n.38, ...), kind=kOutput, calls=%fused_computation.30 | convolution fusion | flops 2426732544 | bytes 9043972 | tf_op jit(solution)/shard_map/dot_general | solution.py:94
  159.9 3.5 %fusion.22 = bf16[1536,384]{1,0:T(8,128)(2,1)S(1)} fusion(bf16[1,4,128,1536]{3,2,1,0:T(8,128)(2,1)S(1)} %bitcast.57, bf16[1,4,128,1536]{3,2,1,0:T(8,128)(2,1)S(1)} %maximum_bitcast_fusion, bf16[1,4,128,1536]{3,2,1,0:T(8,128)(2,1)S(1)} %bitcast.58, bf16[1,4,128,1536]{3,2,1,0:T(8,128)(2,1)S(1)} %bitcast.51, s32[]{:T(128)S(6)} %select_n.38, ...), kind=kOutput, calls=%fused_computation.29 | convolution fusion | flops 2426732544 | bytes 9043972 | tf_op jit(solution)/shard_map/dot_general | solution.py:90
  163.5 1.6 pad_maximum_fusion
  165.1 17.5 %reduce-scatter.2.cloned.1.call-done = bf16[128,3072]{1,0:T(8,128)(2,1)} async-done(((bf16[2048,3072]{1,0:T(8,128)(2,1)}), bf16[128,3072]{1,0:T(8,128)(2,1)}) %reduce-scatter.2.cloned.1.call-update) | async-done | bytes 786448 | tf_op jit(solution)/shard_map/reduce_scatter | solution.py:85
  182.7 2.8 fusion.36
  185.5 0.7 constant_dynamic-update-slice_fusion.7
  186.1 0.7 constant_dynamic-update-slice_fusion.6
  188.2 0.7 constant_dynamic-update-slice_fusion.3
  188.9 0.7 constant_dynamic-update-slice_fusion.2
  191.0 5.6 %all-to-all-start.1 = ((bf16[8,256,384]{2,1,0:T(8,128)(2,1)}), bf16[8,256,384]{2,1,0:T(8,128)(2,1)}, u32[]{:S(2)}, u32[]{:S(2)}) async-start(bf16[8,256,384]{2,1,0:T(8,128)(2,1)} %bitcast.24), calls=%async_computation.2 | async-start | bytes 3145728 | tf_op jit(solution)/shard_map/all_to_all | solution.py:16
  196.6 78.1 %all-gather.5.cloned.1.call-done = bf16[2048,3072]{1,0:T(8,128)(2,1)} async-done(((bf16[128,3072]{1,0:T(8,128)(2,1)}), bf16[2048,3072]{1,0:T(8,128)(2,1)}) %all-gather.5.cloned.1.call-update) | async-done | bytes 12582928 | tf_op jit(solution)/shard_map/all_gather | solution.py:101
  274.7 10.5 %convolution_convert_fusion.2 = bf16[2048,384]{1,0:T(8,128)(2,1)} fusion(bf16[2048,3072]{1,0:T(8,128)(2,1)} %all-gather.5.cloned.1.call-done, bf16[384,3072]{1,0:T(8,128)(2,1)S(1)} %copy-done.14), kind=kOutput, calls=%fused_computation.31 | convolution fusion | flops 4832624640 | bytes 16515072 | tf_op jit(solution)/shard_map/dot_general | solution.py:102
  285.3 5.1 %all-to-all-start = ((bf16[8,256,384]{2,1,0:T(8,128)(2,1)}), bf16[8,256,384]{2,1,0:T(8,128)(2,1)}, u32[]{:S(2)}, u32[]{:S(2)}) async-start(bf16[8,256,384]{2,1,0:T(8,128)(2,1)} %bitcast.22), calls=%async_computation.1 | async-start | bytes 3145728 | tf_op jit(solution)/shard_map/all_to_all | solution.py:20
  290.4 9.7 %convolution_convert_fusion.1 = bf16[384,3072]{1,0:T(8,128)(2,1)} fusion(bf16[2048,384]{1,0:T(8,128)(2,1)} %bitcast.25, bf16[2048,3072]{1,0:T(8,128)(2,1)} %all-gather.5.cloned.1.call-done), kind=kOutput, calls=%fused_computation.17 | convolution fusion | flops 4833017856 | bytes 16515072 | tf_op jit(solution)/shard_map/dot_general | solution.py:106
  300.1 11.0 %all-to-all-done = bf16[8,256,384]{2,1,0:T(8,128)(2,1)} async-done(((bf16[8,256,384]{2,1,0:T(8,128)(2,1)}), bf16[8,256,384]{2,1,0:T(8,128)(2,1)}, u32[]{:S(2)}, u32[]{:S(2)}) %all-to-all-start) | async-done | bytes 1572896 | tf_op jit(solution)/shard_map/all_to_all | solution.py:20
  311.1 2.3 fusion.40
  (60 shorter events, 4.5 us)
Async XLA Ops:
  7.2 30.5 %copy-start = (bf16[3072,384]{1,0:T(8,128)(2,1)S(1)}, bf16[3072,384]{1,0:T(8,128)(2,1)}, u32[]{:S(2)}) copy-start(bf16[3072,384]{1,0:T(8,128)(2,1)} %param.9) | copy-start | bytes 7077892
  7.2 30.5 %all-gather.3.cloned.1.call-start = ((), (), s32[]{:S(2)}) async-start(), calls=%async_computation.3 | async-start | bytes 1769472 | tf_op jit(solution)/shard_map/all_gather | solution.py:79
  7.9 174.7 %reduce-scatter.2.cloned.1.call-start = ((), (), s32[]{:S(2)}) async-start(), calls=%async_computation.4 | async-start | bytes 13369344 | tf_op jit(solution)/shard_map/reduce_scatter | solution.py:85
  9.6 12.4 %collective-permute-start.4 = (bf16[128,1536]{1,0:T(8,128)(2,1)S(1)}, bf16[128,1536]{1,0:T(8,128)(2,1)S(1)}, u32[]{:S(2)}, u32[]{:S(2)}) collective-permute-start(bf16[128,1536]{1,0:T(8,128)(2,1)S(1)} %get-tuple-element.15), channel_id=1, source_target_pairs={{0,96},{8,104},{16,112},{24,120},{32,0},{40,8},{48,16},{56,24},{64... | collective-permute-start | bytes 1179656 | tf_op jit(solution)/shard_map/ppermute | solution.py:52
  14.2 11.3 %collective-permute-start.5 = (bf16[128,1536]{1,0:T(8,128)(2,1)S(1)}, bf16[128,1536]{1,0:T(8,128)(2,1)S(1)}, u32[]{:S(2)}, u32[]{:S(2)}) collective-permute-start(bf16[128,1536]{1,0:T(8,128)(2,1)S(1)} %get-tuple-element.15), channel_id=1, source_target_pairs={{0,32},{8,40},{16,48},{24,56},{32,64},{40,72},{48,80},{56,88},{64,... | collective-permute-start | bytes 1179656 | tf_op jit(solution)/shard_map/ppermute | solution.py:51
  14.2 11.4 %collective-permute-start = (bf16[128,1536]{1,0:T(8,128)(2,1)S(1)}, bf16[128,1536]{1,0:T(8,128)(2,1)S(1)}, u32[]{:S(2)}, u32[]{:S(2)}) collective-permute-start(bf16[128,1536]{1,0:T(8,128)(2,1)S(1)} %get-tuple-element.16), channel_id=1, source_target_pairs={{0,24},{8,0},{16,8},{24,16},{32,56},{40,32},{48,40},{56,48},{64,88... | collective-permute-start | bytes 1179656 | tf_op jit(solution)/shard_map/ppermute | solution.py:52
  16.7 11.5 %collective-permute-start.1 = (bf16[128,1536]{1,0:T(8,128)(2,1)S(1)}, bf16[128,1536]{1,0:T(8,128)(2,1)S(1)}, u32[]{:S(2)}, u32[]{:S(2)}) collective-permute-start(bf16[128,1536]{1,0:T(8,128)(2,1)S(1)} %get-tuple-element.16), channel_id=1, source_target_pairs={{0,8},{8,16},{16,24},{24,0},{32,40},{40,48},{48,56},{56,32},{64,72... | collective-permute-start | bytes 1179656 | tf_op jit(solution)/shard_map/ppermute | solution.py:51
  22.0 6.3 %collective-permute-start.7 = (bf16[64,1536]{1,0:T(8,128)(2,1)S(1)}, bf16[64,1536]{1,0:T(8,128)(2,1)S(1)}, u32[]{:S(2)}, u32[]{:S(2)}) collective-permute-start(bf16[64,1536]{1,0:T(8,128)(2,1)S(1)} %slice.93), channel_id=1, source_target_pairs={{0,96},{8,104},{16,112},{24,120},{32,0},{40,8},{48,16},{56,24},{64... | collective-permute-start | bytes 589832 | tf_op jit(solution)/shard_map/ppermute | solution.py:55
  25.5 6.2 %collective-permute-start.6 = (bf16[64,1536]{1,0:T(8,128)(2,1)S(1)}, bf16[64,1536]{1,0:T(8,128)(2,1)S(1)}, u32[]{:S(2)}, u32[]{:S(2)}) collective-permute-start(bf16[64,1536]{1,0:T(8,128)(2,1)S(1)} %slice.92), channel_id=1, source_target_pairs={{0,32},{8,40},{16,48},{24,56},{32,64},{40,72},{48,80},{56,88},{64,... | collective-permute-start | bytes 589832 | tf_op jit(solution)/shard_map/ppermute | solution.py:55
  25.6 6.1 %collective-permute-start.3 = (bf16[64,1536]{1,0:T(8,128)(2,1)S(1)}, bf16[64,1536]{1,0:T(8,128)(2,1)S(1)}, u32[]{:S(2)}, u32[]{:S(2)}) collective-permute-start(bf16[64,1536]{1,0:T(8,128)(2,1)S(1)} %slice.90), channel_id=1, source_target_pairs={{0,24},{8,0},{16,8},{24,16},{32,56},{40,32},{48,40},{56,48},{64,88... | collective-permute-start | bytes 589832 | tf_op jit(solution)/shard_map/ppermute | solution.py:55
  28.2 5.8 %collective-permute-start.2 = (bf16[64,1536]{1,0:T(8,128)(2,1)S(1)}, bf16[64,1536]{1,0:T(8,128)(2,1)S(1)}, u32[]{:S(2)}, u32[]{:S(2)}) collective-permute-start(bf16[64,1536]{1,0:T(8,128)(2,1)S(1)} %slice.89), channel_id=1, source_target_pairs={{0,8},{8,16},{16,24},{24,0},{32,40},{40,48},{48,56},{56,32},{64,72... | collective-permute-start | bytes 589832 | tf_op jit(solution)/shard_map/ppermute | solution.py:55
  48.8 1.4 copy-start.5
  48.8 4.1 %copy-start.4 = (bf16[4,128,1536]{2,1,0:T(8,128)(2,1)S(1)}, bf16[4,128,1536]{2,1,0:T(8,128)(2,1)}, u32[]{:S(2)}) copy-start(bf16[4,128,1536]{2,1,0:T(8,128)(2,1)} %pad_maximum_fusion.2) | copy-start | bytes 4718596
  48.8 225.9 %all-gather.5.cloned.1.call-start = ((), (), s32[]{:S(2)}) async-start(), calls=%async_computation.5 | async-start | bytes 13369344 | tf_op jit(solution)/shard_map/all_gather | solution.py:101
  50.2 59.4 %collective-permute-start.9 = (bf16[4,128,1536]{2,1,0:T(8,128)(2,1)S(1)}, bf16[4,128,1536]{2,1,0:T(8,128)(2,1)S(1)}, u32[]{:S(2)}, u32[]{:S(2)}) collective-permute-start(bf16[4,128,1536]{2,1,0:T(8,128)(2,1)S(1)} %copy-done.5), channel_id=1, source_target_pairs={{0,32},{8,40},{16,48},{24,56},{32,64},{40,72},{48,80},{56,88},{64,... | collective-permute-start | bytes 4718600 | tf_op jit(solution)/shard_map/ppermute | solution.py:51
  51.4 61.6 %collective-permute-start.8 = (bf16[4,128,1536]{2,1,0:T(8,128)(2,1)S(1)}, bf16[4,128,1536]{2,1,0:T(8,128)(2,1)S(1)}, u32[]{:S(2)}, u32[]{:S(2)}) collective-permute-start(bf16[4,128,1536]{2,1,0:T(8,128)(2,1)S(1)} %copy-done.5), channel_id=1, source_target_pairs={{0,96},{8,104},{16,112},{24,120},{32,0},{40,8},{48,16},{56,24},{64... | collective-permute-start | bytes 4718600 | tf_op jit(solution)/shard_map/ppermute | solution.py:52
  52.9 61.4 %collective-permute-start.13 = (bf16[4,128,1536]{2,1,0:T(8,128)(2,1)S(1)}, bf16[4,128,1536]{2,1,0:T(8,128)(2,1)S(1)}, u32[]{:S(2)}, u32[]{:S(2)}) collective-permute-start(bf16[4,128,1536]{2,1,0:T(8,128)(2,1)S(1)} %copy-done.4), channel_id=1, source_target_pairs={{0,8},{8,16},{16,24},{24,0},{32,40},{40,48},{48,56},{56,32},{64,72... | collective-permute-start | bytes 4718600 | tf_op jit(solution)/shard_map/ppermute | solution.py:51
  54.1 65.9 %collective-permute-start.12 = (bf16[4,128,1536]{2,1,0:T(8,128)(2,1)S(1)}, bf16[4,128,1536]{2,1,0:T(8,128)(2,1)S(1)}, u32[]{:S(2)}, u32[]{:S(2)}) collective-permute-start(bf16[4,128,1536]{2,1,0:T(8,128)(2,1)S(1)} %copy-done.4), channel_id=1, source_target_pairs={{0,24},{8,0},{16,8},{24,16},{32,56},{40,32},{48,40},{56,48},{64,88... | collective-permute-start | bytes 4718600 | tf_op jit(solution)/shard_map/ppermute | solution.py:52
  109.6 4.3 %copy-start.6 = (bf16[4,128,1536]{2,1,0:T(8,128)(2,1)}, bf16[4,128,1536]{2,1,0:T(8,128)(2,1)S(1)}, u32[]{:S(2)}) copy-start(bf16[4,128,1536]{2,1,0:T(8,128)(2,1)S(1)} %collective-permute-done.9) | copy-start | bytes 4718596
  110.6 35.8 %collective-permute-start.10 = (bf16[2,128,1536]{2,1,0:T(8,128)(2,1)}, bf16[2,128,1536]{2,1,0:T(8,128)(2,1)}, u32[]{:S(2)}, u32[]{:S(2)}) collective-permute-start(bf16[2,128,1536]{2,1,0:T(8,128)(2,1)} %slice.94), channel_id=1, source_target_pairs={{0,32},{8,40},{16,48},{24,56},{32,64},{40,72},{48,80},{56,88},{64,... | collective-permute-start | bytes 2359304 | tf_op jit(solution)/shard_map/ppermute | solution.py:55
  112.9 2.4 copy-start.8
  114.0 34.0 %collective-permute-start.11 = (bf16[2,128,1536]{2,1,0:T(8,128)(2,1)}, bf16[2,128,1536]{2,1,0:T(8,128)(2,1)}, u32[]{:S(2)}, u32[]{:S(2)}) collective-permute-start(bf16[2,128,1536]{2,1,0:T(8,128)(2,1)} %slice.95), channel_id=1, source_target_pairs={{0,96},{8,104},{16,112},{24,120},{32,0},{40,8},{48,16},{56,24},{64... | collective-permute-start | bytes 2359304 | tf_op jit(solution)/shard_map/ppermute | solution.py:55
  114.3 6.6 %copy-start.10 = (bf16[4,128,1536]{2,1,0:T(8,128)(2,1)}, bf16[4,128,1536]{2,1,0:T(8,128)(2,1)S(1)}, u32[]{:S(2)}) copy-start(bf16[4,128,1536]{2,1,0:T(8,128)(2,1)S(1)} %collective-permute-done.13) | copy-start | bytes 4718596
  115.4 38.3 %collective-permute-start.14 = (bf16[2,128,1536]{2,1,0:T(8,128)(2,1)}, bf16[2,128,1536]{2,1,0:T(8,128)(2,1)}, u32[]{:S(2)}, u32[]{:S(2)}) collective-permute-start(bf16[2,128,1536]{2,1,0:T(8,128)(2,1)} %slice.96), channel_id=1, source_target_pairs={{0,8},{8,16},{16,24},{24,0},{32,40},{40,48},{48,56},{56,32},{64,72... | collective-permute-start | bytes 2359304 | tf_op jit(solution)/shard_map/ppermute | solution.py:55
  119.9 2.2 copy-start.12
  120.9 33.8 %collective-permute-start.15 = (bf16[2,128,1536]{2,1,0:T(8,128)(2,1)}, bf16[2,128,1536]{2,1,0:T(8,128)(2,1)}, u32[]{:S(2)}, u32[]{:S(2)}) collective-permute-start(bf16[2,128,1536]{2,1,0:T(8,128)(2,1)} %slice.97), channel_id=1, source_target_pairs={{0,24},{8,0},{16,8},{24,16},{32,56},{40,32},{48,40},{56,48},{64,88... | collective-permute-start | bytes 2359304 | tf_op jit(solution)/shard_map/ppermute | solution.py:55
  149.5 6.9 %copy-start.11 = (bf16[4,128,1536]{2,1,0:T(8,128)(2,1)S(1)}, bf16[4,128,1536]{2,1,0:T(8,128)(2,1)}, u32[]{:S(2)}) copy-start(bf16[4,128,1536]{2,1,0:T(8,128)(2,1)} %copy-done.10) | copy-start | bytes 4718596
  149.5 6.9 %copy-start.13 = (bf16[4,128,1536]{2,1,0:T(8,128)(2,1)S(1)}, bf16[4,128,1536]{2,1,0:T(8,128)(2,1)}, u32[]{:S(2)}) copy-start(bf16[4,128,1536]{2,1,0:T(8,128)(2,1)} %copy-done.12) | copy-start | bytes 4718596
  156.4 3.5 %copy-start.7 = (bf16[4,128,1536]{2,1,0:T(8,128)(2,1)S(1)}, bf16[4,128,1536]{2,1,0:T(8,128)(2,1)}, u32[]{:S(2)}) copy-start(bf16[4,128,1536]{2,1,0:T(8,128)(2,1)} %copy-done.6) | copy-start | bytes 4718596
  156.4 3.5 %copy-start.9 = (bf16[4,128,1536]{2,1,0:T(8,128)(2,1)S(1)}, bf16[4,128,1536]{2,1,0:T(8,128)(2,1)}, u32[]{:S(2)}) copy-start(bf16[4,128,1536]{2,1,0:T(8,128)(2,1)} %copy-done.8) | copy-start | bytes 4718596
  163.5 19.2 %copy-start.3 = (bf16[128,3072]{1,0:T(8,128)(2,1)S(1)}, bf16[128,3072]{1,0:T(8,128)(2,1)}, u32[]{:S(2)}) copy-start(bf16[128,3072]{1,0:T(8,128)(2,1)} %param.7) | copy-start | bytes 2359300
  165.1 20.3 %copy-start.2 = (bf16[256,384]{1,0:T(8,128)(2,1)S(1)}, bf16[256,384]{1,0:T(8,128)(2,1)}, u32[]{:S(2)}) copy-start(bf16[256,384]{1,0:T(8,128)(2,1)} %param.5) | copy-start | bytes 589828
  191.0 83.7 %copy-start.14 = (bf16[384,3072]{1,0:T(8,128)(2,1)S(1)}, bf16[384,3072]{1,0:T(8,128)(2,1)}, u32[]{:S(2)}) copy-start(bf16[384,3072]{1,0:T(8,128)(2,1)} %param.8) | copy-start | bytes 7077892
  191.0 94.3 %all-to-all-start.1 = ((bf16[8,256,384]{2,1,0:T(8,128)(2,1)}), bf16[8,256,384]{2,1,0:T(8,128)(2,1)}, u32[]{:S(2)}, u32[]{:S(2)}) async-start(bf16[8,256,384]{2,1,0:T(8,128)(2,1)} %bitcast.24), calls=%async_computation.2 | async-start | bytes 3145728 | tf_op jit(solution)/shard_map/all_to_all | solution.py:16
  285.3 25.8 %all-to-all-start = ((bf16[8,256,384]{2,1,0:T(8,128)(2,1)}), bf16[8,256,384]{2,1,0:T(8,128)(2,1)}, u32[]{:S(2)}, u32[]{:S(2)}) async-start(bf16[8,256,384]{2,1,0:T(8,128)(2,1)} %bitcast.22), calls=%async_computation.1 | async-start | bytes 3145728 | tf_op jit(solution)/shard_map/all_to_all | solution.py:20
  290.4 23.0 %copy-start.1 = (bf16[3072,384]{1,0:T(8,128)(2,1)S(1)}, bf16[3072,384]{1,0:T(8,128)(2,1)}, u32[]{:S(2)}) copy-start(bf16[3072,384]{1,0:T(8,128)(2,1)} %param.9) | copy-start | bytes 7077892
Sparse Core Ops, SparseCore 0:
  9.7 27.9 all-gather.2
  48.9 133.6 reduce-scatter.1
  185.6 89.1 all-gather.4

commit v8 on v5

--- a/solution.py
+++ b/solution.py
@@ -47,25 +47,23 @@
     return lax.dynamic_slice_in_dim(rel, start, rows, axis=0)
 
 
-def ring_gather(x, fwd, bwd):
+def ring_gather(x, fwd, bwd, hold=None):
     from_prev = lax.ppermute(x, "row", fwd)
     from_next = lax.ppermute(x, "row", bwd)
+    if hold is not None:
+        from_prev, from_next, hold = lax.optimization_barrier((from_prev, from_next, hold))
     h = x.shape[0] // 2
     far = jnp.concatenate(
         [lax.ppermute(from_prev[:h], "row", fwd), lax.ppermute(from_next[h:], "row", bwd)], 0
     )
-    return jnp.stack([x, from_next, far, from_prev])
+    return jnp.stack([x, from_next, far, from_prev]), hold
 
 
-def torus_gather(block, n_z, n_x):
+def torus_perms(n_z, n_x):
     def perm(dz, dx):
         return [(z * n_x + x, ((z + dz) % n_z) * n_x + (x + dx) % n_x)
                 for z in range(n_z) for x in range(n_x)]
-    fx, bx, fz, bz = perm(0, 1), perm(0, -1), perm(1, 0), perm(-1, 0)
-    w = block.shape[1] // 2
-    a = ring_gather(ring_gather(block[:, :w], fx, bx), fz, bz)
-    b = ring_gather(ring_gather(block[:, w:], fz, bz), fx, bx)
-    return a, b
+    return perm(0, 1), perm(0, -1), perm(1, 0), perm(-1, 0)
 
 
 def on_device(inputs, out_grad, pre_act, w_in, w_out):
@@ -73,13 +71,21 @@
     value, slope = gelu_parts(pre_act)
     hidden_loc = value.astype(jnp.bfloat16)
     n_z, n_x = 4, 4
-    hid_a, hid_b = torus_gather(hidden_loc, n_z, n_x)
-    grad_all = gather_by_all_to_all(out_grad, "col", n_col)
+    grad_all = lax.all_gather(out_grad, "col", axis=0, tiled=True)
+    fx, bx, fz, bz = torus_perms(n_z, n_x)
+    w = hidden_loc.shape[1] // 2
+    a1, _ = ring_gather(hidden_loc[:, :w], fx, bx)
+    b1, _ = ring_gather(hidden_loc[:, w:], fz, bz)
+    a1, b1, grad_all = lax.optimization_barrier((a1, b1, grad_all))
     inputs_all = gather_by_all_to_all(inputs, "col", n_col)
     partial = lax.dot_general(
         grad_all, w_out, (((1,), (1,)), ((), ())), preferred_element_type=jnp.float32
     ).astype(jnp.bfloat16)
     total = lax.psum_scatter(partial, "row", scatter_dimension=0, tiled=True)
+    hid_a, total = ring_gather(a1, fz, bz, total)
+    hid_b, total = ring_gather(b1, fx, bx, total)
+    pre_grad_loc = (total.astype(jnp.float32) * slope).astype(jnp.bfloat16)
+    pre_grad = lax.all_gather(pre_grad_loc, "row", axis=0, tiled=True)
     me = lax.axis_index("row")
     grad4 = grad_all.reshape((n_z, n_x, -1, grad_all.shape[1]))
     grad_rel = jnp.roll(grad4, (-(me // n_x), -(me % n_x)), axis=(0, 1))
@@ -93,9 +99,7 @@
         (((0,), (0,)), ((), ())), preferred_element_type=jnp.float32
     )
     w_out_grad = jnp.concatenate([w_out_a, w_out_b], axis=0).astype(jnp.bfloat16)
-    total, w_out_grad = lax.optimization_barrier((total, w_out_grad))
-    pre_grad_loc = (total.astype(jnp.float32) * slope).astype(jnp.bfloat16)
-    pre_grad = lax.all_gather(pre_grad_loc, "row", axis=0, tiled=True)
+    pre_grad, w_out_grad = lax.optimization_barrier((pre_grad, w_out_grad))
     in_part = lax.dot_general(
         pre_grad, w_in, (((1,), (1,)), ((), ())), preferred_element_type=jnp.float32
     ).astype(jnp.bfloat16)

time: 338 us -> 317 us (0.938)
  blocking collectives: 26.3 us -> 0 us
  waiting for transfers between devices: 183 us -> 195 us
  starting transfers between devices: 45.4 us -> 35.6 us
  matrix products: 37.7 us -> 43 us
    ppermute x4, waiting for transfers between devices: 70.3 us -> 1.81 us  [ring_gather(): from_next = lax.ppermute(x, 'row', bwd)]
    ppermute x4, waiting for transfers between devices: 0.22 us -> 62.3 us  [ring_gather(): from_prev = lax.ppermute(x, 'row', fwd)]
    reduce_scatter x1, waiting for transfers between devices: 6.16 us -> 55 us  [on_device(): total = lax.psum_scatter(partial, 'row', scatter_dimension=0, tiled=True)]
    all_gather x1, waiting for transfers between devices: 76.4 us -> 43.8 us  [on_device(): pre_grad = lax.all_gather(pre_grad_loc, 'row', axis=0, tiled=True)]
    all_to_all x1 -> x0, blocking collectives: 26.3 us -> none  [gather_by_all_to_all(): return lax.all_to_all(rep, axis, 0, 0, tiled=True)]
    all_to_all x1, starting transfers between devices: 15.2 us -> 6.45 us  [gather_by_all_to_all(): return lax.all_to_all(rep, axis, 0, 0, tiled=True)]
    unnamed x50 -> x19, local copies, waits for them, and re-layouts: 12.4 us -> 4.91 us
    ppermute x4, starting transfers between devices: 0.01 us -> 6.1 us  [ring_gather(): from_prev = lax.ppermute(x, 'row', fwd)]
  transfers between devices with their start and end apart: 20 -> 21, of which waited for: 13 -> 12; matrix products, arithmetic and copies ran while one was open for 13% -> 18% of each run, Pallas kernels for 0% -> 0%
where the time goes in v8:
time: 317 us
  waiting for transfers between devices  195 us (62%)
  matrix products  43 us (14%)
  starting transfers between devices  35.6 us (11%)
  other arithmetic  16 us (5%)
  between operations  13.9 us (4%)
  local copies, waits for them, and re-layouts  13.3 us (4%)
    ppermute x4, waiting for transfers between devices, ring_gather(): from_prev = lax.ppermute(x, 'row', fwd)  62.3 us
    reduce_scatter x1, waiting for transfers between devices, on_device(): total = lax.psum_scatter(partial, 'row', scatter_dimension=0, tiled=True)  55 us
    all_gather x1, waiting for transfers between devices, on_device(): pre_grad = lax.all_gather(pre_grad_loc, 'row', axis=0, tiled=True)  43.8 us
    ppermute x4, waiting for transfers between devices, ring_gather(): lax.ppermute(from_prev[:h], 'row', fwd)  11.3 us
    dot_general x1, matrix products, on_device(): lax.dot_general(pre_grad, w_in, (((1,), (1,)), ((), ())), preferred_eleme...  11.2 us
    dot_general x1, matrix products, on_device(): lax.dot_general(grad_all, w_out, (((1,), (1,)), ((), ())), preferred_elem...  11.1 us
    all_to_all x1, waiting for transfers between devices, scatter_sum_by_all_to_all(): got = lax.all_to_all(x, axis, 0, 0, tiled=True)  11 us
    dot_general x1, matrix products, on_device(): lax.dot_general(inputs_all, pre_grad, (((0,), (0,)), ((), ())), preferred...  9.68 us
  transfers between devices with their start and end apart: 21, of which 12 were waited for; matrix products, arithmetic and copies ran while one was open for 18% of the time, Pallas kernels for 0%

profile of v8, /device:TPU:1, one launch (start us, length us, event | category | flops | bytes accessed | tf_op | source)
XLA Modules:
  0.0 316.8 jit_solution(18381229326398747510)
XLA Ops:
  8.0 1.5 fusion.31
  9.5 2.5 collective-permute-start.5
  12.1 2.2 collective-permute-start.4
  14.3 1.2 collective-permute-start.1
  15.5 1.5 collective-permute-start
  16.9 6.1 %collective-permute-done.5 = bf16[128,1536]{1,0:T(8,128)(2,1)S(1)} collective-permute-done((bf16[128,1536]{1,0:T(8,128)(2,1)S(1)}, bf16[128,1536]{1,0:T(8,128)(2,1)S(1)}, u32[]{:S(2)}, u32[]{:S(2)}) %collective-permute-start.5) | collective-permute-done | bytes 393248 | tf_op jit(solution)/shard_map/ppermute | solution.py:51
  23.1 2.7 collective-permute-start.7
  25.9 1.3 collective-permute-start.2
  27.2 1.5 collective-permute-start.3
  28.7 0.8 collective-permute-done.6
  29.6 2.3 collective-permute-done.2
  31.9 1.3 pad_maximum_fusion.2
  33.3 1.3 pad_maximum_fusion.1
  34.6 3.1 all-gather.3.cloned.1.call-done
  37.7 11.1 %convolution_convert_fusion = bf16[2048,3072]{1,0:T(8,128)(2,1)} fusion(bf16[2048,384]{1,0:T(8,128)(2,1)} %all-gather.3.cloned.1.call-done, bf16[3072,384]{1,0:T(8,128)(2,1)S(1)} %copy-done), kind=kOutput, calls=%fused_computation | convolution fusion | flops 4838129664 | bytes 16515072 | tf_op jit(solution)/shard_map/dot_general | solution.py:81
  48.9 1.2 collective-permute-start.10
  50.1 1.6 collective-permute-start.11
  51.7 1.1 collective-permute-start.8
  52.8 1.6 collective-permute-start.9
  54.4 56.3 %collective-permute-done.10 = bf16[4,128,1536]{2,1,0:T(8,128)(2,1)} collective-permute-done((bf16[4,128,1536]{2,1,0:T(8,128)(2,1)}, bf16[4,128,1536]{2,1,0:T(8,128)(2,1)}, u32[]{:S(2)}, u32[]{:S(2)}) %collective-permute-start.10) | collective-permute-done | bytes 1572896 | tf_op jit(solution)/shard_map/ppermute | solution.py:51
  110.7 1.8 collective-permute-done.11
  112.5 55.0 %reduce-scatter.2.cloned.1.call-done = bf16[128,3072]{1,0:T(8,128)(2,1)} async-done(((bf16[2048,3072]{1,0:T(8,128)(2,1)}), bf16[128,3072]{1,0:T(8,128)(2,1)}) %reduce-scatter.2.cloned.1.call-update) | async-done | bytes 786448 | tf_op jit(solution)/shard_map/reduce_scatter | solution.py:84
  167.4 2.7 fusion.36
  170.2 0.7 constant_dynamic-update-slice_fusion.7
  170.9 0.7 constant_dynamic-update-slice_fusion.6
  171.6 1.2 slice.76
  172.9 2.1 slice.77
  175.0 2.7 collective-permute-start.13
  177.6 0.7 constant_dynamic-update-slice_fusion.5
  179.0 2.1 slice.78
  181.2 2.2 slice.79
  183.3 2.7 collective-permute-start.15
  188.8 6.5 %all-to-all-start.1 = ((bf16[8,256,384]{2,1,0:T(8,128)(2,1)}), bf16[8,256,384]{2,1,0:T(8,128)(2,1)}, u32[]{:S(2)}, u32[]{:S(2)}) async-start(bf16[8,256,384]{2,1,0:T(8,128)(2,1)} %bitcast.24), calls=%async_computation.2 | async-start | bytes 3145728 | tf_op jit(solution)/shard_map/all_to_all | solution.py:16
  195.2 2.1 fusion.38
  197.3 2.0 collective-permute-done.12
  199.4 5.8 %collective-permute-done.13 = bf16[2,128,1536]{2,1,0:T(8,128)(2,1)} collective-permute-done((bf16[2,128,1536]{2,1,0:T(8,128)(2,1)}, bf16[2,128,1536]{2,1,0:T(8,128)(2,1)}, u32[]{:S(2)}, u32[]{:S(2)}) %collective-permute-start.13) | collective-permute-done | bytes 786464 | tf_op jit(solution)/shard_map/ppermute | solution.py:57
  205.2 1.5 maximum_bitcast_fusion
  206.7 6.2 %collective-permute-done.14 = bf16[2,128,1536]{2,1,0:T(8,128)(2,1)} collective-permute-done((bf16[2,128,1536]{2,1,0:T(8,128)(2,1)}, bf16[2,128,1536]{2,1,0:T(8,128)(2,1)}, u32[]{:S(2)}, u32[]{:S(2)}) %collective-permute-start.14) | collective-permute-done | bytes 786464 | tf_op jit(solution)/shard_map/ppermute | solution.py:57
  212.9 1.5 maximum_bitcast_fusion.1
  214.4 5.5 %fusion.25 = bf16[1536,384]{1,0:T(8,128)(2,1)S(1)} fusion(bf16[1,4,128,1536]{3,2,1,0:T(8,128)(2,1)} %bitcast.18, bf16[1,4,128,1536]{3,2,1,0:T(8,128)(2,1)S(1)} %maximum_bitcast_fusion.1, bf16[1,4,128,1536]{3,2,1,0:T(8,128)(2,1)} %bitcast.16, bf16[1,4,128,1536]{3,2,1,0:T(8,128)(2,1)S(1)} %bitcast.50, s32[]{:T(128)S(6)} %select_n.38, ...), kind=kOutput, calls=%fused_computation.30 | convolution fusion | flops 2426732544 | bytes 9043972 | tf_op jit(solution)/shard_map/dot_general | solution.py:97
  219.9 5.4 %fusion.22 = bf16[1536,384]{1,0:T(8,128)(2,1)S(1)} fusion(bf16[1,4,128,1536]{3,2,1,0:T(8,128)(2,1)} %bitcast.11, bf16[1,4,128,1536]{3,2,1,0:T(8,128)(2,1)S(1)} %maximum_bitcast_fusion, bf16[1,4,128,1536]{3,2,1,0:T(8,128)(2,1)} %bitcast.9, bf16[1,4,128,1536]{3,2,1,0:T(8,128)(2,1)S(1)} %bitcast.51, s32[]{:T(128)S(6)} %select_n.38, ...), kind=kOutput, calls=%fused_computation.29 | convolution fusion | flops 2426732544 | bytes 9043972 | tf_op jit(solution)/shard_map/dot_general | solution.py:93
  225.3 1.6 pad_maximum_fusion
  227.0 43.8 %all-gather.5.cloned.1.call-done = bf16[2048,3072]{1,0:T(8,128)(2,1)} async-done(((bf16[128,3072]{1,0:T(8,128)(2,1)}), bf16[2048,3072]{1,0:T(8,128)(2,1)}) %all-gather.5.cloned.1.call-update) | async-done | bytes 12582928 | tf_op jit(solution)/shard_map/all_gather | solution.py:88
  270.8 11.2 %convolution_convert_fusion.2 = bf16[2048,384]{1,0:T(8,128)(2,1)} fusion(bf16[2048,3072]{1,0:T(8,128)(2,1)} %all-gather.5.cloned.1.call-done, bf16[384,3072]{1,0:T(8,128)(2,1)} %param.8), kind=kOutput, calls=%fused_computation.31 | convolution fusion | flops 4832624640 | bytes 16515072 | tf_op jit(solution)/shard_map/dot_general | solution.py:103
  282.1 5.1 %all-to-all-start = ((bf16[8,256,384]{2,1,0:T(8,128)(2,1)}), bf16[8,256,384]{2,1,0:T(8,128)(2,1)}, u32[]{:S(2)}, u32[]{:S(2)}) async-start(bf16[8,256,384]{2,1,0:T(8,128)(2,1)} %bitcast.22), calls=%async_computation.1 | async-start | bytes 3145728 | tf_op jit(solution)/shard_map/all_to_all | solution.py:20
  287.2 9.7 %convolution_convert_fusion.1 = bf16[384,3072]{1,0:T(8,128)(2,1)} fusion(bf16[2048,384]{1,0:T(8,128)(2,1)} %bitcast.25, bf16[2048,3072]{1,0:T(8,128)(2,1)} %all-gather.5.cloned.1.call-done), kind=kOutput, calls=%fused_computation.17 | convolution fusion | flops 4833017856 | bytes 16515072 | tf_op jit(solution)/shard_map/dot_general | solution.py:107
  296.9 11.0 %all-to-all-done = bf16[8,256,384]{2,1,0:T(8,128)(2,1)} async-done(((bf16[8,256,384]{2,1,0:T(8,128)(2,1)}), bf16[8,256,384]{2,1,0:T(8,128)(2,1)}, u32[]{:S(2)}, u32[]{:S(2)}) %all-to-all-start) | async-done | bytes 1572896 | tf_op jit(solution)/shard_map/all_to_all | solution.py:20
  307.9 2.3 fusion.40
  (42 shorter events, 4.7 us)
Async XLA Ops:
  7.2 30.5 %copy-start = (bf16[3072,384]{1,0:T(8,128)(2,1)S(1)}, bf16[3072,384]{1,0:T(8,128)(2,1)}, u32[]{:S(2)}) copy-start(bf16[3072,384]{1,0:T(8,128)(2,1)} %param.9) | copy-start | bytes 7077892
  7.2 30.5 %all-gather.3.cloned.1.call-start = ((), (), s32[]{:S(2)}) async-start(), calls=%async_computation.3 | async-start | bytes 1769472 | tf_op jit(solution)/shard_map/all_gather | solution.py:74
  7.9 159.5 %reduce-scatter.2.cloned.1.call-start = ((), (), s32[]{:S(2)}) async-start(), calls=%async_computation.4 | async-start | bytes 13369344 | tf_op jit(solution)/shard_map/reduce_scatter | solution.py:84
  9.5 13.5 %collective-permute-start.5 = (bf16[128,1536]{1,0:T(8,128)(2,1)S(1)}, bf16[128,1536]{1,0:T(8,128)(2,1)S(1)}, u32[]{:S(2)}, u32[]{:S(2)}) collective-permute-start(bf16[128,1536]{1,0:T(8,128)(2,1)S(1)} %get-tuple-element.27), channel_id=1, source_target_pairs={{0,32},{8,40},{16,48},{24,56},{32,64},{40,72},{48,80},{56,88},{64,... | collective-permute-start | bytes 1179656 | tf_op jit(solution)/shard_map/ppermute | solution.py:51
  12.1 11.0 %collective-permute-start.4 = (bf16[128,1536]{1,0:T(8,128)(2,1)S(1)}, bf16[128,1536]{1,0:T(8,128)(2,1)S(1)}, u32[]{:S(2)}, u32[]{:S(2)}) collective-permute-start(bf16[128,1536]{1,0:T(8,128)(2,1)S(1)} %get-tuple-element.27), channel_id=1, source_target_pairs={{0,96},{8,104},{16,112},{24,120},{32,0},{40,8},{48,16},{56,24},{64... | collective-permute-start | bytes 1179656 | tf_op jit(solution)/shard_map/ppermute | solution.py:52
  14.3 11.6 %collective-permute-start.1 = (bf16[128,1536]{1,0:T(8,128)(2,1)S(1)}, bf16[128,1536]{1,0:T(8,128)(2,1)S(1)}, u32[]{:S(2)}, u32[]{:S(2)}) collective-permute-start(bf16[128,1536]{1,0:T(8,128)(2,1)S(1)} %get-tuple-element.28), channel_id=1, source_target_pairs={{0,8},{8,16},{16,24},{24,0},{32,40},{40,48},{48,56},{56,32},{64,72... | collective-permute-start | bytes 1179656 | tf_op jit(solution)/shard_map/ppermute | solution.py:51
  15.5 11.7 %collective-permute-start = (bf16[128,1536]{1,0:T(8,128)(2,1)S(1)}, bf16[128,1536]{1,0:T(8,128)(2,1)S(1)}, u32[]{:S(2)}, u32[]{:S(2)}) collective-permute-start(bf16[128,1536]{1,0:T(8,128)(2,1)S(1)} %get-tuple-element.28), channel_id=1, source_target_pairs={{0,24},{8,0},{16,8},{24,16},{32,56},{40,32},{48,40},{56,48},{64,88... | collective-permute-start | bytes 1179656 | tf_op jit(solution)/shard_map/ppermute | solution.py:52
  23.0 6.5 %collective-permute-start.6 = (bf16[64,1536]{1,0:T(8,128)(2,1)S(1)}, bf16[64,1536]{1,0:T(8,128)(2,1)S(1)}, u32[]{:S(2)}, u32[]{:S(2)}) collective-permute-start(bf16[64,1536]{1,0:T(8,128)(2,1)S(1)} %slice.92), channel_id=1, source_target_pairs={{0,32},{8,40},{16,48},{24,56},{32,64},{40,72},{48,80},{56,88},{64,... | collective-permute-start | bytes 589832 | tf_op jit(solution)/shard_map/ppermute | solution.py:57
  23.1 6.4 %collective-permute-start.7 = (bf16[64,1536]{1,0:T(8,128)(2,1)S(1)}, bf16[64,1536]{1,0:T(8,128)(2,1)S(1)}, u32[]{:S(2)}, u32[]{:S(2)}) collective-permute-start(bf16[64,1536]{1,0:T(8,128)(2,1)S(1)} %slice.93), channel_id=1, source_target_pairs={{0,96},{8,104},{16,112},{24,120},{32,0},{40,8},{48,16},{56,24},{64... | collective-permute-start | bytes 589832 | tf_op jit(solution)/shard_map/ppermute | solution.py:57
  25.9 6.0 %collective-permute-start.2 = (bf16[64,1536]{1,0:T(8,128)(2,1)S(1)}, bf16[64,1536]{1,0:T(8,128)(2,1)S(1)}, u32[]{:S(2)}, u32[]{:S(2)}) collective-permute-start(bf16[64,1536]{1,0:T(8,128)(2,1)S(1)} %slice.89), channel_id=1, source_target_pairs={{0,8},{8,16},{16,24},{24,0},{32,40},{40,48},{48,56},{56,32},{64,72... | collective-permute-start | bytes 589832 | tf_op jit(solution)/shard_map/ppermute | solution.py:57
  27.2 4.7 %collective-permute-start.3 = (bf16[64,1536]{1,0:T(8,128)(2,1)S(1)}, bf16[64,1536]{1,0:T(8,128)(2,1)S(1)}, u32[]{:S(2)}, u32[]{:S(2)}) collective-permute-start(bf16[64,1536]{1,0:T(8,128)(2,1)S(1)} %slice.90), channel_id=1, source_target_pairs={{0,24},{8,0},{16,8},{24,16},{32,56},{40,32},{48,40},{56,48},{64,88... | collective-permute-start | bytes 589832 | tf_op jit(solution)/shard_map/ppermute | solution.py:57
  48.8 2.9 copy-start.4
  48.8 118.6 %copy-start.3 = (bf16[128,3072]{1,0:T(8,128)(2,1)S(1)}, bf16[128,3072]{1,0:T(8,128)(2,1)}, u32[]{:S(2)}) copy-start(bf16[128,3072]{1,0:T(8,128)(2,1)} %param.7) | copy-start | bytes 2359300
  48.8 121.4 %copy-start.2 = (bf16[256,384]{1,0:T(8,128)(2,1)S(1)}, bf16[256,384]{1,0:T(8,128)(2,1)}, u32[]{:S(2)}) copy-start(bf16[256,384]{1,0:T(8,128)(2,1)} %param.5) | copy-start | bytes 589828
  48.8 222.0 %all-gather.5.cloned.1.call-start = ((), (), s32[]{:S(2)}) async-start(), calls=%async_computation.5 | async-start | bytes 13369344 | tf_op jit(solution)/shard_map/all_gather | solution.py:88
  48.9 61.8 %collective-permute-start.10 = (bf16[4,128,1536]{2,1,0:T(8,128)(2,1)}, bf16[4,128,1536]{2,1,0:T(8,128)(2,1)}, u32[]{:S(2)}, u32[]{:S(2)}) collective-permute-start(bf16[4,128,1536]{2,1,0:T(8,128)(2,1)} %pad_maximum_fusion.1), channel_id=1, source_target_pairs={{0,32},{8,40},{16,48},{24,56},{32,64},{40,72},{48,80},{56,88},{64,... | collective-permute-start | bytes 4718600 | tf_op jit(solution)/shard_map/ppermute | solution.py:51
  50.1 62.3 %collective-permute-start.11 = (bf16[4,128,1536]{2,1,0:T(8,128)(2,1)}, bf16[4,128,1536]{2,1,0:T(8,128)(2,1)}, u32[]{:S(2)}, u32[]{:S(2)}) collective-permute-start(bf16[4,128,1536]{2,1,0:T(8,128)(2,1)} %pad_maximum_fusion.1), channel_id=1, source_target_pairs={{0,96},{8,104},{16,112},{24,120},{32,0},{40,8},{48,16},{56,24},{64... | collective-permute-start | bytes 4718600 | tf_op jit(solution)/shard_map/ppermute | solution.py:52
  51.7 115.7 %collective-permute-start.8 = (bf16[4,128,1536]{2,1,0:T(8,128)(2,1)S(1)}, bf16[4,128,1536]{2,1,0:T(8,128)(2,1)}, u32[]{:S(2)}, u32[]{:S(2)}) collective-permute-start(bf16[4,128,1536]{2,1,0:T(8,128)(2,1)S(1)} %copy-done.4), channel_id=1, source_target_pairs={{0,8},{8,16},{16,24},{24,0},{32,40},{40,48},{48,56},{56,32},{64,72... | collective-permute-start | bytes 4718600 | tf_op jit(solution)/shard_map/ppermute | solution.py:51
  52.8 114.6 %collective-permute-start.9 = (bf16[4,128,1536]{2,1,0:T(8,128)(2,1)S(1)}, bf16[4,128,1536]{2,1,0:T(8,128)(2,1)}, u32[]{:S(2)}, u32[]{:S(2)}) collective-permute-start(bf16[4,128,1536]{2,1,0:T(8,128)(2,1)S(1)} %copy-done.4), channel_id=1, source_target_pairs={{0,24},{8,0},{16,8},{24,16},{32,56},{40,32},{48,40},{56,48},{64,88... | collective-permute-start | bytes 4718600 | tf_op jit(solution)/shard_map/ppermute | solution.py:52
  172.8 26.6 %collective-permute-start.12 = (bf16[2,128,1536]{2,1,0:T(8,128)(2,1)S(1)}, bf16[2,128,1536]{2,1,0:T(8,128)(2,1)}, u32[]{:S(2)}, u32[]{:S(2)}) collective-permute-start(bf16[2,128,1536]{2,1,0:T(8,128)(2,1)S(1)} %slice.76), channel_id=1, source_target_pairs={{0,32},{8,40},{16,48},{24,56},{32,64},{40,72},{48,80},{56,88},{64,... | collective-permute-start | bytes 2359304 | tf_op jit(solution)/shard_map/ppermute | solution.py:57
  175.0 30.3 %collective-permute-start.13 = (bf16[2,128,1536]{2,1,0:T(8,128)(2,1)}, bf16[2,128,1536]{2,1,0:T(8,128)(2,1)}, u32[]{:S(2)}, u32[]{:S(2)}) collective-permute-start(bf16[2,128,1536]{2,1,0:T(8,128)(2,1)} %slice.77), channel_id=1, source_target_pairs={{0,96},{8,104},{16,112},{24,120},{32,0},{40,8},{48,16},{56,24},{64... | collective-permute-start | bytes 2359304 | tf_op jit(solution)/shard_map/ppermute | solution.py:57
  181.1 31.7 %collective-permute-start.14 = (bf16[2,128,1536]{2,1,0:T(8,128)(2,1)}, bf16[2,128,1536]{2,1,0:T(8,128)(2,1)}, u32[]{:S(2)}, u32[]{:S(2)}) collective-permute-start(bf16[2,128,1536]{2,1,0:T(8,128)(2,1)} %slice.78), channel_id=1, source_target_pairs={{0,8},{8,16},{16,24},{24,0},{32,40},{40,48},{48,56},{56,32},{64,72... | collective-permute-start | bytes 2359304 | tf_op jit(solution)/shard_map/ppermute | solution.py:57
  183.3 29.5 %collective-permute-start.15 = (bf16[2,128,1536]{2,1,0:T(8,128)(2,1)}, bf16[2,128,1536]{2,1,0:T(8,128)(2,1)}, u32[]{:S(2)}, u32[]{:S(2)}) collective-permute-start(bf16[2,128,1536]{2,1,0:T(8,128)(2,1)} %slice.79), channel_id=1, source_target_pairs={{0,24},{8,0},{16,8},{24,16},{32,56},{40,32},{48,40},{56,48},{64,88... | collective-permute-start | bytes 2359304 | tf_op jit(solution)/shard_map/ppermute | solution.py:57
  188.8 93.3 %all-to-all-start.1 = ((bf16[8,256,384]{2,1,0:T(8,128)(2,1)}), bf16[8,256,384]{2,1,0:T(8,128)(2,1)}, u32[]{:S(2)}, u32[]{:S(2)}) async-start(bf16[8,256,384]{2,1,0:T(8,128)(2,1)} %bitcast.24), calls=%async_computation.2 | async-start | bytes 3145728 | tf_op jit(solution)/shard_map/all_to_all | solution.py:16
  214.4 5.5 %copy-start.5 = (bf16[4,128,1536]{2,1,0:T(8,128)(2,1)S(1)}, bf16[4,128,1536]{2,1,0:T(8,128)(2,1)}, u32[]{:S(2)}) copy-start(bf16[4,128,1536]{2,1,0:T(8,128)(2,1)} %pad_maximum_fusion.1) | copy-start | bytes 4718596
  282.1 25.8 %all-to-all-start = ((bf16[8,256,384]{2,1,0:T(8,128)(2,1)}), bf16[8,256,384]{2,1,0:T(8,128)(2,1)}, u32[]{:S(2)}, u32[]{:S(2)}) async-start(bf16[8,256,384]{2,1,0:T(8,128)(2,1)} %bitcast.22), calls=%async_computation.1 | async-start | bytes 3145728 | tf_op jit(solution)/shard_map/all_to_all | solution.py:20
  287.2 23.0 %copy-start.1 = (bf16[3072,384]{1,0:T(8,128)(2,1)S(1)}, bf16[3072,384]{1,0:T(8,128)(2,1)}, u32[]{:S(2)}) copy-start(bf16[3072,384]{1,0:T(8,128)(2,1)} %param.9) | copy-start | bytes 7077892
Sparse Core Ops, SparseCore 0:
  9.7 27.9 all-gather.2
  48.9 118.4 reduce-scatter.1
  170.3 100.4 all-gather.4

commit v9 on v8

--- a/solution.py
+++ b/solution.py
@@ -66,6 +66,25 @@
     return perm(0, 1), perm(0, -1), perm(1, 0), perm(-1, 0)
 
 
+def scatter_sum_col(x, n_y):
+    n_col = 2 * n_y
+    me = lax.axis_index("col")
+    k, y = me % 2, me // 2
+    blk = x.shape[0] // n_col
+    x4 = x.reshape((n_y, 2, blk) + x.shape[1:])
+    mine = lax.dynamic_index_in_dim(x4, k, axis=1, keepdims=False)
+    other = lax.dynamic_index_in_dim(x4, 1 - k, axis=1, keepdims=False)
+    got = lax.ppermute(other, "col", [(c, c ^ 1) for c in range(n_col)])
+    pair = mine.astype(jnp.float32) + got.astype(jnp.float32)
+    pair_b = pair.astype(jnp.bfloat16)
+    acc = lax.dynamic_index_in_dim(pair, y, axis=0, keepdims=False)
+    for d in range(1, n_y):
+        send = lax.dynamic_index_in_dim(pair_b, (y + d) % n_y, axis=0, keepdims=False)
+        recv = lax.ppermute(send, "col", [(c, (c + 2 * d) % n_col) for c in range(n_col)])
+        acc = acc + recv.astype(jnp.float32)
+    return acc
+
+
 def on_device(inputs, out_grad, pre_act, w_in, w_out):
     n_col = lax.psum(1, "col")
     value, slope = gelu_parts(pre_act)
@@ -103,7 +122,7 @@
     in_part = lax.dot_general(
         pre_grad, w_in, (((1,), (1,)), ((), ())), preferred_element_type=jnp.float32
     ).astype(jnp.bfloat16)
-    in_grad = scatter_sum_by_all_to_all(in_part, "col", n_col).astype(jnp.bfloat16)
+    in_grad = scatter_sum_col(in_part, n_col // 2).astype(jnp.bfloat16)
     w_in_grad = lax.dot_general(
         inputs_all, pre_grad, (((0,), (0,)), ((), ())), preferred_element_type=jnp.float32
     ).astype(jnp.bfloat16)

time: 317 us -> 309 us (0.975)
  waiting for transfers between devices: 195 us -> 186 us
    all_to_all x1 -> x0, waiting for transfers between devices: 11 us -> none  [scatter_sum_by_all_to_all(): got = lax.all_to_all(x, axis, 0, 0, tiled=True)]
    ppermute x0 -> x4, starting transfers between devices: none -> 5.79 us  [the longest x3 4.87 us: scatter_sum_col(): lax.ppermute(send, 'col', [(c, (c + 2 * d) % n_col) for c in range(n_col)])]
    all_to_all x1 -> x0, starting transfers between devices: 5.13 us -> none  [scatter_sum_by_all_to_all(): got = lax.all_to_all(x, axis, 0, 0, tiled=True)]
  transfers between devices with their start and end apart: 21 -> 24, of which waited for: 12 -> 12; matrix products, arithmetic and copies ran while one was open for 18% -> 18% of each run, Pallas kernels for 0% -> 0%
where the time goes in v9:
time: 309 us; the launch traced here: 308 us
  waiting for transfers between devices  186 us (60%)
  matrix products  42.1 us (14%)
  starting transfers between devices  36.3 us (12%)
  other arithmetic  16.8 us (5%)
  between operations  13.9 us (4%)
  local copies, waits for them, and re-layouts  13.5 us (4%)
    ppermute x4, waiting for transfers between devices, ring_gather(): from_prev = lax.ppermute(x, 'row', fwd)  62.3 us
    reduce_scatter x1, waiting for transfers between devices, on_device(): total = lax.psum_scatter(partial, 'row', scatter_dimension=0, tiled=True)  55 us
    all_gather x1, waiting for transfers between devices, on_device(): pre_grad = lax.all_gather(pre_grad_loc, 'row', axis=0, tiled=True)  43.8 us
    ppermute x4, waiting for transfers between devices, ring_gather(): lax.ppermute(from_prev[:h], 'row', fwd)  11.3 us
    dot_general x1, matrix products, on_device(): lax.dot_general(grad_all, w_out, (((1,), (1,)), ((), ())), preferred_elem...  11.2 us
    dot_general x1, matrix products, on_device(): lax.dot_general(pre_grad, w_in, (((1,), (1,)), ((), ())), preferred_eleme...  10.4 us
    dot_general x1, matrix products, on_device(): lax.dot_general(inputs_all, pre_grad, (((0,), (0,)), ((), ())), preferred...  9.68 us
    ppermute x4, starting transfers between devices, ring_gather(): lax.ppermute(from_next[h:], 'row', bwd)  9.57 us
  transfers between devices with their start and end apart: 24, of which 12 were waited for; matrix products, arithmetic and copies ran while one was open for 18% of the time, Pallas kernels for 0%

profile of v9, /device:TPU:1, one launch (start us, length us, event | category | flops | bytes accessed | tf_op | source)
XLA Modules:
  0.0 308.5 jit_solution(4408262417279364138)
XLA Ops:
  8.0 1.5 fusion.31
  9.5 2.5 collective-permute-start.5
  12.1 2.2 collective-permute-start.4
  14.3 1.2 collective-permute-start.1
  15.5 1.5 collective-permute-start
  16.9 6.1 %collective-permute-done.5 = bf16[128,1536]{1,0:T(8,128)(2,1)S(1)} collective-permute-done((bf16[128,1536]{1,0:T(8,128)(2,1)S(1)}, bf16[128,1536]{1,0:T(8,128)(2,1)S(1)}, u32[]{:S(2)}, u32[]{:S(2)}) %collective-permute-start.5) | collective-permute-done | bytes 393248 | tf_op jit(solution)/shard_map/ppermute | solution.py:51
  23.1 2.7 collective-permute-start.7
  25.9 1.3 collective-permute-start.2
  27.2 1.5 collective-permute-start.3
  29.6 2.3 collective-permute-done.2
  31.9 1.3 pad_maximum_fusion.2
  33.3 1.3 pad_maximum_fusion.1
  34.6 3.1 all-gather.3.cloned.1.call-done
  37.7 11.2 %convolution_convert_fusion = bf16[2048,3072]{1,0:T(8,128)(2,1)} fusion(bf16[2048,384]{1,0:T(8,128)(2,1)} %all-gather.3.cloned.1.call-done, bf16[3072,384]{1,0:T(8,128)(2,1)S(1)} %copy-done), kind=kOutput, calls=%fused_computation | convolution fusion | flops 4838129664 | bytes 16515072 | tf_op jit(solution)/shard_map/dot_general | solution.py:100
  48.9 1.2 collective-permute-start.10
  50.2 1.6 collective-permute-start.11
  51.8 1.1 collective-permute-start.8
  52.9 1.6 collective-permute-start.9
  54.4 56.3 %collective-permute-done.10 = bf16[4,128,1536]{2,1,0:T(8,128)(2,1)} collective-permute-done((bf16[4,128,1536]{2,1,0:T(8,128)(2,1)}, bf16[4,128,1536]{2,1,0:T(8,128)(2,1)}, u32[]{:S(2)}, u32[]{:S(2)}) %collective-permute-start.10) | collective-permute-done | bytes 1572896 | tf_op jit(solution)/shard_map/ppermute | solution.py:51
  110.7 1.8 collective-permute-done.11
  112.5 55.0 %reduce-scatter.2.cloned.1.call-done = bf16[128,3072]{1,0:T(8,128)(2,1)} async-done(((bf16[2048,3072]{1,0:T(8,128)(2,1)}), bf16[128,3072]{1,0:T(8,128)(2,1)}) %reduce-scatter.2.cloned.1.call-update) | async-done | bytes 786448 | tf_op jit(solution)/shard_map/reduce_scatter | solution.py:103
  167.5 2.8 fusion.36
  171.7 1.2 slice.36
  172.9 2.1 slice.37
  175.0 2.7 collective-permute-start.13
  179.1 2.1 slice.38
  181.2 2.2 slice.39
  183.4 2.7 collective-permute-start.15
  188.8 6.4 %all-to-all-start = ((bf16[8,256,384]{2,1,0:T(8,128)(2,1)}), bf16[8,256,384]{2,1,0:T(8,128)(2,1)}, u32[]{:S(2)}, u32[]{:S(2)}) async-start(bf16[8,256,384]{2,1,0:T(8,128)(2,1)} %bitcast.29), calls=%async_computation.1 | async-start | bytes 3145728 | tf_op jit(solution)/shard_map/all_to_all | solution.py:16
  195.3 2.1 fusion.38
  197.4 2.0 collective-permute-done.12
  199.4 5.9 %collective-permute-done.13 = bf16[2,128,1536]{2,1,0:T(8,128)(2,1)} collective-permute-done((bf16[2,128,1536]{2,1,0:T(8,128)(2,1)}, bf16[2,128,1536]{2,1,0:T(8,128)(2,1)}, u32[]{:S(2)}, u32[]{:S(2)}) %collective-permute-start.13) | collective-permute-done | bytes 786464 | tf_op jit(solution)/shard_map/ppermute | solution.py:57
  205.3 1.5 maximum_bitcast_fusion
  206.8 6.1 %collective-permute-done.14 = bf16[2,128,1536]{2,1,0:T(8,128)(2,1)} collective-permute-done((bf16[2,128,1536]{2,1,0:T(8,128)(2,1)}, bf16[2,128,1536]{2,1,0:T(8,128)(2,1)}, u32[]{:S(2)}, u32[]{:S(2)}) %collective-permute-start.14) | collective-permute-done | bytes 786464 | tf_op jit(solution)/shard_map/ppermute | solution.py:57
  212.9 1.5 maximum_bitcast_fusion.1
  214.5 5.5 %fusion.25 = bf16[1536,384]{1,0:T(8,128)(2,1)S(1)} fusion(bf16[1,4,128,1536]{3,2,1,0:T(8,128)(2,1)} %bitcast.18, bf16[1,4,128,1536]{3,2,1,0:T(8,128)(2,1)S(1)} %maximum_bitcast_fusion.1, bf16[1,4,128,1536]{3,2,1,0:T(8,128)(2,1)} %bitcast.16, bf16[1,4,128,1536]{3,2,1,0:T(8,128)(2,1)S(1)} %bitcast.68, s32[]{:T(128)S(6)} %select_n.78, ...), kind=kOutput, calls=%fused_computation.30 | convolution fusion | flops 2426732544 | bytes 9043972 | tf_op jit(solution)/shard_map/dot_general | solution.py:116
  220.0 5.4 %fusion.22 = bf16[1536,384]{1,0:T(8,128)(2,1)S(1)} fusion(bf16[1,4,128,1536]{3,2,1,0:T(8,128)(2,1)} %bitcast.11, bf16[1,4,128,1536]{3,2,1,0:T(8,128)(2,1)S(1)} %maximum_bitcast_fusion, bf16[1,4,128,1536]{3,2,1,0:T(8,128)(2,1)} %bitcast.9, bf16[1,4,128,1536]{3,2,1,0:T(8,128)(2,1)S(1)} %bitcast.69, s32[]{:T(128)S(6)} %select_n.78, ...), kind=kOutput, calls=%fused_computation.29 | convolution fusion | flops 2426732544 | bytes 9043972 | tf_op jit(solution)/shard_map/dot_general | solution.py:112
  225.4 1.6 pad_maximum_fusion
  227.0 43.8 %all-gather.5.cloned.1.call-done = bf16[2048,3072]{1,0:T(8,128)(2,1)} async-done(((bf16[128,3072]{1,0:T(8,128)(2,1)}), bf16[2048,3072]{1,0:T(8,128)(2,1)}) %all-gather.5.cloned.1.call-update) | async-done | bytes 12582928 | tf_op jit(solution)/shard_map/all_gather | solution.py:107
  270.9 10.4 %convolution_convert_fusion.2 = bf16[2048,384]{1,0:T(8,128)(2,1)S(1)} fusion(bf16[2048,3072]{1,0:T(8,128)(2,1)} %all-gather.5.cloned.1.call-done, bf16[384,3072]{1,0:T(8,128)(2,1)} %param.8), kind=kOutput, calls=%fused_computation.31 | convolution fusion | flops 4832624640 | bytes 16515072 | tf_op jit(solution)/shard_map/dot_general | solution.py:122
  281.3 0.9 collective-permute-start.16
  282.3 1.9 collective-permute-done.16
  284.2 1.3 fusion.47
  285.6 1.3 collective-permute-start.17
  286.9 2.4 collective-permute-start.18
  289.3 1.2 collective-permute-start.19
  290.5 9.7 %convolution_convert_fusion.1 = bf16[384,3072]{1,0:T(8,128)(2,1)} fusion(bf16[2048,384]{1,0:T(8,128)(2,1)} %bitcast.30, bf16[2048,3072]{1,0:T(8,128)(2,1)} %all-gather.5.cloned.1.call-done), kind=kOutput, calls=%fused_computation.17 | convolution fusion | flops 4833017856 | bytes 16515072 | tf_op jit(solution)/shard_map/dot_general | solution.py:126
  300.2 1.8 fusion.42
  (51 shorter events, 7.8 us)
Async XLA Ops:
  7.2 30.5 %copy-start = (bf16[3072,384]{1,0:T(8,128)(2,1)S(1)}, bf16[3072,384]{1,0:T(8,128)(2,1)}, u32[]{:S(2)}) copy-start(bf16[3072,384]{1,0:T(8,128)(2,1)} %param.9) | copy-start | bytes 7077892
  7.2 30.5 %all-gather.3.cloned.1.call-start = ((), (), s32[]{:S(2)}) async-start(), calls=%async_computation.2 | async-start | bytes 1769472 | tf_op jit(solution)/shard_map/all_gather | solution.py:93
  7.9 159.6 %reduce-scatter.2.cloned.1.call-start = ((), (), s32[]{:S(2)}) async-start(), calls=%async_computation.3 | async-start | bytes 13369344 | tf_op jit(solution)/shard_map/reduce_scatter | solution.py:103
  9.5 13.5 %collective-permute-start.5 = (bf16[128,1536]{1,0:T(8,128)(2,1)S(1)}, bf16[128,1536]{1,0:T(8,128)(2,1)S(1)}, u32[]{:S(2)}, u32[]{:S(2)}) collective-permute-start(bf16[128,1536]{1,0:T(8,128)(2,1)S(1)} %get-tuple-element.32), channel_id=1, source_target_pairs={{0,32},{8,40},{16,48},{24,56},{32,64},{40,72},{48,80},{56,88},{64,... | collective-permute-start | bytes 1179656 | tf_op jit(solution)/shard_map/ppermute | solution.py:51
  12.1 11.0 %collective-permute-start.4 = (bf16[128,1536]{1,0:T(8,128)(2,1)S(1)}, bf16[128,1536]{1,0:T(8,128)(2,1)S(1)}, u32[]{:S(2)}, u32[]{:S(2)}) collective-permute-start(bf16[128,1536]{1,0:T(8,128)(2,1)S(1)} %get-tuple-element.32), channel_id=1, source_target_pairs={{0,96},{8,104},{16,112},{24,120},{32,0},{40,8},{48,16},{56,24},{64... | collective-permute-start | bytes 1179656 | tf_op jit(solution)/shard_map/ppermute | solution.py:52
  14.3 11.6 %collective-permute-start.1 = (bf16[128,1536]{1,0:T(8,128)(2,1)S(1)}, bf16[128,1536]{1,0:T(8,128)(2,1)S(1)}, u32[]{:S(2)}, u32[]{:S(2)}) collective-permute-start(bf16[128,1536]{1,0:T(8,128)(2,1)S(1)} %get-tuple-element.33), channel_id=1, source_target_pairs={{0,8},{8,16},{16,24},{24,0},{32,40},{40,48},{48,56},{56,32},{64,72... | collective-permute-start | bytes 1179656 | tf_op jit(solution)/shard_map/ppermute | solution.py:51
  15.5 11.7 %collective-permute-start = (bf16[128,1536]{1,0:T(8,128)(2,1)S(1)}, bf16[128,1536]{1,0:T(8,128)(2,1)S(1)}, u32[]{:S(2)}, u32[]{:S(2)}) collective-permute-start(bf16[128,1536]{1,0:T(8,128)(2,1)S(1)} %get-tuple-element.33), channel_id=1, source_target_pairs={{0,24},{8,0},{16,8},{24,16},{32,56},{40,32},{48,40},{56,48},{64,88... | collective-permute-start | bytes 1179656 | tf_op jit(solution)/shard_map/ppermute | solution.py:52
  23.0 6.5 %collective-permute-start.6 = (bf16[64,1536]{1,0:T(8,128)(2,1)S(1)}, bf16[64,1536]{1,0:T(8,128)(2,1)S(1)}, u32[]{:S(2)}, u32[]{:S(2)}) collective-permute-start(bf16[64,1536]{1,0:T(8,128)(2,1)S(1)} %slice.44), channel_id=1, source_target_pairs={{0,32},{8,40},{16,48},{24,56},{32,64},{40,72},{48,80},{56,88},{64,... | collective-permute-start | bytes 589832 | tf_op jit(solution)/shard_map/ppermute | solution.py:57
  23.1 6.4 %collective-permute-start.7 = (bf16[64,1536]{1,0:T(8,128)(2,1)S(1)}, bf16[64,1536]{1,0:T(8,128)(2,1)S(1)}, u32[]{:S(2)}, u32[]{:S(2)}) collective-permute-start(bf16[64,1536]{1,0:T(8,128)(2,1)S(1)} %slice.45), channel_id=1, source_target_pairs={{0,96},{8,104},{16,112},{24,120},{32,0},{40,8},{48,16},{56,24},{64... | collective-permute-start | bytes 589832 | tf_op jit(solution)/shard_map/ppermute | solution.py:57
  25.9 6.0 %collective-permute-start.2 = (bf16[64,1536]{1,0:T(8,128)(2,1)S(1)}, bf16[64,1536]{1,0:T(8,128)(2,1)S(1)}, u32[]{:S(2)}, u32[]{:S(2)}) collective-permute-start(bf16[64,1536]{1,0:T(8,128)(2,1)S(1)} %slice.41), channel_id=1, source_target_pairs={{0,8},{8,16},{16,24},{24,0},{32,40},{40,48},{48,56},{56,32},{64,72... | collective-permute-start | bytes 589832 | tf_op jit(solution)/shard_map/ppermute | solution.py:57
  27.2 4.7 %collective-permute-start.3 = (bf16[64,1536]{1,0:T(8,128)(2,1)S(1)}, bf16[64,1536]{1,0:T(8,128)(2,1)S(1)}, u32[]{:S(2)}, u32[]{:S(2)}) collective-permute-start(bf16[64,1536]{1,0:T(8,128)(2,1)S(1)} %slice.42), channel_id=1, source_target_pairs={{0,24},{8,0},{16,8},{24,16},{32,56},{40,32},{48,40},{56,48},{64,88... | collective-permute-start | bytes 589832 | tf_op jit(solution)/shard_map/ppermute | solution.py:57
  48.8 2.9 copy-start.4
  48.8 118.6 %copy-start.3 = (bf16[128,3072]{1,0:T(8,128)(2,1)S(1)}, bf16[128,3072]{1,0:T(8,128)(2,1)}, u32[]{:S(2)}) copy-start(bf16[128,3072]{1,0:T(8,128)(2,1)} %param.7) | copy-start | bytes 2359300
  48.9 121.4 %copy-start.2 = (bf16[256,384]{1,0:T(8,128)(2,1)S(1)}, bf16[256,384]{1,0:T(8,128)(2,1)}, u32[]{:S(2)}) copy-start(bf16[256,384]{1,0:T(8,128)(2,1)} %param.5) | copy-start | bytes 589828
  48.9 222.0 %all-gather.5.cloned.1.call-start = ((), (), s32[]{:S(2)}) async-start(), calls=%async_computation.4 | async-start | bytes 13369344 | tf_op jit(solution)/shard_map/all_gather | solution.py:107
  48.9 61.8 %collective-permute-start.10 = (bf16[4,128,1536]{2,1,0:T(8,128)(2,1)}, bf16[4,128,1536]{2,1,0:T(8,128)(2,1)}, u32[]{:S(2)}, u32[]{:S(2)}) collective-permute-start(bf16[4,128,1536]{2,1,0:T(8,128)(2,1)} %pad_maximum_fusion.1), channel_id=1, source_target_pairs={{0,32},{8,40},{16,48},{24,56},{32,64},{40,72},{48,80},{56,88},{64,... | collective-permute-start | bytes 4718600 | tf_op jit(solution)/shard_map/ppermute | solution.py:51
  50.2 62.3 %collective-permute-start.11 = (bf16[4,128,1536]{2,1,0:T(8,128)(2,1)}, bf16[4,128,1536]{2,1,0:T(8,128)(2,1)}, u32[]{:S(2)}, u32[]{:S(2)}) collective-permute-start(bf16[4,128,1536]{2,1,0:T(8,128)(2,1)} %pad_maximum_fusion.1), channel_id=1, source_target_pairs={{0,96},{8,104},{16,112},{24,120},{32,0},{40,8},{48,16},{56,24},{64... | collective-permute-start | bytes 4718600 | tf_op jit(solution)/shard_map/ppermute | solution.py:52
  51.8 115.7 %collective-permute-start.8 = (bf16[4,128,1536]{2,1,0:T(8,128)(2,1)S(1)}, bf16[4,128,1536]{2,1,0:T(8,128)(2,1)}, u32[]{:S(2)}, u32[]{:S(2)}) collective-permute-start(bf16[4,128,1536]{2,1,0:T(8,128)(2,1)S(1)} %copy-done.4), channel_id=1, source_target_pairs={{0,8},{8,16},{16,24},{24,0},{32,40},{40,48},{48,56},{56,32},{64,72... | collective-permute-start | bytes 4718600 | tf_op jit(solution)/shard_map/ppermute | solution.py:51
  52.9 114.6 %collective-permute-start.9 = (bf16[4,128,1536]{2,1,0:T(8,128)(2,1)S(1)}, bf16[4,128,1536]{2,1,0:T(8,128)(2,1)}, u32[]{:S(2)}, u32[]{:S(2)}) collective-permute-start(bf16[4,128,1536]{2,1,0:T(8,128)(2,1)S(1)} %copy-done.4), channel_id=1, source_target_pairs={{0,24},{8,0},{16,8},{24,16},{32,56},{40,32},{48,40},{56,48},{64,88... | collective-permute-start | bytes 4718600 | tf_op jit(solution)/shard_map/ppermute | solution.py:52
  172.9 26.6 %collective-permute-start.12 = (bf16[2,128,1536]{2,1,0:T(8,128)(2,1)S(1)}, bf16[2,128,1536]{2,1,0:T(8,128)(2,1)}, u32[]{:S(2)}, u32[]{:S(2)}) collective-permute-start(bf16[2,128,1536]{2,1,0:T(8,128)(2,1)S(1)} %slice.36), channel_id=1, source_target_pairs={{0,32},{8,40},{16,48},{24,56},{32,64},{40,72},{48,80},{56,88},{64,... | collective-permute-start | bytes 2359304 | tf_op jit(solution)/shard_map/ppermute | solution.py:57
  175.0 30.3 %collective-permute-start.13 = (bf16[2,128,1536]{2,1,0:T(8,128)(2,1)}, bf16[2,128,1536]{2,1,0:T(8,128)(2,1)}, u32[]{:S(2)}, u32[]{:S(2)}) collective-permute-start(bf16[2,128,1536]{2,1,0:T(8,128)(2,1)} %slice.37), channel_id=1, source_target_pairs={{0,96},{8,104},{16,112},{24,120},{32,0},{40,8},{48,16},{56,24},{64... | collective-permute-start | bytes 2359304 | tf_op jit(solution)/shard_map/ppermute | solution.py:57
  181.2 31.7 %collective-permute-start.14 = (bf16[2,128,1536]{2,1,0:T(8,128)(2,1)}, bf16[2,128,1536]{2,1,0:T(8,128)(2,1)}, u32[]{:S(2)}, u32[]{:S(2)}) collective-permute-start(bf16[2,128,1536]{2,1,0:T(8,128)(2,1)} %slice.38), channel_id=1, source_target_pairs={{0,8},{8,16},{16,24},{24,0},{32,40},{40,48},{48,56},{56,32},{64,72... | collective-permute-start | bytes 2359304 | tf_op jit(solution)/shard_map/ppermute | solution.py:57
  183.4 29.5 %collective-permute-start.15 = (bf16[2,128,1536]{2,1,0:T(8,128)(2,1)}, bf16[2,128,1536]{2,1,0:T(8,128)(2,1)}, u32[]{:S(2)}, u32[]{:S(2)}) collective-permute-start(bf16[2,128,1536]{2,1,0:T(8,128)(2,1)} %slice.39), channel_id=1, source_target_pairs={{0,24},{8,0},{16,8},{24,16},{32,56},{40,32},{48,40},{56,48},{64,88... | collective-permute-start | bytes 2359304 | tf_op jit(solution)/shard_map/ppermute | solution.py:57
  188.8 101.6 %all-to-all-start = ((bf16[8,256,384]{2,1,0:T(8,128)(2,1)}), bf16[8,256,384]{2,1,0:T(8,128)(2,1)}, u32[]{:S(2)}, u32[]{:S(2)}) async-start(bf16[8,256,384]{2,1,0:T(8,128)(2,1)} %bitcast.29), calls=%async_computation.1 | async-start | bytes 3145728 | tf_op jit(solution)/shard_map/all_to_all | solution.py:16
  214.4 5.5 %copy-start.5 = (bf16[4,128,1536]{2,1,0:T(8,128)(2,1)S(1)}, bf16[4,128,1536]{2,1,0:T(8,128)(2,1)}, u32[]{:S(2)}) copy-start(bf16[4,128,1536]{2,1,0:T(8,128)(2,1)} %pad_maximum_fusion.1) | copy-start | bytes 4718596
  281.3 2.8 collective-permute-start.16
  285.6 14.6 %collective-permute-start.17 = (bf16[256,384]{1,0:T(8,128)(2,1)S(1)}, bf16[256,384]{1,0:T(8,128)(2,1)S(1)}, u32[]{:S(2)}, u32[]{:S(2)}) collective-permute-start(bf16[256,384]{1,0:T(8,128)(2,1)S(1)} %get-tuple-element.27), channel_id=1, source_target_pairs={{0,2},{1,3},{2,4},{3,5},{4,6},{5,7},{6,0},{7,1},{8,10},{9,11},{10,... | collective-permute-start | bytes 589832 | tf_op jit(solution)/shard_map/ppermute | solution.py:83
  286.9 13.3 %collective-permute-start.18 = (bf16[256,384]{1,0:T(8,128)(2,1)S(1)}, bf16[256,384]{1,0:T(8,128)(2,1)S(1)}, u32[]{:S(2)}, u32[]{:S(2)}) collective-permute-start(bf16[256,384]{1,0:T(8,128)(2,1)S(1)} %get-tuple-element.29), channel_id=1, source_target_pairs={{0,4},{1,5},{2,6},{3,7},{4,0},{5,1},{6,2},{7,3},{8,12},{9,13},{10,... | collective-permute-start | bytes 589832 | tf_op jit(solution)/shard_map/ppermute | solution.py:83
  289.3 10.9 %collective-permute-start.19 = (bf16[256,384]{1,0:T(8,128)(2,1)S(1)}, bf16[256,384]{1,0:T(8,128)(2,1)S(1)}, u32[]{:S(2)}, u32[]{:S(2)}) collective-permute-start(bf16[256,384]{1,0:T(8,128)(2,1)S(1)} %get-tuple-element.28), channel_id=1, source_target_pairs={{0,6},{1,7},{2,0},{3,1},{4,2},{5,3},{6,4},{7,5},{8,14},{9,15},{10,... | collective-permute-start | bytes 589832 | tf_op jit(solution)/shard_map/ppermute | solution.py:83
  290.5 11.5 %copy-start.1 = (bf16[3072,384]{1,0:T(8,128)(2,1)S(1)}, bf16[3072,384]{1,0:T(8,128)(2,1)}, u32[]{:S(2)}) copy-start(bf16[3072,384]{1,0:T(8,128)(2,1)} %param.9) | copy-start | bytes 7077892
Sparse Core Ops, SparseCore 0:
  9.7 27.9 all-gather.2
  49.0 118.4 reduce-scatter.1
  170.4 100.4 all-gather.4

commit v10 on v9

--- a/solution.py
+++ b/solution.py
@@ -102,7 +102,8 @@
     ).astype(jnp.bfloat16)
     total = lax.psum_scatter(partial, "row", scatter_dimension=0, tiled=True)
     hid_a, total = ring_gather(a1, fz, bz, total)
-    hid_b, total = ring_gather(b1, fx, bx, total)
+    b1, total = lax.optimization_barrier((b1, total))
+    hid_b, _ = ring_gather(b1, fx, bx)
     pre_grad_loc = (total.astype(jnp.float32) * slope).astype(jnp.bfloat16)
     pre_grad = lax.all_gather(pre_grad_loc, "row", axis=0, tiled=True)
     me = lax.axis_index("row")

time: 309 us -> 325 us (1.052)
  waiting for transfers between devices: 186 us -> 205 us
    ppermute x4, waiting for transfers between devices: 11.3 us -> 41.3 us  [ring_gather(): lax.ppermute(from_prev[:h], 'row', fwd)]
    all_gather x1, waiting for transfers between devices: 43.8 us -> 23.6 us  [on_device(): pre_grad = lax.all_gather(pre_grad_loc, 'row', axis=0, tiled=True)]
    ppermute x4, waiting for transfers between devices: 62.3 us -> 72.9 us  [ring_gather(): from_prev = lax.ppermute(x, 'row', fwd)]
  transfers between devices with their start and end apart: 24 -> 24, of which waited for: 12 -> 13; matrix products, arithmetic and copies ran while one was open for 18% -> 16% of each run, Pallas kernels for 0% -> 0%
where the time goes in v10:
time: 325 us
  waiting for transfers between devices  205 us (63%)
  matrix products  42 us (13%)
  starting transfers between devices  36.8 us (11%)
  other arithmetic  15.4 us (5%)
  between operations  14 us (4%)
  local copies, waits for them, and re-layouts  11.6 us (4%)
    ppermute x4, waiting for transfers between devices, ring_gather(): from_prev = lax.ppermute(x, 'row', fwd)  72.9 us
    reduce_scatter x1, waiting for transfers between devices, on_device(): total = lax.psum_scatter(partial, 'row', scatter_dimension=0, tiled=True)  53.5 us
    ppermute x4, waiting for transfers between devices, ring_gather(): lax.ppermute(from_prev[:h], 'row', fwd)  41.3 us
    all_gather x1, waiting for transfers between devices, on_device(): pre_grad = lax.all_gather(pre_grad_loc, 'row', axis=0, tiled=True)  23.6 us
    dot_general x1, matrix products, on_device(): lax.dot_general(grad_all, w_out, (((1,), (1,)), ((), ())), preferred_elem...  11.2 us
    dot_general x1, matrix products, on_device(): lax.dot_general(pre_grad, w_in, (((1,), (1,)), ((), ())), preferred_eleme...  10.4 us
    dot_general x1, matrix products, on_device(): lax.dot_general(inputs_all, pre_grad, (((0,), (0,)), ((), ())), preferred...  9.68 us
    ppermute x4, starting transfers between devices, ring_gather(): lax.ppermute(from_next[h:], 'row', bwd)  9.64 us
  transfers between devices with their start and end apart: 24, of which 13 were waited for; matrix products, arithmetic and copies ran while one was open for 16% of the time, Pallas kernels for 0%

profile of v10, /device:TPU:1, one launch (start us, length us, event | category | flops | bytes accessed | tf_op | source)
XLA Modules:
  0.0 324.8 jit_solution(17741300733545355622)
XLA Ops:
  8.0 1.5 fusion.31
  9.5 2.5 collective-permute-start.5
  12.1 2.2 collective-permute-start.4
  14.3 1.2 collective-permute-start.1
  15.5 1.5 collective-permute-start
  16.9 6.1 %collective-permute-done.5 = bf16[128,1536]{1,0:T(8,128)(2,1)S(1)} collective-permute-done((bf16[128,1536]{1,0:T(8,128)(2,1)S(1)}, bf16[128,1536]{1,0:T(8,128)(2,1)S(1)}, u32[]{:S(2)}, u32[]{:S(2)}) %collective-permute-start.5) | collective-permute-done | bytes 393248 | tf_op jit(solution)/shard_map/ppermute | solution.py:51
  23.1 2.7 collective-permute-start.7
  25.9 1.3 collective-permute-start.2
  27.2 1.5 collective-permute-start.3
  28.7 0.8 collective-permute-done.6
  29.6 2.3 collective-permute-done.2
  31.9 1.3 pad_maximum_fusion.2
  33.3 1.3 pad_maximum_fusion.1
  34.6 3.1 all-gather.3.cloned.1.call-done
  37.7 11.2 %convolution_convert_fusion = bf16[2048,3072]{1,0:T(8,128)(2,1)} fusion(bf16[2048,384]{1,0:T(8,128)(2,1)} %all-gather.3.cloned.1.call-done, bf16[3072,384]{1,0:T(8,128)(2,1)S(1)} %copy-done), kind=kOutput, calls=%fused_computation | convolution fusion | flops 4838129664 | bytes 16515072 | tf_op jit(solution)/shard_map/dot_general | solution.py:100
  48.9 1.2 collective-permute-start.8
  50.2 1.6 collective-permute-start.9
  51.8 59.0 %collective-permute-done.8 = bf16[4,128,1536]{2,1,0:T(8,128)(2,1)} collective-permute-done((bf16[4,128,1536]{2,1,0:T(8,128)(2,1)}, bf16[4,128,1536]{2,1,0:T(8,128)(2,1)}, u32[]{:S(2)}, u32[]{:S(2)}) %collective-permute-start.8) | collective-permute-done | bytes 1572896 | tf_op jit(solution)/shard_map/ppermute | solution.py:51
  110.7 1.8 collective-permute-done.9
  112.5 53.5 %reduce-scatter.2.cloned.1.call-done = bf16[128,3072]{1,0:T(8,128)(2,1)} async-done(((bf16[2048,3072]{1,0:T(8,128)(2,1)}), bf16[128,3072]{1,0:T(8,128)(2,1)}) %reduce-scatter.2.cloned.1.call-update) | async-done | bytes 786448 | tf_op jit(solution)/shard_map/reduce_scatter | solution.py:103
  166.1 2.8 fusion.36
  169.0 2.7 collective-permute-start.12
  173.0 1.2 slice.36
  174.3 2.1 slice.37
  176.3 2.7 collective-permute-start.11
  183.2 6.6 %all-to-all-start = ((bf16[8,256,384]{2,1,0:T(8,128)(2,1)}), bf16[8,256,384]{2,1,0:T(8,128)(2,1)}, u32[]{:S(2)}, u32[]{:S(2)}) async-start(bf16[8,256,384]{2,1,0:T(8,128)(2,1)} %bitcast.29), calls=%async_computation.1 | async-start | bytes 3145728 | tf_op jit(solution)/shard_map/all_to_all | solution.py:16
  189.8 2.1 fusion.38
  191.9 10.4 %collective-permute-done.10 = bf16[2,128,1536]{2,1,0:T(8,128)(2,1)} collective-permute-done((bf16[2,128,1536]{2,1,0:T(8,128)(2,1)S(1)}, bf16[2,128,1536]{2,1,0:T(8,128)(2,1)}, u32[]{:S(2)}, u32[]{:S(2)}) %collective-permute-start.10) | collective-permute-done | bytes 786464 | tf_op jit(solution)/shard_map/ppermute | solution.py:57
  202.3 5.9 %collective-permute-done.11 = bf16[2,128,1536]{2,1,0:T(8,128)(2,1)} collective-permute-done((bf16[2,128,1536]{2,1,0:T(8,128)(2,1)}, bf16[2,128,1536]{2,1,0:T(8,128)(2,1)}, u32[]{:S(2)}, u32[]{:S(2)}) %collective-permute-start.11) | collective-permute-done | bytes 786464 | tf_op jit(solution)/shard_map/ppermute | solution.py:57
  208.2 1.5 maximum_bitcast_fusion
  209.8 7.9 %collective-permute-done.13 = bf16[4,128,1536]{2,1,0:T(8,128)(2,1)} collective-permute-done((bf16[4,128,1536]{2,1,0:T(8,128)(2,1)S(1)}, bf16[4,128,1536]{2,1,0:T(8,128)(2,1)}, u32[]{:S(2)}, u32[]{:S(2)}) %collective-permute-start.13) | collective-permute-done | bytes 1572896 | tf_op jit(solution)/shard_map/ppermute | solution.py:51
  217.6 1.3 slice.46
  219.0 1.2 slice.47
  220.2 2.7 collective-permute-start.15
  222.9 5.4 %fusion.22 = bf16[1536,384]{1,0:T(8,128)(2,1)S(1)} fusion(bf16[1,4,128,1536]{3,2,1,0:T(8,128)(2,1)} %bitcast.11, bf16[1,4,128,1536]{3,2,1,0:T(8,128)(2,1)S(1)} %maximum_bitcast_fusion, bf16[1,4,128,1536]{3,2,1,0:T(8,128)(2,1)} %bitcast.9, bf16[1,4,128,1536]{3,2,1,0:T(8,128)(2,1)S(1)} %bitcast.69, s32[]{:T(128)S(6)} %select_n.78, ...), kind=kOutput, calls=%fused_computation.29 | convolution fusion | flops 2426732544 | bytes 9043972 | tf_op jit(solution)/shard_map/dot_general | solution.py:113
  228.3 27.7 %collective-permute-done.14 = bf16[2,128,1536]{2,1,0:T(8,128)(2,1)S(1)} collective-permute-done((bf16[2,128,1536]{2,1,0:T(8,128)(2,1)S(1)}, bf16[2,128,1536]{2,1,0:T(8,128)(2,1)S(1)}, u32[]{:S(2)}, u32[]{:S(2)}) %collective-permute-start.14) | collective-permute-done | bytes 786464 | tf_op jit(solution)/shard_map/ppermute | solution.py:57
  256.2 5.4 %fusion.25 = bf16[1536,384]{1,0:T(8,128)(2,1)S(1)} fusion(bf16[1,4,128,1536]{3,2,1,0:T(8,128)(2,1)} %bitcast.18, bf16[1,4,128,1536]{3,2,1,0:T(8,128)(2,1)S(1)} %maximum_bitcast_fusion.1, bf16[1,4,128,1536]{3,2,1,0:T(8,128)(2,1)} %bitcast.16, bf16[1,4,128,1536]{3,2,1,0:T(8,128)(2,1)S(1)} %bitcast.68, s32[]{:T(128)S(6)} %select_n.78, ...), kind=kOutput, calls=%fused_computation.30 | convolution fusion | flops 2426732544 | bytes 9043972 | tf_op jit(solution)/shard_map/dot_general | solution.py:117
  261.7 1.6 pad_maximum_fusion
  263.3 23.6 %all-gather.5.cloned.1.call-done = bf16[2048,3072]{1,0:T(8,128)(2,1)} async-done(((bf16[128,3072]{1,0:T(8,128)(2,1)}), bf16[2048,3072]{1,0:T(8,128)(2,1)}) %all-gather.5.cloned.1.call-update) | async-done | bytes 12582928 | tf_op jit(solution)/shard_map/all_gather | solution.py:108
  287.0 10.4 %convolution_convert_fusion.2 = bf16[2048,384]{1,0:T(8,128)(2,1)S(1)} fusion(bf16[2048,3072]{1,0:T(8,128)(2,1)} %all-gather.5.cloned.1.call-done, bf16[384,3072]{1,0:T(8,128)(2,1)} %param.8), kind=kOutput, calls=%fused_computation.31 | convolution fusion | flops 4832624640 | bytes 16515072 | tf_op jit(solution)/shard_map/dot_general | solution.py:123
  297.4 1.1 collective-permute-start.16
  298.6 1.9 collective-permute-done.16
  300.5 1.3 fusion.47
  301.9 1.3 collective-permute-start.17
  303.2 2.4 collective-permute-start.18
  305.6 1.2 collective-permute-start.19
  306.8 9.7 %convolution_convert_fusion.1 = bf16[384,3072]{1,0:T(8,128)(2,1)} fusion(bf16[2048,384]{1,0:T(8,128)(2,1)} %bitcast.30, bf16[2048,3072]{1,0:T(8,128)(2,1)} %all-gather.5.cloned.1.call-done), kind=kOutput, calls=%fused_computation.17 | convolution fusion | flops 4833017856 | bytes 16515072 | tf_op jit(solution)/shard_map/dot_general | solution.py:127
  316.5 1.8 fusion.42
  (51 shorter events, 7.3 us)
Async XLA Ops:
  7.2 30.5 %copy-start = (bf16[3072,384]{1,0:T(8,128)(2,1)S(1)}, bf16[3072,384]{1,0:T(8,128)(2,1)}, u32[]{:S(2)}) copy-start(bf16[3072,384]{1,0:T(8,128)(2,1)} %param.9) | copy-start | bytes 7077892
  7.2 30.5 %all-gather.3.cloned.1.call-start = ((), (), s32[]{:S(2)}) async-start(), calls=%async_computation.2 | async-start | bytes 1769472 | tf_op jit(solution)/shard_map/all_gather | solution.py:93
  7.9 158.2 %reduce-scatter.2.cloned.1.call-start = ((), (), s32[]{:S(2)}) async-start(), calls=%async_computation.3 | async-start | bytes 13369344 | tf_op jit(solution)/shard_map/reduce_scatter | solution.py:103
  9.5 13.5 %collective-permute-start.5 = (bf16[128,1536]{1,0:T(8,128)(2,1)S(1)}, bf16[128,1536]{1,0:T(8,128)(2,1)S(1)}, u32[]{:S(2)}, u32[]{:S(2)}) collective-permute-start(bf16[128,1536]{1,0:T(8,128)(2,1)S(1)} %get-tuple-element.30), channel_id=1, source_target_pairs={{0,32},{8,40},{16,48},{24,56},{32,64},{40,72},{48,80},{56,88},{64,... | collective-permute-start | bytes 1179656 | tf_op jit(solution)/shard_map/ppermute | solution.py:51
  12.1 11.0 %collective-permute-start.4 = (bf16[128,1536]{1,0:T(8,128)(2,1)S(1)}, bf16[128,1536]{1,0:T(8,128)(2,1)S(1)}, u32[]{:S(2)}, u32[]{:S(2)}) collective-permute-start(bf16[128,1536]{1,0:T(8,128)(2,1)S(1)} %get-tuple-element.30), channel_id=1, source_target_pairs={{0,96},{8,104},{16,112},{24,120},{32,0},{40,8},{48,16},{56,24},{64... | collective-permute-start | bytes 1179656 | tf_op jit(solution)/shard_map/ppermute | solution.py:52
  14.3 11.6 %collective-permute-start.1 = (bf16[128,1536]{1,0:T(8,128)(2,1)S(1)}, bf16[128,1536]{1,0:T(8,128)(2,1)S(1)}, u32[]{:S(2)}, u32[]{:S(2)}) collective-permute-start(bf16[128,1536]{1,0:T(8,128)(2,1)S(1)} %get-tuple-element.31), channel_id=1, source_target_pairs={{0,8},{8,16},{16,24},{24,0},{32,40},{40,48},{48,56},{56,32},{64,72... | collective-permute-start | bytes 1179656 | tf_op jit(solution)/shard_map/ppermute | solution.py:51
  15.5 11.7 %collective-permute-start = (bf16[128,1536]{1,0:T(8,128)(2,1)S(1)}, bf16[128,1536]{1,0:T(8,128)(2,1)S(1)}, u32[]{:S(2)}, u32[]{:S(2)}) collective-permute-start(bf16[128,1536]{1,0:T(8,128)(2,1)S(1)} %get-tuple-element.31), channel_id=1, source_target_pairs={{0,24},{8,0},{16,8},{24,16},{32,56},{40,32},{48,40},{56,48},{64,88... | collective-permute-start | bytes 1179656 | tf_op jit(solution)/shard_map/ppermute | solution.py:52
  23.0 6.5 %collective-permute-start.6 = (bf16[64,1536]{1,0:T(8,128)(2,1)S(1)}, bf16[64,1536]{1,0:T(8,128)(2,1)S(1)}, u32[]{:S(2)}, u32[]{:S(2)}) collective-permute-start(bf16[64,1536]{1,0:T(8,128)(2,1)S(1)} %slice.44), channel_id=1, source_target_pairs={{0,32},{8,40},{16,48},{24,56},{32,64},{40,72},{48,80},{56,88},{64,... | collective-permute-start | bytes 589832 | tf_op jit(solution)/shard_map/ppermute | solution.py:57
  23.1 6.4 %collective-permute-start.7 = (bf16[64,1536]{1,0:T(8,128)(2,1)S(1)}, bf16[64,1536]{1,0:T(8,128)(2,1)S(1)}, u32[]{:S(2)}, u32[]{:S(2)}) collective-permute-start(bf16[64,1536]{1,0:T(8,128)(2,1)S(1)} %slice.45), channel_id=1, source_target_pairs={{0,96},{8,104},{16,112},{24,120},{32,0},{40,8},{48,16},{56,24},{64... | collective-permute-start | bytes 589832 | tf_op jit(solution)/shard_map/ppermute | solution.py:57
  25.9 6.0 %collective-permute-start.2 = (bf16[64,1536]{1,0:T(8,128)(2,1)S(1)}, bf16[64,1536]{1,0:T(8,128)(2,1)S(1)}, u32[]{:S(2)}, u32[]{:S(2)}) collective-permute-start(bf16[64,1536]{1,0:T(8,128)(2,1)S(1)} %slice.41), channel_id=1, source_target_pairs={{0,8},{8,16},{16,24},{24,0},{32,40},{40,48},{48,56},{56,32},{64,72... | collective-permute-start | bytes 589832 | tf_op jit(solution)/shard_map/ppermute | solution.py:57
  27.2 4.7 %collective-permute-start.3 = (bf16[64,1536]{1,0:T(8,128)(2,1)S(1)}, bf16[64,1536]{1,0:T(8,128)(2,1)S(1)}, u32[]{:S(2)}, u32[]{:S(2)}) collective-permute-start(bf16[64,1536]{1,0:T(8,128)(2,1)S(1)} %slice.42), channel_id=1, source_target_pairs={{0,24},{8,0},{16,8},{24,16},{32,56},{40,32},{48,40},{56,48},{64,88... | collective-permute-start | bytes 589832 | tf_op jit(solution)/shard_map/ppermute | solution.py:57
  48.8 117.2 %copy-start.3 = (bf16[128,3072]{1,0:T(8,128)(2,1)S(1)}, bf16[128,3072]{1,0:T(8,128)(2,1)}, u32[]{:S(2)}) copy-start(bf16[128,3072]{1,0:T(8,128)(2,1)} %param.7) | copy-start | bytes 2359300
  48.9 120.0 %copy-start.4 = (bf16[4,128,1536]{2,1,0:T(8,128)(2,1)S(1)}, bf16[4,128,1536]{2,1,0:T(8,128)(2,1)}, u32[]{:S(2)}) copy-start(bf16[4,128,1536]{2,1,0:T(8,128)(2,1)} %pad_maximum_fusion.2) | copy-start | bytes 4718596
  48.9 122.7 %copy-start.2 = (bf16[256,384]{1,0:T(8,128)(2,1)S(1)}, bf16[256,384]{1,0:T(8,128)(2,1)}, u32[]{:S(2)}) copy-start(bf16[256,384]{1,0:T(8,128)(2,1)} %param.5) | copy-start | bytes 589828
  48.9 238.1 %all-gather.5.cloned.1.call-start = ((), (), s32[]{:S(2)}) async-start(), calls=%async_computation.4 | async-start | bytes 13369344 | tf_op jit(solution)/shard_map/all_gather | solution.py:108
  48.9 61.8 %collective-permute-start.8 = (bf16[4,128,1536]{2,1,0:T(8,128)(2,1)}, bf16[4,128,1536]{2,1,0:T(8,128)(2,1)}, u32[]{:S(2)}, u32[]{:S(2)}) collective-permute-start(bf16[4,128,1536]{2,1,0:T(8,128)(2,1)} %pad_maximum_fusion.1), channel_id=1, source_target_pairs={{0,32},{8,40},{16,48},{24,56},{32,64},{40,72},{48,80},{56,88},{64,... | collective-permute-start | bytes 4718600 | tf_op jit(solution)/shard_map/ppermute | solution.py:51
  50.2 62.4 %collective-permute-start.9 = (bf16[4,128,1536]{2,1,0:T(8,128)(2,1)}, bf16[4,128,1536]{2,1,0:T(8,128)(2,1)}, u32[]{:S(2)}, u32[]{:S(2)}) collective-permute-start(bf16[4,128,1536]{2,1,0:T(8,128)(2,1)} %pad_maximum_fusion.1), channel_id=1, source_target_pairs={{0,96},{8,104},{16,112},{24,120},{32,0},{40,8},{48,16},{56,24},{64... | collective-permute-start | bytes 4718600 | tf_op jit(solution)/shard_map/ppermute | solution.py:52
  168.9 48.8 %collective-permute-start.13 = (bf16[4,128,1536]{2,1,0:T(8,128)(2,1)S(1)}, bf16[4,128,1536]{2,1,0:T(8,128)(2,1)}, u32[]{:S(2)}, u32[]{:S(2)}) collective-permute-start(bf16[4,128,1536]{2,1,0:T(8,128)(2,1)S(1)} %copy-done.4), channel_id=1, source_target_pairs={{0,8},{8,16},{16,24},{24,0},{32,40},{40,48},{48,56},{56,32},{64,72... | collective-permute-start | bytes 4718600 | tf_op jit(solution)/shard_map/ppermute | solution.py:51
  169.0 50.1 %collective-permute-start.12 = (bf16[4,128,1536]{2,1,0:T(8,128)(2,1)S(1)}, bf16[4,128,1536]{2,1,0:T(8,128)(2,1)}, u32[]{:S(2)}, u32[]{:S(2)}) collective-permute-start(bf16[4,128,1536]{2,1,0:T(8,128)(2,1)S(1)} %copy-done.4), channel_id=1, source_target_pairs={{0,24},{8,0},{16,8},{24,16},{32,56},{40,32},{48,40},{56,48},{64,88... | collective-permute-start | bytes 4718600 | tf_op jit(solution)/shard_map/ppermute | solution.py:52
  174.2 28.1 %collective-permute-start.10 = (bf16[2,128,1536]{2,1,0:T(8,128)(2,1)S(1)}, bf16[2,128,1536]{2,1,0:T(8,128)(2,1)}, u32[]{:S(2)}, u32[]{:S(2)}) collective-permute-start(bf16[2,128,1536]{2,1,0:T(8,128)(2,1)S(1)} %slice.36), channel_id=1, source_target_pairs={{0,32},{8,40},{16,48},{24,56},{32,64},{40,72},{48,80},{56,88},{64,... | collective-permute-start | bytes 2359304 | tf_op jit(solution)/shard_map/ppermute | solution.py:57
  176.3 31.9 %collective-permute-start.11 = (bf16[2,128,1536]{2,1,0:T(8,128)(2,1)}, bf16[2,128,1536]{2,1,0:T(8,128)(2,1)}, u32[]{:S(2)}, u32[]{:S(2)}) collective-permute-start(bf16[2,128,1536]{2,1,0:T(8,128)(2,1)} %slice.37), channel_id=1, source_target_pairs={{0,96},{8,104},{16,112},{24,120},{32,0},{40,8},{48,16},{56,24},{64... | collective-permute-start | bytes 2359304 | tf_op jit(solution)/shard_map/ppermute | solution.py:57
  183.2 123.6 %all-to-all-start = ((bf16[8,256,384]{2,1,0:T(8,128)(2,1)}), bf16[8,256,384]{2,1,0:T(8,128)(2,1)}, u32[]{:S(2)}, u32[]{:S(2)}) async-start(bf16[8,256,384]{2,1,0:T(8,128)(2,1)} %bitcast.29), calls=%async_computation.1 | async-start | bytes 3145728 | tf_op jit(solution)/shard_map/all_to_all | solution.py:16
  209.8 13.2 %copy-start.5 = (bf16[4,128,1536]{2,1,0:T(8,128)(2,1)S(1)}, bf16[4,128,1536]{2,1,0:T(8,128)(2,1)}, u32[]{:S(2)}) copy-start(bf16[4,128,1536]{2,1,0:T(8,128)(2,1)} %pad_maximum_fusion.1) | copy-start | bytes 4718596
  218.9 37.2 %collective-permute-start.14 = (bf16[2,128,1536]{2,1,0:T(8,128)(2,1)S(1)}, bf16[2,128,1536]{2,1,0:T(8,128)(2,1)S(1)}, u32[]{:S(2)}, u32[]{:S(2)}) collective-permute-start(bf16[2,128,1536]{2,1,0:T(8,128)(2,1)S(1)} %slice.46), channel_id=1, source_target_pairs={{0,8},{8,16},{16,24},{24,0},{32,40},{40,48},{48,56},{56,32},{64,72... | collective-permute-start | bytes 2359304 | tf_op jit(solution)/shard_map/ppermute | solution.py:57
  220.2 35.9 %collective-permute-start.15 = (bf16[2,128,1536]{2,1,0:T(8,128)(2,1)S(1)}, bf16[2,128,1536]{2,1,0:T(8,128)(2,1)S(1)}, u32[]{:S(2)}, u32[]{:S(2)}) collective-permute-start(bf16[2,128,1536]{2,1,0:T(8,128)(2,1)S(1)} %slice.47), channel_id=1, source_target_pairs={{0,24},{8,0},{16,8},{24,16},{32,56},{40,32},{48,40},{56,48},{64,88... | collective-permute-start | bytes 2359304 | tf_op jit(solution)/shard_map/ppermute | solution.py:57
  297.4 3.1 collective-permute-start.16
  301.9 14.6 %collective-permute-start.17 = (bf16[256,384]{1,0:T(8,128)(2,1)S(1)}, bf16[256,384]{1,0:T(8,128)(2,1)S(1)}, u32[]{:S(2)}, u32[]{:S(2)}) collective-permute-start(bf16[256,384]{1,0:T(8,128)(2,1)S(1)} %get-tuple-element.25), channel_id=1, source_target_pairs={{0,2},{1,3},{2,4},{3,5},{4,6},{5,7},{6,0},{7,1},{8,10},{9,11},{10,... | collective-permute-start | bytes 589832 | tf_op jit(solution)/shard_map/ppermute | solution.py:83
  303.2 13.3 %collective-permute-start.18 = (bf16[256,384]{1,0:T(8,128)(2,1)S(1)}, bf16[256,384]{1,0:T(8,128)(2,1)S(1)}, u32[]{:S(2)}, u32[]{:S(2)}) collective-permute-start(bf16[256,384]{1,0:T(8,128)(2,1)S(1)} %get-tuple-element.27), channel_id=1, source_target_pairs={{0,4},{1,5},{2,6},{3,7},{4,0},{5,1},{6,2},{7,3},{8,12},{9,13},{10,... | collective-permute-start | bytes 589832 | tf_op jit(solution)/shard_map/ppermute | solution.py:83
  305.6 10.8 %collective-permute-start.19 = (bf16[256,384]{1,0:T(8,128)(2,1)S(1)}, bf16[256,384]{1,0:T(8,128)(2,1)S(1)}, u32[]{:S(2)}, u32[]{:S(2)}) collective-permute-start(bf16[256,384]{1,0:T(8,128)(2,1)S(1)} %get-tuple-element.26), channel_id=1, source_target_pairs={{0,6},{1,7},{2,0},{3,1},{4,2},{5,3},{6,4},{7,5},{8,14},{9,15},{10,... | collective-permute-start | bytes 589832 | tf_op jit(solution)/shard_map/ppermute | solution.py:83
  306.8 11.5 %copy-start.1 = (bf16[3072,384]{1,0:T(8,128)(2,1)S(1)}, bf16[3072,384]{1,0:T(8,128)(2,1)}, u32[]{:S(2)}) copy-start(bf16[3072,384]{1,0:T(8,128)(2,1)} %param.9) | copy-start | bytes 7077892
Sparse Core Ops, SparseCore 0:
  9.7 27.9 all-gather.2
  49.0 117.0 reduce-scatter.1
  169.0 117.9 all-gather.4

commit v11 on v9

--- a/solution.py
+++ b/solution.py
@@ -66,15 +66,21 @@
     return perm(0, 1), perm(0, -1), perm(1, 0), perm(-1, 0)
 
 
-def scatter_sum_col(x, n_y):
+def in_grad_col(pre_grad, w_in, n_y):
     n_col = 2 * n_y
     me = lax.axis_index("col")
     k, y = me % 2, me // 2
-    blk = x.shape[0] // n_col
-    x4 = x.reshape((n_y, 2, blk) + x.shape[1:])
-    mine = lax.dynamic_index_in_dim(x4, k, axis=1, keepdims=False)
-    other = lax.dynamic_index_in_dim(x4, 1 - k, axis=1, keepdims=False)
+    blk = pre_grad.shape[0] // n_col
+    p4 = pre_grad.reshape((n_y, 2, blk) + pre_grad.shape[1:])
+
+    def rows_for(core):
+        p = lax.dynamic_index_in_dim(p4, core, axis=1, keepdims=False)
+        return lax.dot_general(p, w_in, (((2,), (1,)), ((), ())),
+                               preferred_element_type=jnp.float32)
+
+    other = rows_for(1 - k).astype(jnp.bfloat16)
     got = lax.ppermute(other, "col", [(c, c ^ 1) for c in range(n_col)])
+    mine = lax.optimization_barrier(rows_for(k).astype(jnp.bfloat16))
     pair = mine.astype(jnp.float32) + got.astype(jnp.float32)
     pair_b = pair.astype(jnp.bfloat16)
     acc = lax.dynamic_index_in_dim(pair, y, axis=0, keepdims=False)
@@ -119,10 +125,7 @@
     )
     w_out_grad = jnp.concatenate([w_out_a, w_out_b], axis=0).astype(jnp.bfloat16)
     pre_grad, w_out_grad = lax.optimization_barrier((pre_grad, w_out_grad))
-    in_part = lax.dot_general(
-        pre_grad, w_in, (((1,), (1,)), ((), ())), preferred_element_type=jnp.float32
-    ).astype(jnp.bfloat16)
-    in_grad = scatter_sum_col(in_part, n_col // 2).astype(jnp.bfloat16)
+    in_grad = in_grad_col(pre_grad, w_in, n_col // 2).astype(jnp.bfloat16)
     w_in_grad = lax.dot_general(
         inputs_all, pre_grad, (((0,), (0,)), ((), ())), preferred_element_type=jnp.float32
     ).astype(jnp.bfloat16)

time: 309 us -> 311 us (level)
  matrix products: 42.1 us -> 45.6 us
    dot_general x1 -> x2, matrix products: 10.4 us -> 13.8 us  [rows_for(): lax.dot_general(p, w_in, (((2,), (1,)), ((), ())), preferred_element_type...]
  transfers between devices with their start and end apart: 24 -> 24, of which waited for: 12 -> 11; matrix products, arithmetic and copies ran while one was open for 18% -> 19% of each run, Pallas kernels for 0% -> 0%
where the time goes in v11:
time: 311 us; the launch traced here: 310 us
  waiting for transfers between devices  184 us (59%)
  matrix products  45.6 us (15%)
  starting transfers between devices  36.5 us (12%)
  other arithmetic  16.8 us (5%)
  between operations  13.9 us (4%)
  local copies, waits for them, and re-layouts  13.4 us (4%)
    ppermute x4, waiting for transfers between devices, ring_gather(): from_prev = lax.ppermute(x, 'row', fwd)  62.3 us
    reduce_scatter x1, waiting for transfers between devices, on_device(): total = lax.psum_scatter(partial, 'row', scatter_dimension=0, tiled=True)  55 us
    all_gather x1, waiting for transfers between devices, on_device(): pre_grad = lax.all_gather(pre_grad_loc, 'row', axis=0, tiled=True)  43.8 us
    dot_general x2, matrix products, rows_for(): lax.dot_general(p, w_in, (((2,), (1,)), ((), ())), preferred_element_type...  13.8 us
    ppermute x4, waiting for transfers between devices, ring_gather(): lax.ppermute(from_prev[:h], 'row', fwd)  11.3 us
    dot_general x1, matrix products, on_device(): lax.dot_general(grad_all, w_out, (((1,), (1,)), ((), ())), preferred_elem...  11.2 us
    dot_general x1, matrix products, on_device(): lax.dot_general(inputs_all, pre_grad, (((0,), (0,)), ((), ())), preferred...  9.68 us
    ppermute x4, starting transfers between devices, ring_gather(): lax.ppermute(from_next[h:], 'row', bwd)  9.57 us
  transfers between devices with their start and end apart: 24, of which 11 were waited for; matrix products, arithmetic and copies ran while one was open for 19% of the time, Pallas kernels for 0%

profile of v11, /device:TPU:1, one launch (start us, length us, event | category | flops | bytes accessed | tf_op | source)
XLA Modules:
  0.0 310.1 jit_solution(849052751061191373)
XLA Ops:
  8.0 1.5 fusion.39
  9.5 2.5 collective-permute-start.5
  12.1 2.2 collective-permute-start.4
  14.3 1.2 collective-permute-start.1
  15.5 1.5 collective-permute-start
  16.9 6.1 %collective-permute-done.5 = bf16[128,1536]{1,0:T(8,128)(2,1)S(1)} collective-permute-done((bf16[128,1536]{1,0:T(8,128)(2,1)S(1)}, bf16[128,1536]{1,0:T(8,128)(2,1)S(1)}, u32[]{:S(2)}, u32[]{:S(2)}) %collective-permute-start.5) | collective-permute-done | bytes 393248 | tf_op jit(solution)/shard_map/ppermute | solution.py:51
  23.1 2.7 collective-permute-start.7
  25.9 1.3 collective-permute-start.2
  27.2 1.5 collective-permute-start.3
  29.6 2.3 collective-permute-done.2
  31.9 1.3 pad_maximum_fusion.2
  33.3 1.3 pad_maximum_fusion.1
  34.6 3.1 all-gather.3.cloned.1.call-done
  37.7 11.2 %convolution_convert_fusion = bf16[2048,3072]{1,0:T(8,128)(2,1)} fusion(bf16[2048,384]{1,0:T(8,128)(2,1)} %all-gather.3.cloned.1.call-done, bf16[3072,384]{1,0:T(8,128)(2,1)S(1)} %copy-done), kind=kOutput, calls=%fused_computation | convolution fusion | flops 4838129664 | bytes 16515072 | tf_op jit(solution)/shard_map/dot_general | solution.py:106
  48.9 1.2 collective-permute-start.10
  50.2 1.6 collective-permute-start.11
  51.8 1.1 collective-permute-start.8
  52.9 1.6 collective-permute-start.9
  54.4 56.3 %collective-permute-done.10 = bf16[4,128,1536]{2,1,0:T(8,128)(2,1)} collective-permute-done((bf16[4,128,1536]{2,1,0:T(8,128)(2,1)}, bf16[4,128,1536]{2,1,0:T(8,128)(2,1)}, u32[]{:S(2)}, u32[]{:S(2)}) %collective-permute-start.10) | collective-permute-done | bytes 1572896 | tf_op jit(solution)/shard_map/ppermute | solution.py:51
  110.7 1.8 collective-permute-done.11
  112.5 55.0 %reduce-scatter.2.cloned.1.call-done = bf16[128,3072]{1,0:T(8,128)(2,1)} async-done(((bf16[2048,3072]{1,0:T(8,128)(2,1)}), bf16[128,3072]{1,0:T(8,128)(2,1)}) %reduce-scatter.2.cloned.1.call-update) | async-done | bytes 786448 | tf_op jit(solution)/shard_map/reduce_scatter | solution.py:109
  167.5 2.8 fusion.44
  171.7 1.2 slice.36
  172.9 2.1 slice.37
  175.0 2.7 collective-permute-start.13
  179.1 2.1 slice.38
  181.2 2.2 slice.39
  183.4 2.7 collective-permute-start.15
  188.8 6.4 %all-to-all-start = ((bf16[8,256,384]{2,1,0:T(8,128)(2,1)}), bf16[8,256,384]{2,1,0:T(8,128)(2,1)}, u32[]{:S(2)}, u32[]{:S(2)}) async-start(bf16[8,256,384]{2,1,0:T(8,128)(2,1)} %bitcast.30), calls=%async_computation.1 | async-start | bytes 3145728 | tf_op jit(solution)/shard_map/all_to_all | solution.py:16
  195.3 2.1 fusion.46
  197.4 2.0 collective-permute-done.12
  199.4 5.9 %collective-permute-done.13 = bf16[2,128,1536]{2,1,0:T(8,128)(2,1)} collective-permute-done((bf16[2,128,1536]{2,1,0:T(8,128)(2,1)}, bf16[2,128,1536]{2,1,0:T(8,128)(2,1)}, u32[]{:S(2)}, u32[]{:S(2)}) %collective-permute-start.13) | collective-permute-done | bytes 786464 | tf_op jit(solution)/shard_map/ppermute | solution.py:57
  205.3 1.5 maximum_bitcast_fusion
  206.8 6.1 %collective-permute-done.14 = bf16[2,128,1536]{2,1,0:T(8,128)(2,1)} collective-permute-done((bf16[2,128,1536]{2,1,0:T(8,128)(2,1)}, bf16[2,128,1536]{2,1,0:T(8,128)(2,1)}, u32[]{:S(2)}, u32[]{:S(2)}) %collective-permute-start.14) | collective-permute-done | bytes 786464 | tf_op jit(solution)/shard_map/ppermute | solution.py:57
  212.9 1.5 maximum_bitcast_fusion.1
  214.5 5.5 %fusion.31 = bf16[1536,384]{1,0:T(8,128)(2,1)S(1)} fusion(bf16[1,4,128,1536]{3,2,1,0:T(8,128)(2,1)} %bitcast.18, bf16[1,4,128,1536]{3,2,1,0:T(8,128)(2,1)S(1)} %maximum_bitcast_fusion.1, bf16[1,4,128,1536]{3,2,1,0:T(8,128)(2,1)} %bitcast.16, bf16[1,4,128,1536]{3,2,1,0:T(8,128)(2,1)S(1)} %bitcast.79, s32[]{:T(128)S(6)} %select_n.78, ...), kind=kOutput, calls=%fused_computation.36 | convolution fusion | flops 2426732544 | bytes 9043972 | tf_op jit(solution)/shard_map/dot_general | solution.py:122
  220.0 5.4 %fusion.28 = bf16[1536,384]{1,0:T(8,128)(2,1)S(1)} fusion(bf16[1,4,128,1536]{3,2,1,0:T(8,128)(2,1)} %bitcast.11, bf16[1,4,128,1536]{3,2,1,0:T(8,128)(2,1)S(1)} %maximum_bitcast_fusion, bf16[1,4,128,1536]{3,2,1,0:T(8,128)(2,1)} %bitcast.9, bf16[1,4,128,1536]{3,2,1,0:T(8,128)(2,1)S(1)} %bitcast.80, s32[]{:T(128)S(6)} %select_n.78, ...), kind=kOutput, calls=%fused_computation.35 | convolution fusion | flops 2426732544 | bytes 9043972 | tf_op jit(solution)/shard_map/dot_general | solution.py:118
  225.4 1.6 pad_maximum_fusion
  227.0 43.8 %all-gather.5.cloned.1.call-done = bf16[2048,3072]{1,0:T(8,128)(2,1)} async-done(((bf16[128,3072]{1,0:T(8,128)(2,1)}), bf16[2048,3072]{1,0:T(8,128)(2,1)}) %all-gather.5.cloned.1.call-update) | async-done | bytes 12582928 | tf_op jit(solution)/shard_map/all_gather | solution.py:113
  270.9 6.9 %fusion.53 = bf16[4,256,384]{2,1,0:T(8,128)(2,1)S(1)} fusion(bf16[384,3072]{1,0:T(8,128)(2,1)} %param.8, bf16[4,2,256,3072]{3,2,1,0:T(8,128)(2,1)} %bitcast.86, s32[]{:T(128)S(6)} %select_n.81), kind=kOutput, calls=%fused_computation.58 | convolution fusion | flops 2416312320 | bytes 9437188 | tf_op jit(solution)/shard_map/dot_general | solution.py:78
  277.8 1.1 collective-permute-start.16
  278.9 6.9 %fusion.48 = bf16[4,256,384]{2,1,0:T(8,128)(2,1)S(1)} fusion(bf16[384,3072]{1,0:T(8,128)(2,1)} %param.8, bf16[4,2,256,3072]{3,2,1,0:T(8,128)(2,1)} %bitcast.87, s32[]{:T(128)S(6)} %select_n.80), kind=kOutput, calls=%fused_computation.57 | convolution fusion | flops 2416312320 | bytes 9437188 | tf_op jit(solution)/shard_map/dot_general | solution.py:78
  285.9 1.3 convert_add_fusion
  287.3 1.3 collective-permute-start.17
  288.5 2.4 collective-permute-start.18
  291.0 1.2 collective-permute-start.19
  292.1 9.7 %convolution_convert_fusion.1 = bf16[384,3072]{1,0:T(8,128)(2,1)} fusion(bf16[2048,384]{1,0:T(8,128)(2,1)} %bitcast.31, bf16[2048,3072]{1,0:T(8,128)(2,1)} %all-gather.5.cloned.1.call-done), kind=kOutput, calls=%fused_computation.23 | convolution fusion | flops 4833017856 | bytes 16515072 | tf_op jit(solution)/shard_map/dot_general | solution.py:129
  301.8 1.8 fusion.60
  (51 shorter events, 7.7 us)
Async XLA Ops:
  7.2 30.5 %copy-start = (bf16[3072,384]{1,0:T(8,128)(2,1)S(1)}, bf16[3072,384]{1,0:T(8,128)(2,1)}, u32[]{:S(2)}) copy-start(bf16[3072,384]{1,0:T(8,128)(2,1)} %param.9) | copy-start | bytes 7077892
  7.2 30.5 %all-gather.3.cloned.1.call-start = ((), (), s32[]{:S(2)}) async-start(), calls=%async_computation.2 | async-start | bytes 1769472 | tf_op jit(solution)/shard_map/all_gather | solution.py:99
  7.9 159.6 %reduce-scatter.2.cloned.1.call-start = ((), (), s32[]{:S(2)}) async-start(), calls=%async_computation.3 | async-start | bytes 13369344 | tf_op jit(solution)/shard_map/reduce_scatter | solution.py:109
  9.5 13.5 %collective-permute-start.5 = (bf16[128,1536]{1,0:T(8,128)(2,1)S(1)}, bf16[128,1536]{1,0:T(8,128)(2,1)S(1)}, u32[]{:S(2)}, u32[]{:S(2)}) collective-permute-start(bf16[128,1536]{1,0:T(8,128)(2,1)S(1)} %get-tuple-element.32), channel_id=1, source_target_pairs={{0,32},{8,40},{16,48},{24,56},{32,64},{40,72},{48,80},{56,88},{64,... | collective-permute-start | bytes 1179656 | tf_op jit(solution)/shard_map/ppermute | solution.py:51
  12.1 11.0 %collective-permute-start.4 = (bf16[128,1536]{1,0:T(8,128)(2,1)S(1)}, bf16[128,1536]{1,0:T(8,128)(2,1)S(1)}, u32[]{:S(2)}, u32[]{:S(2)}) collective-permute-start(bf16[128,1536]{1,0:T(8,128)(2,1)S(1)} %get-tuple-element.32), channel_id=1, source_target_pairs={{0,96},{8,104},{16,112},{24,120},{32,0},{40,8},{48,16},{56,24},{64... | collective-permute-start | bytes 1179656 | tf_op jit(solution)/shard_map/ppermute | solution.py:52
  14.3 11.6 %collective-permute-start.1 = (bf16[128,1536]{1,0:T(8,128)(2,1)S(1)}, bf16[128,1536]{1,0:T(8,128)(2,1)S(1)}, u32[]{:S(2)}, u32[]{:S(2)}) collective-permute-start(bf16[128,1536]{1,0:T(8,128)(2,1)S(1)} %get-tuple-element.33), channel_id=1, source_target_pairs={{0,8},{8,16},{16,24},{24,0},{32,40},{40,48},{48,56},{56,32},{64,72... | collective-permute-start | bytes 1179656 | tf_op jit(solution)/shard_map/ppermute | solution.py:51
  15.5 11.7 %collective-permute-start = (bf16[128,1536]{1,0:T(8,128)(2,1)S(1)}, bf16[128,1536]{1,0:T(8,128)(2,1)S(1)}, u32[]{:S(2)}, u32[]{:S(2)}) collective-permute-start(bf16[128,1536]{1,0:T(8,128)(2,1)S(1)} %get-tuple-element.33), channel_id=1, source_target_pairs={{0,24},{8,0},{16,8},{24,16},{32,56},{40,32},{48,40},{56,48},{64,88... | collective-permute-start | bytes 1179656 | tf_op jit(solution)/shard_map/ppermute | solution.py:52
  23.0 6.5 %collective-permute-start.6 = (bf16[64,1536]{1,0:T(8,128)(2,1)S(1)}, bf16[64,1536]{1,0:T(8,128)(2,1)S(1)}, u32[]{:S(2)}, u32[]{:S(2)}) collective-permute-start(bf16[64,1536]{1,0:T(8,128)(2,1)S(1)} %slice.44), channel_id=1, source_target_pairs={{0,32},{8,40},{16,48},{24,56},{32,64},{40,72},{48,80},{56,88},{64,... | collective-permute-start | bytes 589832 | tf_op jit(solution)/shard_map/ppermute | solution.py:57
  23.1 6.4 %collective-permute-start.7 = (bf16[64,1536]{1,0:T(8,128)(2,1)S(1)}, bf16[64,1536]{1,0:T(8,128)(2,1)S(1)}, u32[]{:S(2)}, u32[]{:S(2)}) collective-permute-start(bf16[64,1536]{1,0:T(8,128)(2,1)S(1)} %slice.45), channel_id=1, source_target_pairs={{0,96},{8,104},{16,112},{24,120},{32,0},{40,8},{48,16},{56,24},{64... | collective-permute-start | bytes 589832 | tf_op jit(solution)/shard_map/ppermute | solution.py:57
  25.9 6.0 %collective-permute-start.2 = (bf16[64,1536]{1,0:T(8,128)(2,1)S(1)}, bf16[64,1536]{1,0:T(8,128)(2,1)S(1)}, u32[]{:S(2)}, u32[]{:S(2)}) collective-permute-start(bf16[64,1536]{1,0:T(8,128)(2,1)S(1)} %slice.41), channel_id=1, source_target_pairs={{0,8},{8,16},{16,24},{24,0},{32,40},{40,48},{48,56},{56,32},{64,72... | collective-permute-start | bytes 589832 | tf_op jit(solution)/shard_map/ppermute | solution.py:57
  27.2 4.7 %collective-permute-start.3 = (bf16[64,1536]{1,0:T(8,128)(2,1)S(1)}, bf16[64,1536]{1,0:T(8,128)(2,1)S(1)}, u32[]{:S(2)}, u32[]{:S(2)}) collective-permute-start(bf16[64,1536]{1,0:T(8,128)(2,1)S(1)} %slice.42), channel_id=1, source_target_pairs={{0,24},{8,0},{16,8},{24,16},{32,56},{40,32},{48,40},{56,48},{64,88... | collective-permute-start | bytes 589832 | tf_op jit(solution)/shard_map/ppermute | solution.py:57
  48.8 2.9 copy-start.4
  48.8 118.6 %copy-start.3 = (bf16[128,3072]{1,0:T(8,128)(2,1)S(1)}, bf16[128,3072]{1,0:T(8,128)(2,1)}, u32[]{:S(2)}) copy-start(bf16[128,3072]{1,0:T(8,128)(2,1)} %param.7) | copy-start | bytes 2359300
  48.9 121.4 %copy-start.2 = (bf16[256,384]{1,0:T(8,128)(2,1)S(1)}, bf16[256,384]{1,0:T(8,128)(2,1)}, u32[]{:S(2)}) copy-start(bf16[256,384]{1,0:T(8,128)(2,1)} %param.5) | copy-start | bytes 589828
  48.9 222.0 %all-gather.5.cloned.1.call-start = ((), (), s32[]{:S(2)}) async-start(), calls=%async_computation.4 | async-start | bytes 13369344 | tf_op jit(solution)/shard_map/all_gather | solution.py:113
  48.9 61.8 %collective-permute-start.10 = (bf16[4,128,1536]{2,1,0:T(8,128)(2,1)}, bf16[4,128,1536]{2,1,0:T(8,128)(2,1)}, u32[]{:S(2)}, u32[]{:S(2)}) collective-permute-start(bf16[4,128,1536]{2,1,0:T(8,128)(2,1)} %pad_maximum_fusion.1), channel_id=1, source_target_pairs={{0,32},{8,40},{16,48},{24,56},{32,64},{40,72},{48,80},{56,88},{64,... | collective-permute-start | bytes 4718600 | tf_op jit(solution)/shard_map/ppermute | solution.py:51
  50.2 62.3 %collective-permute-start.11 = (bf16[4,128,1536]{2,1,0:T(8,128)(2,1)}, bf16[4,128,1536]{2,1,0:T(8,128)(2,1)}, u32[]{:S(2)}, u32[]{:S(2)}) collective-permute-start(bf16[4,128,1536]{2,1,0:T(8,128)(2,1)} %pad_maximum_fusion.1), channel_id=1, source_target_pairs={{0,96},{8,104},{16,112},{24,120},{32,0},{40,8},{48,16},{56,24},{64... | collective-permute-start | bytes 4718600 | tf_op jit(solution)/shard_map/ppermute | solution.py:52
  51.8 115.7 %collective-permute-start.8 = (bf16[4,128,1536]{2,1,0:T(8,128)(2,1)S(1)}, bf16[4,128,1536]{2,1,0:T(8,128)(2,1)}, u32[]{:S(2)}, u32[]{:S(2)}) collective-permute-start(bf16[4,128,1536]{2,1,0:T(8,128)(2,1)S(1)} %copy-done.4), channel_id=1, source_target_pairs={{0,8},{8,16},{16,24},{24,0},{32,40},{40,48},{48,56},{56,32},{64,72... | collective-permute-start | bytes 4718600 | tf_op jit(solution)/shard_map/ppermute | solution.py:51
  52.9 114.6 %collective-permute-start.9 = (bf16[4,128,1536]{2,1,0:T(8,128)(2,1)S(1)}, bf16[4,128,1536]{2,1,0:T(8,128)(2,1)}, u32[]{:S(2)}, u32[]{:S(2)}) collective-permute-start(bf16[4,128,1536]{2,1,0:T(8,128)(2,1)S(1)} %copy-done.4), channel_id=1, source_target_pairs={{0,24},{8,0},{16,8},{24,16},{32,56},{40,32},{48,40},{56,48},{64,88... | collective-permute-start | bytes 4718600 | tf_op jit(solution)/shard_map/ppermute | solution.py:52
  172.9 26.6 %collective-permute-start.12 = (bf16[2,128,1536]{2,1,0:T(8,128)(2,1)S(1)}, bf16[2,128,1536]{2,1,0:T(8,128)(2,1)}, u32[]{:S(2)}, u32[]{:S(2)}) collective-permute-start(bf16[2,128,1536]{2,1,0:T(8,128)(2,1)S(1)} %slice.36), channel_id=1, source_target_pairs={{0,32},{8,40},{16,48},{24,56},{32,64},{40,72},{48,80},{56,88},{64,... | collective-permute-start | bytes 2359304 | tf_op jit(solution)/shard_map/ppermute | solution.py:57
  175.0 30.3 %collective-permute-start.13 = (bf16[2,128,1536]{2,1,0:T(8,128)(2,1)}, bf16[2,128,1536]{2,1,0:T(8,128)(2,1)}, u32[]{:S(2)}, u32[]{:S(2)}) collective-permute-start(bf16[2,128,1536]{2,1,0:T(8,128)(2,1)} %slice.37), channel_id=1, source_target_pairs={{0,96},{8,104},{16,112},{24,120},{32,0},{40,8},{48,16},{56,24},{64... | collective-permute-start | bytes 2359304 | tf_op jit(solution)/shard_map/ppermute | solution.py:57
  181.2 31.7 %collective-permute-start.14 = (bf16[2,128,1536]{2,1,0:T(8,128)(2,1)}, bf16[2,128,1536]{2,1,0:T(8,128)(2,1)}, u32[]{:S(2)}, u32[]{:S(2)}) collective-permute-start(bf16[2,128,1536]{2,1,0:T(8,128)(2,1)} %slice.38), channel_id=1, source_target_pairs={{0,8},{8,16},{16,24},{24,0},{32,40},{40,48},{48,56},{56,32},{64,72... | collective-permute-start | bytes 2359304 | tf_op jit(solution)/shard_map/ppermute | solution.py:57
  183.4 29.5 %collective-permute-start.15 = (bf16[2,128,1536]{2,1,0:T(8,128)(2,1)}, bf16[2,128,1536]{2,1,0:T(8,128)(2,1)}, u32[]{:S(2)}, u32[]{:S(2)}) collective-permute-start(bf16[2,128,1536]{2,1,0:T(8,128)(2,1)} %slice.39), channel_id=1, source_target_pairs={{0,24},{8,0},{16,8},{24,16},{32,56},{40,32},{48,40},{56,48},{64,88... | collective-permute-start | bytes 2359304 | tf_op jit(solution)/shard_map/ppermute | solution.py:57
  188.8 103.3 %all-to-all-start = ((bf16[8,256,384]{2,1,0:T(8,128)(2,1)}), bf16[8,256,384]{2,1,0:T(8,128)(2,1)}, u32[]{:S(2)}, u32[]{:S(2)}) async-start(bf16[8,256,384]{2,1,0:T(8,128)(2,1)} %bitcast.30), calls=%async_computation.1 | async-start | bytes 3145728 | tf_op jit(solution)/shard_map/all_to_all | solution.py:16
  214.4 5.5 %copy-start.5 = (bf16[4,128,1536]{2,1,0:T(8,128)(2,1)S(1)}, bf16[4,128,1536]{2,1,0:T(8,128)(2,1)}, u32[]{:S(2)}) copy-start(bf16[4,128,1536]{2,1,0:T(8,128)(2,1)} %pad_maximum_fusion.1) | copy-start | bytes 4718596
  277.8 8.1 %collective-permute-start.16 = (bf16[4,256,384]{2,1,0:T(8,128)(2,1)S(1)}, bf16[4,256,384]{2,1,0:T(8,128)(2,1)S(1)}, u32[]{:S(2)}, u32[]{:S(2)}) collective-permute-start(bf16[4,256,384]{2,1,0:T(8,128)(2,1)S(1)} %fusion.53), channel_id=1, source_target_pairs={{0,1},{1,0},{2,3},{3,2},{4,5},{5,4},{6,7},{7,6},{8,9},{9,8},{10,11... | collective-permute-start | bytes 2359304 | tf_op jit(solution)/shard_map/ppermute | solution.py:82
  287.3 14.6 %collective-permute-start.17 = (bf16[256,384]{1,0:T(8,128)(2,1)S(1)}, bf16[256,384]{1,0:T(8,128)(2,1)S(1)}, u32[]{:S(2)}, u32[]{:S(2)}) collective-permute-start(bf16[256,384]{1,0:T(8,128)(2,1)S(1)} %get-tuple-element.27), channel_id=1, source_target_pairs={{0,2},{1,3},{2,4},{3,5},{4,6},{5,7},{6,0},{7,1},{8,10},{9,11},{10,... | collective-permute-start | bytes 589832 | tf_op jit(solution)/shard_map/ppermute | solution.py:89
  288.5 13.3 %collective-permute-start.18 = (bf16[256,384]{1,0:T(8,128)(2,1)S(1)}, bf16[256,384]{1,0:T(8,128)(2,1)S(1)}, u32[]{:S(2)}, u32[]{:S(2)}) collective-permute-start(bf16[256,384]{1,0:T(8,128)(2,1)S(1)} %get-tuple-element.29), channel_id=1, source_target_pairs={{0,4},{1,5},{2,6},{3,7},{4,0},{5,1},{6,2},{7,3},{8,12},{9,13},{10,... | collective-permute-start | bytes 589832 | tf_op jit(solution)/shard_map/ppermute | solution.py:89
  291.0 10.9 %collective-permute-start.19 = (bf16[256,384]{1,0:T(8,128)(2,1)S(1)}, bf16[256,384]{1,0:T(8,128)(2,1)S(1)}, u32[]{:S(2)}, u32[]{:S(2)}) collective-permute-start(bf16[256,384]{1,0:T(8,128)(2,1)S(1)} %get-tuple-element.28), channel_id=1, source_target_pairs={{0,6},{1,7},{2,0},{3,1},{4,2},{5,3},{6,4},{7,5},{8,14},{9,15},{10,... | collective-permute-start | bytes 589832 | tf_op jit(solution)/shard_map/ppermute | solution.py:89
  292.1 11.5 %copy-start.1 = (bf16[3072,384]{1,0:T(8,128)(2,1)S(1)}, bf16[3072,384]{1,0:T(8,128)(2,1)}, u32[]{:S(2)}) copy-start(bf16[3072,384]{1,0:T(8,128)(2,1)} %param.9) | copy-start | bytes 7077892
Sparse Core Ops, SparseCore 0:
  9.7 27.9 all-gather.2
  49.0 118.4 reduce-scatter.1
  170.4 100.4 all-gather.4

commit v12 on v9

--- a/solution.py
+++ b/solution.py
@@ -85,12 +85,24 @@
     return acc
 
 
+def gather_col_pair_ring(x, n_y):
+    n_col = 2 * n_y
+    me = lax.axis_index("col")
+    k, y = me % 2, me // 2
+    other = lax.ppermute(x, "col", [(c, c ^ 1) for c in range(n_col)])
+    both = jnp.where(k == 0, jnp.concatenate([x, other], 0), jnp.concatenate([other, x], 0))
+    recv = [lax.ppermute(both, "col", [(c, (c + 2 * d) % n_col) for c in range(n_col)])
+            for d in range(1, n_y)]
+    rel = jnp.stack([both] + recv[::-1])
+    return jnp.roll(rel, y, axis=0).reshape((-1,) + x.shape[1:])
+
+
 def on_device(inputs, out_grad, pre_act, w_in, w_out):
     n_col = lax.psum(1, "col")
     value, slope = gelu_parts(pre_act)
     hidden_loc = value.astype(jnp.bfloat16)
     n_z, n_x = 4, 4
-    grad_all = lax.all_gather(out_grad, "col", axis=0, tiled=True)
+    grad_all = gather_col_pair_ring(out_grad, n_col // 2)
     fx, bx, fz, bz = torus_perms(n_z, n_x)
     w = hidden_loc.shape[1] // 2
     a1, _ = ring_gather(hidden_loc[:, :w], fx, bx)

time: 309 us -> 325 us (1.052)
  local copies, waits for them, and re-layouts: 13.5 us -> 23.5 us
  starting transfers between devices: 36.3 us -> 43.4 us
    ppermute x0 -> x4, starting transfers between devices: none -> 7.58 us  [the longest x3 6.11 us: gather_col_pair_ring(): lax.ppermute(both, 'col', [(c, (c + 2 * d) % n_col) for c in range(n_col)])]
    ppermute x0 -> x4, waiting for transfers between devices: none -> 5.84 us  [the longest x3 5.84 us: gather_col_pair_ring(): lax.ppermute(both, 'col', [(c, (c + 2 * d) % n_col) for c in range(n_col)])]
    unnamed x19 -> x30, local copies, waits for them, and re-layouts: 4.91 us -> 9.22 us
  transfers between devices with their start and end apart: 24 -> 27, of which waited for: 12 -> 10; matrix products, arithmetic and copies ran while one was open for 18% -> 20% of each run, Pallas kernels for 0% -> 0%
where the time goes in v12:
time: 325 us; the launch traced here: 324 us
  waiting for transfers between devices  183 us (56%)
  starting transfers between devices  43.4 us (13%)
  matrix products  40.7 us (13%)
  local copies, waits for them, and re-layouts  23.5 us (7%)
  other arithmetic  19.3 us (6%)
  between operations  14.3 us (4%)
    ppermute x4, waiting for transfers between devices, ring_gather(): from_prev = lax.ppermute(x, 'row', fwd)  59.4 us
    reduce_scatter x1, waiting for transfers between devices, on_device(): total = lax.psum_scatter(partial, 'row', scatter_dimension=0, tiled=True)  56.1 us
    all_gather x1, waiting for transfers between devices, on_device(): pre_grad = lax.all_gather(pre_grad_loc, 'row', axis=0, tiled=True)  43.5 us
    dot_general x1, matrix products, on_device(): lax.dot_general(pre_grad, w_in, (((1,), (1,)), ((), ())), preferred_eleme...  10.4 us
    ppermute x4, starting transfers between devices, ring_gather(): lax.ppermute(from_next[h:], 'row', bwd)  9.9 us
    dot_general x1, matrix products, on_device(): lax.dot_general(grad_all, w_out, (((1,), (1,)), ((), ())), preferred_elem...  9.76 us
    dot_general x1, matrix products, on_device(): lax.dot_general(inputs_all, pre_grad, (((0,), (0,)), ((), ())), preferred...  9.68 us
    unnamed x30, local copies, waits for them, and re-layouts  9.22 us
  transfers between devices with their start and end apart: 27, of which 10 were waited for; matrix products, arithmetic and copies ran while one was open for 20% of the time, Pallas kernels for 0%

profile of v12, /device:TPU:1, one launch (start us, length us, event | category | flops | bytes accessed | tf_op | source)
XLA Modules:
  0.0 324.0 jit_solution(17288205535593828785)
XLA Ops:
  7.2 1.5 collective-permute-start.8
  8.7 1.5 fusion.31
  11.2 1.7 collective-permute-start.5
  12.9 2.1 collective-permute-start.4
  15.0 1.2 collective-permute-start.1
  16.3 1.5 collective-permute-start
  18.6 2.7 collective-permute-start.9
  21.3 3.3 %collective-permute-done.5 = bf16[128,1536]{1,0:T(8,128)(2,1)} collective-permute-done((bf16[128,1536]{1,0:T(8,128)(2,1)}, bf16[128,1536]{1,0:T(8,128)(2,1)}, u32[]{:S(2)}, u32[]{:S(2)}) %collective-permute-start.5) | collective-permute-done | bytes 393248 | tf_op jit(solution)/shard_map/ppermute | solution.py:51
  24.7 2.9 collective-permute-start.10
  31.1 2.7 collective-permute-start.7
  34.8 1.3 collective-permute-start.2
  37.2 1.8 collective-permute-start.3
  40.0 5.8 %collective-permute-done.11 = bf16[512,384]{1,0:T(8,128)(2,1)S(1)} collective-permute-done((bf16[512,384]{1,0:T(8,128)(2,1)}, bf16[512,384]{1,0:T(8,128)(2,1)S(1)}, u32[]{:S(2)}, u32[]{:S(2)}) %collective-permute-start.11) | collective-permute-done | bytes 393248 | tf_op jit(solution)/shard_map/ppermute | solution.py:94
  46.2 2.5 pad_maximum_fusion.2
  49.7 1.1 bitcast_dynamic-update-slice_fusion.3
  51.1 3.0 pad_maximum_fusion.1
  54.0 9.8 %convolution_convert_fusion = bf16[2048,3072]{1,0:T(8,128)(2,1)} fusion(bf16[2048,384]{1,0:T(8,128)(2,1)S(1)} %bitcast.80, bf16[3072,384]{1,0:T(8,128)(2,1)S(1)} %copy-done), kind=kOutput, calls=%fused_computation | convolution fusion | flops 4838129664 | bytes 16515072 | tf_op jit(solution)/shard_map/dot_general | solution.py:112
  64.0 2.7 collective-permute-start.15
  66.6 1.2 collective-permute-start.12
  67.8 1.5 collective-permute-start.13
  69.3 56.0 %collective-permute-done.14 = bf16[4,128,1536]{2,1,0:T(8,128)(2,1)} collective-permute-done((bf16[4,128,1536]{2,1,0:T(8,128)(2,1)}, bf16[4,128,1536]{2,1,0:T(8,128)(2,1)}, u32[]{:S(2)}, u32[]{:S(2)}) %collective-permute-start.14) | collective-permute-done | bytes 1572896 | tf_op jit(solution)/shard_map/ppermute | solution.py:51
  125.3 1.5 collective-permute-done.15
  126.8 56.1 %reduce-scatter.2.cloned.1.call-done = bf16[128,3072]{1,0:T(8,128)(2,1)} async-done(((bf16[2048,3072]{1,0:T(8,128)(2,1)}), bf16[128,3072]{1,0:T(8,128)(2,1)}) %reduce-scatter.2.cloned.1.call-update) | async-done | bytes 786448 | tf_op jit(solution)/shard_map/reduce_scatter | solution.py:115
  182.9 2.7 fusion.36
  187.1 2.1 slice.36
  189.2 2.1 slice.37
  191.3 2.7 collective-permute-start.17
  195.4 2.1 slice.38
  197.5 2.1 slice.39
  199.6 2.7 collective-permute-start.19
  205.1 6.8 %all-to-all-start = ((bf16[8,256,384]{2,1,0:T(8,128)(2,1)}), bf16[8,256,384]{2,1,0:T(8,128)(2,1)}, u32[]{:S(2)}, u32[]{:S(2)}) async-start(bf16[8,256,384]{2,1,0:T(8,128)(2,1)} %bitcast.35), calls=%async_computation.1 | async-start | bytes 3145728 | tf_op jit(solution)/shard_map/all_to_all | solution.py:16
  212.5 4.5 %collective-permute-done.16 = bf16[2,128,1536]{2,1,0:T(8,128)(2,1)} collective-permute-done((bf16[2,128,1536]{2,1,0:T(8,128)(2,1)}, bf16[2,128,1536]{2,1,0:T(8,128)(2,1)}, u32[]{:S(2)}, u32[]{:S(2)}) %collective-permute-start.16) | collective-permute-done | bytes 786464 | tf_op jit(solution)/shard_map/ppermute | solution.py:57
  216.9 5.5 %collective-permute-done.17 = bf16[2,128,1536]{2,1,0:T(8,128)(2,1)} collective-permute-done((bf16[2,128,1536]{2,1,0:T(8,128)(2,1)}, bf16[2,128,1536]{2,1,0:T(8,128)(2,1)}, u32[]{:S(2)}, u32[]{:S(2)}) %collective-permute-start.17) | collective-permute-done | bytes 786464 | tf_op jit(solution)/shard_map/ppermute | solution.py:57
  222.4 1.5 maximum_bitcast_fusion
  223.9 4.5 %collective-permute-done.18 = bf16[2,128,1536]{2,1,0:T(8,128)(2,1)} collective-permute-done((bf16[2,128,1536]{2,1,0:T(8,128)(2,1)}, bf16[2,128,1536]{2,1,0:T(8,128)(2,1)}, u32[]{:S(2)}, u32[]{:S(2)}) %collective-permute-start.18) | collective-permute-done | bytes 786464 | tf_op jit(solution)/shard_map/ppermute | solution.py:57
  228.4 1.5 maximum_bitcast_fusion.1
  230.0 5.5 %fusion.25 = bf16[1536,384]{1,0:T(8,128)(2,1)S(1)} fusion(bf16[1,4,128,1536]{3,2,1,0:T(8,128)(2,1)} %bitcast.24, bf16[1,4,128,1536]{3,2,1,0:T(8,128)(2,1)S(1)} %maximum_bitcast_fusion.1, bf16[1,4,128,1536]{3,2,1,0:T(8,128)(2,1)} %bitcast.22, bf16[1,4,128,1536]{3,2,1,0:T(8,128)(2,1)S(1)} %bitcast.86, s32[]{:T(128)S(6)} %select_n.118, ...), kind=kOutput, calls=%fused_computation.30 | convolution fusion | flops 2426732544 | bytes 9043972 | tf_op jit(solution)/shard_map/dot_general | solution.py:128
  235.5 5.4 %fusion.22 = bf16[1536,384]{1,0:T(8,128)(2,1)S(1)} fusion(bf16[1,4,128,1536]{3,2,1,0:T(8,128)(2,1)} %bitcast.17, bf16[1,4,128,1536]{3,2,1,0:T(8,128)(2,1)S(1)} %maximum_bitcast_fusion, bf16[1,4,128,1536]{3,2,1,0:T(8,128)(2,1)} %bitcast.15, bf16[1,4,128,1536]{3,2,1,0:T(8,128)(2,1)S(1)} %bitcast.87, s32[]{:T(128)S(6)} %select_n.118, ...), kind=kOutput, calls=%fused_computation.29 | convolution fusion | flops 2426732544 | bytes 9043972 | tf_op jit(solution)/shard_map/dot_general | solution.py:124
  240.9 1.6 pad_maximum_fusion
  242.5 43.5 %all-gather.2.cloned.1.call-done = bf16[2048,3072]{1,0:T(8,128)(2,1)} async-done(((bf16[128,3072]{1,0:T(8,128)(2,1)}), bf16[2048,3072]{1,0:T(8,128)(2,1)}) %all-gather.2.cloned.1.call-update) | async-done | bytes 12582928 | tf_op jit(solution)/shard_map/all_gather | solution.py:119
  286.0 10.4 %convolution_convert_fusion.2 = bf16[2048,384]{1,0:T(8,128)(2,1)S(1)} fusion(bf16[2048,3072]{1,0:T(8,128)(2,1)} %all-gather.2.cloned.1.call-done, bf16[384,3072]{1,0:T(8,128)(2,1)} %param.8), kind=kOutput, calls=%fused_computation.31 | convolution fusion | flops 4832624640 | bytes 16515072 | tf_op jit(solution)/shard_map/dot_general | solution.py:134
  297.4 1.9 collective-permute-done.20
  299.3 1.4 fusion.49
  300.8 1.3 collective-permute-start.21
  302.0 2.4 collective-permute-start.22
  304.5 1.2 collective-permute-start.23
  305.6 9.7 %convolution_convert_fusion.1 = bf16[384,3072]{1,0:T(8,128)(2,1)} fusion(bf16[2048,384]{1,0:T(8,128)(2,1)} %bitcast.36, bf16[2048,3072]{1,0:T(8,128)(2,1)} %all-gather.2.cloned.1.call-done), kind=kOutput, calls=%fused_computation.17 | convolution fusion | flops 4833017856 | bytes 16515072 | tf_op jit(solution)/shard_map/dot_general | solution.py:138
  315.3 1.8 fusion.42
  (72 shorter events, 17.6 us)
Async XLA Ops:
  7.2 46.9 %copy-start = (bf16[3072,384]{1,0:T(8,128)(2,1)S(1)}, bf16[3072,384]{1,0:T(8,128)(2,1)}, u32[]{:S(2)}) copy-start(bf16[3072,384]{1,0:T(8,128)(2,1)} %param.9) | copy-start | bytes 7077892
  7.2 175.7 %reduce-scatter.2.cloned.1.call-start = ((), (), s32[]{:S(2)}) async-start(), calls=%async_computation.2 | async-start | bytes 13369344 | tf_op jit(solution)/shard_map/reduce_scatter | solution.py:115
  7.2 10.5 %collective-permute-start.8 = (bf16[256,384]{1,0:T(8,128)(2,1)}, bf16[256,384]{1,0:T(8,128)(2,1)S(1)}, u32[]{:S(2)}, u32[]{:S(2)}) collective-permute-start(bf16[256,384]{1,0:T(8,128)(2,1)} %param.6), channel_id=1, source_target_pairs={{0,1},{1,0},{2,3},{3,2},{4,5},{5,4},{6,7},{7,6},{8,9},{9,8},{10,11... | collective-permute-start | bytes 589832 | tf_op jit(solution)/shard_map/ppermute | solution.py:92
  10.2 7.6 %copy-start.6 = (bf16[256,384]{1,0:T(8,128)(2,1)S(1)}, bf16[256,384]{1,0:T(8,128)(2,1)}, u32[]{:S(2)}) copy-start(bf16[256,384]{1,0:T(8,128)(2,1)} %param.6) | copy-start | bytes 589828
  11.2 13.5 %collective-permute-start.5 = (bf16[128,1536]{1,0:T(8,128)(2,1)}, bf16[128,1536]{1,0:T(8,128)(2,1)}, u32[]{:S(2)}, u32[]{:S(2)}) collective-permute-start(bf16[128,1536]{1,0:T(8,128)(2,1)} %get-tuple-element.32), channel_id=1, source_target_pairs={{0,32},{8,40},{16,48},{24,56},{32,64},{40,72},{48,80},{56,88},{64,... | collective-permute-start | bytes 1179656 | tf_op jit(solution)/shard_map/ppermute | solution.py:51
  12.9 15.7 %collective-permute-start.4 = (bf16[128,1536]{1,0:T(8,128)(2,1)}, bf16[128,1536]{1,0:T(8,128)(2,1)}, u32[]{:S(2)}, u32[]{:S(2)}) collective-permute-start(bf16[128,1536]{1,0:T(8,128)(2,1)} %get-tuple-element.32), channel_id=1, source_target_pairs={{0,96},{8,104},{16,112},{24,120},{32,0},{40,8},{48,16},{56,24},{64... | collective-permute-start | bytes 1179656 | tf_op jit(solution)/shard_map/ppermute | solution.py:52
  15.0 15.0 %collective-permute-start.1 = (bf16[128,1536]{1,0:T(8,128)(2,1)}, bf16[128,1536]{1,0:T(8,128)(2,1)}, u32[]{:S(2)}, u32[]{:S(2)}) collective-permute-start(bf16[128,1536]{1,0:T(8,128)(2,1)} %get-tuple-element.33), channel_id=1, source_target_pairs={{0,8},{8,16},{16,24},{24,0},{32,40},{40,48},{48,56},{56,32},{64,72... | collective-permute-start | bytes 1179656 | tf_op jit(solution)/shard_map/ppermute | solution.py:51
  16.3 14.9 %collective-permute-start = (bf16[128,1536]{1,0:T(8,128)(2,1)}, bf16[128,1536]{1,0:T(8,128)(2,1)}, u32[]{:S(2)}, u32[]{:S(2)}) collective-permute-start(bf16[128,1536]{1,0:T(8,128)(2,1)} %get-tuple-element.33), channel_id=1, source_target_pairs={{0,24},{8,0},{16,8},{24,16},{32,56},{40,32},{48,40},{56,48},{64,88... | collective-permute-start | bytes 1179656 | tf_op jit(solution)/shard_map/ppermute | solution.py:52
  18.6 16.2 %collective-permute-start.9 = (bf16[512,384]{1,0:T(8,128)(2,1)}, bf16[512,384]{1,0:T(8,128)(2,1)}, u32[]{:S(2)}, u32[]{:S(2)}) collective-permute-start(bf16[512,384]{1,0:T(8,128)(2,1)} %maximum_select_fusion.1), channel_id=1, source_target_pairs={{0,6},{1,7},{2,0},{3,1},{4,2},{5,3},{6,4},{7,5},{8,14},{9,15},{10,... | collective-permute-start | bytes 1179656 | tf_op jit(solution)/shard_map/ppermute | solution.py:94
  24.7 12.5 %collective-permute-start.10 = (bf16[512,384]{1,0:T(8,128)(2,1)}, bf16[512,384]{1,0:T(8,128)(2,1)}, u32[]{:S(2)}, u32[]{:S(2)}) collective-permute-start(bf16[512,384]{1,0:T(8,128)(2,1)} %maximum_select_fusion.1), channel_id=1, source_target_pairs={{0,4},{1,5},{2,6},{3,7},{4,0},{5,1},{6,2},{7,3},{8,12},{9,13},{10,... | collective-permute-start | bytes 1179656 | tf_op jit(solution)/shard_map/ppermute | solution.py:94
  28.7 17.2 %collective-permute-start.11 = (bf16[512,384]{1,0:T(8,128)(2,1)}, bf16[512,384]{1,0:T(8,128)(2,1)S(1)}, u32[]{:S(2)}, u32[]{:S(2)}) collective-permute-start(bf16[512,384]{1,0:T(8,128)(2,1)} %maximum_select_fusion.1), channel_id=1, source_target_pairs={{0,2},{1,3},{2,4},{3,5},{4,6},{5,7},{6,0},{7,1},{8,10},{9,11},{10,... | collective-permute-start | bytes 1179656 | tf_op jit(solution)/shard_map/ppermute | solution.py:94
  30.1 16.0 %collective-permute-start.6 = (bf16[64,1536]{1,0:T(8,128)(2,1)S(1)}, bf16[64,1536]{1,0:T(8,128)(2,1)S(1)}, u32[]{:S(2)}, u32[]{:S(2)}) collective-permute-start(bf16[64,1536]{1,0:T(8,128)(2,1)S(1)} %slice.44), channel_id=1, source_target_pairs={{0,32},{8,40},{16,48},{24,56},{32,64},{40,72},{48,80},{56,88},{64,... | collective-permute-start | bytes 589832 | tf_op jit(solution)/shard_map/ppermute | solution.py:57
  31.1 15.0 %collective-permute-start.7 = (bf16[64,1536]{1,0:T(8,128)(2,1)S(1)}, bf16[64,1536]{1,0:T(8,128)(2,1)S(1)}, u32[]{:S(2)}, u32[]{:S(2)}) collective-permute-start(bf16[64,1536]{1,0:T(8,128)(2,1)S(1)} %slice.45), channel_id=1, source_target_pairs={{0,96},{8,104},{16,112},{24,120},{32,0},{40,8},{48,16},{56,24},{64... | collective-permute-start | bytes 589832 | tf_op jit(solution)/shard_map/ppermute | solution.py:57
  34.8 16.2 %collective-permute-start.2 = (bf16[64,1536]{1,0:T(8,128)(2,1)S(1)}, bf16[64,1536]{1,0:T(8,128)(2,1)S(1)}, u32[]{:S(2)}, u32[]{:S(2)}) collective-permute-start(bf16[64,1536]{1,0:T(8,128)(2,1)S(1)} %slice.41), channel_id=1, source_target_pairs={{0,8},{8,16},{16,24},{24,0},{32,40},{40,48},{48,56},{56,32},{64,72... | collective-permute-start | bytes 589832 | tf_op jit(solution)/shard_map/ppermute | solution.py:57
  37.2 13.9 %collective-permute-start.3 = (bf16[64,1536]{1,0:T(8,128)(2,1)S(1)}, bf16[64,1536]{1,0:T(8,128)(2,1)S(1)}, u32[]{:S(2)}, u32[]{:S(2)}) collective-permute-start(bf16[64,1536]{1,0:T(8,128)(2,1)S(1)} %slice.42), channel_id=1, source_target_pairs={{0,24},{8,0},{16,8},{24,16},{32,56},{40,32},{48,40},{56,48},{64,88... | collective-permute-start | bytes 589832 | tf_op jit(solution)/shard_map/ppermute | solution.py:57
  51.0 3.0 copy-start.3
  63.8 2.8 copy-start.7
  63.8 119.1 %copy-start.5 = (bf16[128,3072]{1,0:T(8,128)(2,1)S(1)}, bf16[128,3072]{1,0:T(8,128)(2,1)}, u32[]{:S(2)}) copy-start(bf16[128,3072]{1,0:T(8,128)(2,1)} %param.7) | copy-start | bytes 2359300
  63.8 121.9 %copy-start.2 = (bf16[256,384]{1,0:T(8,128)(2,1)S(1)}, bf16[256,384]{1,0:T(8,128)(2,1)}, u32[]{:S(2)}) copy-start(bf16[256,384]{1,0:T(8,128)(2,1)} %param.5) | copy-start | bytes 589828
  63.8 222.2 %all-gather.2.cloned.1.call-start = ((), (), s32[]{:S(2)}) async-start(), calls=%async_computation.3 | async-start | bytes 13369344 | tf_op jit(solution)/shard_map/all_gather | solution.py:119
  63.9 61.4 %collective-permute-start.14 = (bf16[4,128,1536]{2,1,0:T(8,128)(2,1)}, bf16[4,128,1536]{2,1,0:T(8,128)(2,1)}, u32[]{:S(2)}, u32[]{:S(2)}) collective-permute-start(bf16[4,128,1536]{2,1,0:T(8,128)(2,1)} %pad_maximum_fusion.1), channel_id=1, source_target_pairs={{0,32},{8,40},{16,48},{24,56},{32,64},{40,72},{48,80},{56,88},{64,... | collective-permute-start | bytes 4718600 | tf_op jit(solution)/shard_map/ppermute | solution.py:51
  64.0 62.9 %collective-permute-start.15 = (bf16[4,128,1536]{2,1,0:T(8,128)(2,1)}, bf16[4,128,1536]{2,1,0:T(8,128)(2,1)}, u32[]{:S(2)}, u32[]{:S(2)}) collective-permute-start(bf16[4,128,1536]{2,1,0:T(8,128)(2,1)} %pad_maximum_fusion.1), channel_id=1, source_target_pairs={{0,96},{8,104},{16,112},{24,120},{32,0},{40,8},{48,16},{56,24},{64... | collective-permute-start | bytes 4718600 | tf_op jit(solution)/shard_map/ppermute | solution.py:52
  66.6 116.3 %collective-permute-start.12 = (bf16[4,128,1536]{2,1,0:T(8,128)(2,1)S(1)}, bf16[4,128,1536]{2,1,0:T(8,128)(2,1)}, u32[]{:S(2)}, u32[]{:S(2)}) collective-permute-start(bf16[4,128,1536]{2,1,0:T(8,128)(2,1)S(1)} %copy-done.7), channel_id=1, source_target_pairs={{0,8},{8,16},{16,24},{24,0},{32,40},{40,48},{48,56},{56,32},{64,72... | collective-permute-start | bytes 4718600 | tf_op jit(solution)/shard_map/ppermute | solution.py:51
  67.8 115.1 %collective-permute-start.13 = (bf16[4,128,1536]{2,1,0:T(8,128)(2,1)S(1)}, bf16[4,128,1536]{2,1,0:T(8,128)(2,1)}, u32[]{:S(2)}, u32[]{:S(2)}) collective-permute-start(bf16[4,128,1536]{2,1,0:T(8,128)(2,1)S(1)} %copy-done.7), channel_id=1, source_target_pairs={{0,24},{8,0},{16,8},{24,16},{32,56},{40,32},{48,40},{56,48},{64,88... | collective-permute-start | bytes 4718600 | tf_op jit(solution)/shard_map/ppermute | solution.py:52
  189.2 27.7 %collective-permute-start.16 = (bf16[2,128,1536]{2,1,0:T(8,128)(2,1)}, bf16[2,128,1536]{2,1,0:T(8,128)(2,1)}, u32[]{:S(2)}, u32[]{:S(2)}) collective-permute-start(bf16[2,128,1536]{2,1,0:T(8,128)(2,1)} %slice.36), channel_id=1, source_target_pairs={{0,32},{8,40},{16,48},{24,56},{32,64},{40,72},{48,80},{56,88},{64,... | collective-permute-start | bytes 2359304 | tf_op jit(solution)/shard_map/ppermute | solution.py:57
  191.3 31.1 %collective-permute-start.17 = (bf16[2,128,1536]{2,1,0:T(8,128)(2,1)}, bf16[2,128,1536]{2,1,0:T(8,128)(2,1)}, u32[]{:S(2)}, u32[]{:S(2)}) collective-permute-start(bf16[2,128,1536]{2,1,0:T(8,128)(2,1)} %slice.37), channel_id=1, source_target_pairs={{0,96},{8,104},{16,112},{24,120},{32,0},{40,8},{48,16},{56,24},{64... | collective-permute-start | bytes 2359304 | tf_op jit(solution)/shard_map/ppermute | solution.py:57
  197.5 30.9 %collective-permute-start.18 = (bf16[2,128,1536]{2,1,0:T(8,128)(2,1)}, bf16[2,128,1536]{2,1,0:T(8,128)(2,1)}, u32[]{:S(2)}, u32[]{:S(2)}) collective-permute-start(bf16[2,128,1536]{2,1,0:T(8,128)(2,1)} %slice.38), channel_id=1, source_target_pairs={{0,8},{8,16},{16,24},{24,0},{32,40},{40,48},{48,56},{56,32},{64,72... | collective-permute-start | bytes 2359304 | tf_op jit(solution)/shard_map/ppermute | solution.py:57
  199.6 28.8 %collective-permute-start.19 = (bf16[2,128,1536]{2,1,0:T(8,128)(2,1)}, bf16[2,128,1536]{2,1,0:T(8,128)(2,1)}, u32[]{:S(2)}, u32[]{:S(2)}) collective-permute-start(bf16[2,128,1536]{2,1,0:T(8,128)(2,1)} %slice.39), channel_id=1, source_target_pairs={{0,24},{8,0},{16,8},{24,16},{32,56},{40,32},{48,40},{56,48},{64,88... | collective-permute-start | bytes 2359304 | tf_op jit(solution)/shard_map/ppermute | solution.py:57
  205.1 6.8 %copy-start.4 = (bf16[4,512,384]{2,1,0:T(8,128)(2,1)S(1)}, bf16[4,512,384]{2,1,0:T(8,128)(2,1)}, u32[]{:S(2)}) copy-start(bf16[4,512,384]{2,1,0:T(8,128)(2,1)} %copy-done.3) | copy-start | bytes 4718596
  205.1 100.6 %all-to-all-start = ((bf16[8,256,384]{2,1,0:T(8,128)(2,1)}), bf16[8,256,384]{2,1,0:T(8,128)(2,1)}, u32[]{:S(2)}, u32[]{:S(2)}) async-start(bf16[8,256,384]{2,1,0:T(8,128)(2,1)} %bitcast.35), calls=%async_computation.1 | async-start | bytes 3145728 | tf_op jit(solution)/shard_map/all_to_all | solution.py:16
  229.9 5.5 %copy-start.8 = (bf16[4,128,1536]{2,1,0:T(8,128)(2,1)S(1)}, bf16[4,128,1536]{2,1,0:T(8,128)(2,1)}, u32[]{:S(2)}) copy-start(bf16[4,128,1536]{2,1,0:T(8,128)(2,1)} %pad_maximum_fusion.1) | copy-start | bytes 4718596
  296.5 2.8 collective-permute-start.20
  300.8 14.6 %collective-permute-start.21 = (bf16[256,384]{1,0:T(8,128)(2,1)S(1)}, bf16[256,384]{1,0:T(8,128)(2,1)S(1)}, u32[]{:S(2)}, u32[]{:S(2)}) collective-permute-start(bf16[256,384]{1,0:T(8,128)(2,1)S(1)} %get-tuple-element.27), channel_id=1, source_target_pairs={{0,2},{1,3},{2,4},{3,5},{4,6},{5,7},{6,0},{7,1},{8,10},{9,11},{10,... | collective-permute-start | bytes 589832 | tf_op jit(solution)/shard_map/ppermute | solution.py:83
  302.0 13.3 %collective-permute-start.22 = (bf16[256,384]{1,0:T(8,128)(2,1)S(1)}, bf16[256,384]{1,0:T(8,128)(2,1)S(1)}, u32[]{:S(2)}, u32[]{:S(2)}) collective-permute-start(bf16[256,384]{1,0:T(8,128)(2,1)S(1)} %get-tuple-element.29), channel_id=1, source_target_pairs={{0,4},{1,5},{2,6},{3,7},{4,0},{5,1},{6,2},{7,3},{8,12},{9,13},{10,... | collective-permute-start | bytes 589832 | tf_op jit(solution)/shard_map/ppermute | solution.py:83
  304.5 10.9 %collective-permute-start.23 = (bf16[256,384]{1,0:T(8,128)(2,1)S(1)}, bf16[256,384]{1,0:T(8,128)(2,1)S(1)}, u32[]{:S(2)}, u32[]{:S(2)}) collective-permute-start(bf16[256,384]{1,0:T(8,128)(2,1)S(1)} %get-tuple-element.28), channel_id=1, source_target_pairs={{0,6},{1,7},{2,0},{3,1},{4,2},{5,3},{6,4},{7,5},{8,14},{9,15},{10,... | collective-permute-start | bytes 589832 | tf_op jit(solution)/shard_map/ppermute | solution.py:83
  305.6 11.5 %copy-start.1 = (bf16[3072,384]{1,0:T(8,128)(2,1)S(1)}, bf16[3072,384]{1,0:T(8,128)(2,1)}, u32[]{:S(2)}) copy-start(bf16[3072,384]{1,0:T(8,128)(2,1)} %param.9) | copy-start | bytes 7077892
Sparse Core Ops, SparseCore 0:
  63.9 118.9 reduce-scatter.1
  185.8 100.1 all-gather.1
